TPU v7x, 512 devices: a whole 4x4x16 slice. The times are simulated.
512 devices in a mesh: row: 16 (over x, y), col: 32 (over z, core).
Axes of the slice: x: 4, y: 4, z: 16, core: 2. Of those that a mesh axis runs over, the one named last changes fastest.
Arguments:
- a_tiles: bfloat16 [4096, 16, 128, 128], P(('row', 'col')), may hold values from -0.5 to 0.5
- a_cols: int32 [4096, 16], P(('row', 'col')), may hold values from -1 to 103, as said below
- p_tiles: bfloat16 [4096, 2, 128, 128], P(('row', 'col')), may hold values from -0.375 to 0.375
- p_cols: int32 [4096, 2], P(('row', 'col')), may hold values from 0 to 3, all different within a row
- send_list: int32 [512, 96], P(('row', 'col')), may hold values from 0 to 7
Outputs:
- coarse: float32 [8192, 1536], P(('row', 'col'))
Inputs may be any that keep to these rules, and one draw needn't show every extreme that they name: a_cols is -1 for an empty slot, else an index below 104 into the buffer of step one; slot 0 of every block row is live and names the row itself; rows of the first row group never use t = 0 and rows of the last never t = 2; a device holds at most 80 live slots, and some device exactly 80. The 2 entries of a row of p_cols differ.
All inputs are finite; a program needn't handle non-finite values.
Results may differ from a plain program's by a relative error of at most 0.0029.
Values may be sent and summed in bfloat16 or wider, within the bound.
No kernel may reach another device: no remote copies, remote signals or barrier semaphores. Data moves between devices by JAX's collectives and lax.ppermute only.
A program may use at most 64 MiB of HBM per device.

v0:
```python
import jax
import jax.numpy as jnp
from jax import lax
from jax.sharding import PartitionSpec as P

CG = 4


def from_behind(value, axis, steps):
    count = lax.axis_size(axis)
    leading, last = (max(0, -steps), min(count, count - steps))
    return lax.ppermute(value, axis, [(source, source + steps) for source in range(leading, last)])


def exchange_rows(send_tiles, send_cols):
    return (
        lax.all_to_all(send_tiles, "col", split_axis=0, concat_axis=0, tiled=True),
        lax.all_to_all(send_cols, "col", split_axis=0, concat_axis=0, tiled=True),
    )


def body(a_tiles, a_cols, p_tiles, p_cols, send_list):
    col_count = lax.axis_size("col")
    own_rows, slot_count = a_cols.shape
    tile_count = p_cols.shape[1]
    block_size = a_tiles.shape[-1]
    window = 3 * CG
    stream_ids = jnp.arange(3, dtype=jnp.int32)
    picked = send_list[0]
    send_tiles = p_tiles[picked].reshape(col_count, 3, tile_count, block_size, block_size)
    send_cols = p_cols[picked].reshape(col_count, 3, tile_count)
    got_tiles, got_cols = exchange_rows(send_tiles, send_cols)
    lower_tiles, lower_cols = from_behind((got_tiles[:, 0], got_cols[:, 0]), "row", 1)
    upper_tiles, upper_cols = from_behind((got_tiles[:, 2], got_cols[:, 2]), "row", -1)
    ghost_tiles = jnp.stack([lower_tiles, got_tiles[:, 1], upper_tiles], axis=1)
    ghost_cols = jnp.stack([lower_cols, got_cols[:, 1], upper_cols], axis=1)
    buffer_tiles = jnp.concatenate(
        [p_tiles, ghost_tiles.reshape(3 * col_count, tile_count, block_size, block_size)], axis=0
    )
    buffer_cols = jnp.concatenate(
        [
            p_cols + CG,
            (ghost_cols + CG * stream_ids[None, :, None]).reshape(3 * col_count, tile_count),
        ],
        axis=0,
    )
    flat_tiles = a_tiles.reshape(own_rows * slot_count, block_size, block_size)
    flat_cols = a_cols.reshape(-1)
    slot_pos = jnp.arange(own_rows * slot_count, dtype=jnp.int32)

    def add_block(coarse_acc, slot_ids):
        col_ids = flat_cols[slot_ids]
        is_live = (col_ids >= 0).astype(jnp.float32)
        buffer_index = jnp.maximum(col_ids, 0)
        a_block = flat_tiles[slot_ids]
        p_block = buffer_tiles[buffer_index]
        tile_prod = jnp.einsum(
            "kxy,kpyz->kpxz", a_block, p_block, preferred_element_type=jnp.float32
        )
        tile_prod = tile_prod * is_live[:, None, None, None]
        target = (slot_ids // slot_count)[:, None] * window + buffer_cols[buffer_index]
        coarse_acc = coarse_acc.at[target.reshape(-1)].add(
            tile_prod.reshape(-1, block_size, block_size)
        )
        return (coarse_acc, None)

    start_acc = jnp.zeros((own_rows * window, block_size, block_size), jnp.float32)
    accumulated, unused = lax.scan(add_block, start_acc, slot_pos.reshape(-1, slot_count))
    product_rows = accumulated.reshape(own_rows, window, block_size, block_size).transpose(
        0, 2, 1, 3
    )
    product_rows = product_rows.reshape(own_rows * block_size, window * block_size).astype(
        jnp.bfloat16
    )
    member = (p_cols[:, :, None] == jnp.arange(CG, dtype=jnp.int32)).astype(jnp.bfloat16)
    dense_prolong = jnp.einsum(
        "fpm,fpxy->fxmy", member, p_tiles, preferred_element_type=jnp.float32
    )
    dense_prolong = dense_prolong.astype(jnp.bfloat16).reshape(
        own_rows * block_size, CG * block_size
    )
    return lax.psum_scatter(
        jnp.dot(dense_prolong.T, product_rows, preferred_element_type=jnp.float32),
        "col",
        scatter_dimension=0,
        tiled=True,
    )


def solution(mesh):
    in_specs = (
        P(("row", "col"), None, None, None),
        P(("row", "col"), None),
        P(("row", "col"), None, None, None),
        P(("row", "col"), None),
        P(("row", "col"), None),
    )
    out_specs = P(("row", "col"), None)
    return jax.shard_map(body, mesh=mesh, in_specs=in_specs, out_specs=out_specs, check_vma=False)
```

profile of v0, /device:TPU:1, one launch (start us, length us, event | category | flops | bytes accessed | tf_op | source)
XLA Modules:
  0.0 644.2 jit_solution(11576718944204558817)
XLA Ops:
  7.2 7.0 %gather_fusion.5 = bf16[96,2,128,128]{3,2,1,0:T(8,128)(2,1)} fusion(bf16[8,2,128,128]{3,2,1,0:T(8,128)(2,1)} %param.9, s32[1024]{0:T(1024)S(1)} %pad_clamp_fusion.2), kind=kCustom, calls=%fused_computation.5 | custom fusion | bytes 12583296 | tf_op jit(solution)/shard_map/gather | solution.py:30
  14.2 297.2 %all_to_all.10 = bf16[32,3,2,128,128]{4,3,2,1,0:T(8,128)(2,1)S(1)} all-to-all(bf16[32,3,2,128,128]{4,3,2,1,0:T(8,128)(2,1)} %bitcast.85), channel_id=1, replica_groups=mesh['row'=16,'col'=32] {'col'}, dimensions={0} | all-to-all | bytes 12582912 | tf_op jit(solution)/shard_map/all_to_all | solution.py:17
  311.4 4.1 slice_bitcast_fusion.1
  315.6 4.7 collective-permute-start.2
  323.1 4.3 all-to-all-start
  329.6 10.1 %all-to-all-done = s32[32,3,2]{1,2,0:T(2,128)S(1)} async-done(((s32[32,3,2]{1,2,0:T(2,128)}), s32[32,3,2]{1,2,0:T(2,128)S(1)}, u32[]{:S(2)}, u32[]{:S(2)}) %all-to-all-start) | async-done | bytes 800 | tf_op jit(solution)/shard_map/all_to_all | solution.py:18
  339.9 4.3 collective-permute-start
  345.9 17.8 %collective-permute-done = s32[32,2]{0,1:T(2,128)S(1)} collective-permute-done((s32[32,2]{0,1:T(2,128)S(1)}, s32[32,2]{0,1:T(2,128)S(1)}, u32[]{:S(2)}, u32[]{:S(2)}) %collective-permute-start) | collective-permute-done | bytes 288 | tf_op jit(solution)/shard_map/ppermute | solution.py:12
  363.7 5.1 collective-permute-done.1
  369.2 3.3 pad_maximum_fusion.1
  372.5 3.4 pad_maximum_fusion
  375.9 3.4 broadcast_in_dim.2
  379.3 144.3 %while.12 = (s32[]{:T(128)}, f32[96,128,128]{2,1,0:T(8,128)}, s32[8,16]{1,0:T(8,128)S(1)}, s32[128]{0:T(128)S(1)}, s32[104,2]{1,0:T(8,128)S(1)}, /*index=5*/bf16...) while((s32[]{:T(128)}, f32[96,128,128]{2,1,0:T(8,128)}, s32[8,16]{1,0:T(8,128)S(1)}, ...), condition=%wide.region_2.3_spmd, body=%wide.region_0.2_spmd.sunk | while | flops 135268832 | bytes 17312092 | solution.py:68
  380.0 3.7 gather_fusion.2
  391.1 6.4 scatter_fusion
  398.1 3.7 gather_fusion.2
  409.2 6.2 scatter_fusion
  416.1 3.7 gather_fusion.2
  427.1 6.3 scatter_fusion
  434.1 3.7 gather_fusion.2
  445.2 6.7 %scatter_fusion = f32[96,128,128]{2,1,0:T(8,128)} fusion(f32[96,128,128]{2,1,0:T(8,128)} %get-tuple-element.203, s32[32]{0:T(128)S(1)} %fusion.26, f32[32,128,128]{2,1,0:T(8,128)S(1)} %copy.106), kind=kCustom, calls=%fused_computation.6.clone.1 | custom fusion | flops 524288 | bytes 6291584 | tf_op jit(solution)/shard_map/while/body/eval_jaxpr/scatter-add | solution.py:62
  452.6 3.7 gather_fusion.2
  463.6 6.2 scatter_fusion
  470.5 3.7 gather_fusion.2
  481.6 6.3 scatter_fusion
  488.6 3.7 gather_fusion.2
  499.6 5.9 scatter_fusion
  506.3 3.7 gather_fusion.2
  517.3 6.3 scatter_fusion
  523.6 3.5 convert_element_type.31
  530.2 5.7 fusion.4
  535.9 101.4 %reduce-scatter.2.cloned.1.call-done = f32[16,1536]{1,0:T(8,128)} async-done(((f32[512,1536]{1,0:T(8,128)}), f32[16,1536]{1,0:T(8,128)}) %reduce-scatter.2.cloned.1.call-update) | async-done | bytes 98320 | tf_op jit(solution)/shard_map/reduce_scatter | solution.py:82
  (149 shorter events, 75.2 us)
Async XLA Ops:
  311.4 10.1 %copy-start.1 = (s32[8,2]{0,1:T(2,128)S(1)}, s32[8,2]{0,1:T(2,128)}, u32[]{:S(2)}) copy-start(s32[8,2]{0,1:T(2,128)} %param.10) | copy-start | bytes 196
  311.4 16.0 %copy-start = (bf16[8,2,128,128]{3,2,1,0:T(8,128)(2,1)S(1)}, bf16[8,2,128,128]{3,2,1,0:T(8,128)(2,1)}, u32[]{:S(2)}) copy-start(bf16[8,2,128,128]{3,2,1,0:T(8,128)(2,1)} %param.9) | copy-start | bytes 1572868
  315.6 30.2 %copy-start.2 = (s32[8,16]{1,0:T(8,128)S(1)}, s32[8,16]{1,0:T(8,128)}, u32[]{:S(2)}) copy-start(s32[8,16]{1,0:T(8,128)} %param.8) | copy-start | bytes 1540
  315.6 53.7 %collective-permute-start.2 = (bf16[32,2,128,128]{3,2,1,0:T(8,128)(2,1)}, bf16[32,2,128,128]{3,2,1,0:T(8,128)(2,1)}, u32[]{:S(2)}, u32[]{:S(2)}) collective-permute-start(bf16[32,2,128,128]{3,2,1,0:T(8,128)(2,1)} %get-tuple-element.145), channel_id=1, source_target_pairs={{0,32},{32,64},{64,96},{96,128},{128,160},{160,192},{192,224},{224... | collective-permute-start | bytes 6291464 | tf_op jit(solution)/shard_map/ppermute | solution.py:12
  320.2 49.0 %collective-permute-start.3 = (bf16[32,2,128,128]{3,2,1,0:T(8,128)(2,1)}, bf16[32,2,128,128]{3,2,1,0:T(8,128)(2,1)}, u32[]{:S(2)}, u32[]{:S(2)}) collective-permute-start(bf16[32,2,128,128]{3,2,1,0:T(8,128)(2,1)} %get-tuple-element.147), channel_id=1, source_target_pairs={{32,0},{64,32},{96,64},{128,96},{160,128},{192,160},{224,192},{256... | collective-permute-start | bytes 6291464 | tf_op jit(solution)/shard_map/ppermute | solution.py:12
  323.1 16.6 %all-to-all-start = ((s32[32,3,2]{1,2,0:T(2,128)}), s32[32,3,2]{1,2,0:T(2,128)S(1)}, u32[]{:S(2)}, u32[]{:S(2)}) async-start(s32[32,3,2]{1,2,0:T(2,128)} %copy.78), calls=%async_computation | async-start | bytes 65536 | tf_op jit(solution)/shard_map/all_to_all | solution.py:18
  327.4 309.9 %reduce-scatter.2.cloned.1.call-start = ((), (), s32[]{:S(2)}) async-start(), calls=%async_computation.3 | async-start | bytes 3244032 | tf_op jit(solution)/shard_map/reduce_scatter | solution.py:82
  339.9 23.8 %collective-permute-start = (s32[32,2]{0,1:T(2,128)S(1)}, s32[32,2]{0,1:T(2,128)S(1)}, u32[]{:S(2)}, u32[]{:S(2)}) collective-permute-start(s32[32,2]{0,1:T(2,128)S(1)} %bitcast.90), channel_id=1, source_target_pairs={{0,32},{32,64},{64,96},{96,128},{128,160},{160,192},{192,224},{224... | collective-permute-start | bytes 776 | tf_op jit(solution)/shard_map/ppermute | solution.py:12
  344.2 24.6 %collective-permute-start.1 = (s32[32,2]{0,1:T(2,128)S(1)}, s32[32,2]{0,1:T(2,128)S(1)}, u32[]{:S(2)}, u32[]{:S(2)}) collective-permute-start(s32[32,2]{0,1:T(2,128)S(1)} %bitcast.91), channel_id=1, source_target_pairs={{32,0},{64,32},{96,64},{128,96},{160,128},{192,160},{224,192},{256... | collective-permute-start | bytes 776 | tf_op jit(solution)/shard_map/ppermute | solution.py:12
Sparse Core Ops, SparseCore 0:
  536.1 101.2 reduce-scatter.1
where the time goes:
time: 649 us; the launch traced here: 644 us
  blocking collectives  297 us (46%)
  waiting for transfers between devices  134 us (21%)
  local copies, waits for them, and re-layouts  98.1 us (15%)
  other arithmetic  62.1 us (10%)
  matrix products  22.3 us (3%)
  starting transfers between devices  16 us (2%)
  between operations  13.5 us (2%)
    all_to_all x1, blocking collectives, exchange_rows(): lax.all_to_all(send_tiles, 'col', split_axis=0, concat_axis=0, tiled=True)  297 us
    reduce_scatter x1, waiting for transfers between devices, body(): lax.psum_scatter(jnp.dot(dense_prolong.T, product_rows, preferred_element...  101 us
    scatter-add x8, other arithmetic, add_block(): coarse_acc.at[target.reshape(-1)]  50.3 us
    gather x8, local copies, waits for them, and re-layouts, add_block(): p_block = buffer_tiles[buffer_index]  29.5 us
    ppermute x4, waiting for transfers between devices, from_behind(): lax.ppermute(value, axis, [(source, source + steps) for source in range(l...  22.9 us
    gather x8, local copies, waits for them, and re-layouts, add_block(): a_block = flat_tiles[slot_ids]  22.7 us
    reshape x8, local copies, waits for them, and re-layouts, add_block(): tile_prod.reshape(-1, block_size, block_size)  15.3 us
    dot_general x8, matrix products, add_block(): jnp.einsum('kxy,kpyz->kpxz', a_block, p_block, preferred_element_type=jnp...  14.5 us
  transfers between devices with their start and end apart: 6, of which 4 were waited for; matrix products, arithmetic and copies ran while one was open for 1% of the time, Pallas kernels for 0%

commit v1 on v0

v1 whole, which is shorter than its diff:
```python
import functools

import jax
import jax.numpy as jnp
from jax import lax
from jax.experimental import pallas as pl
from jax.experimental.pallas import tpu as pltpu
from jax.sharding import PartitionSpec as P

CG = 4


def from_behind(value, axis, steps):
    count = lax.axis_size(axis)
    leading, last = (max(0, -steps), min(count, count - steps))
    return lax.ppermute(value, axis, [(source, source + steps) for source in range(leading, last)])


def product_kernel(rows, slots, src_ref, live_ref, lcol_ref, pcol_ref, a_ref, b_ref, pt_ref, out_ref, acc_ref):
    bs = a_ref.shape[-1]
    out_ref[...] = jnp.zeros_like(out_ref)
    for i in range(rows):
        acc_ref[...] = jnp.zeros_like(acc_ref)

        def slot(k, carry):
            s = i * slots + k

            @pl.when(live_ref[s] != 0)
            def _():
                src = src_ref[s]
                a = a_ref[i, k]
                for p in range(2):
                    col = pl.multiple_of(lcol_ref[2 * s + p] * bs, bs)
                    acc_ref[:, pl.ds(col, bs)] += jnp.dot(
                        a, b_ref[src, p], preferred_element_type=jnp.float32
                    )

            return carry

        lax.fori_loop(0, slots, slot, 0)
        prod = acc_ref[...].astype(jnp.bfloat16)
        for p in range(2):
            m = pcol_ref[2 * i + p]
            out_ref[m] += jnp.dot(pt_ref[i, p], prod, preferred_element_type=jnp.float32)


def local_product(a_tiles, buffer_tiles, p_t, src, live, lcol, pcol, window):
    rows, slots, bs, _ = a_tiles.shape
    smem = pl.BlockSpec(memory_space=pltpu.SMEM)
    vmem = pl.BlockSpec(memory_space=pltpu.VMEM)
    flops = 2 * rows * slots * 2 * bs ** 3 + 2 * rows * 2 * bs * bs * window * bs
    nbytes = (a_tiles.size + buffer_tiles.size + p_t.size) * 2 + CG * bs * window * bs * 4
    return pl.pallas_call(
        functools.partial(product_kernel, rows, slots),
        out_shape=jax.ShapeDtypeStruct((CG, bs, window * bs), jnp.float32),
        in_specs=[smem, smem, smem, smem, vmem, vmem, vmem],
        out_specs=vmem,
        scratch_shapes=[pltpu.VMEM((bs, window * bs), jnp.float32)],
        compiler_params=pltpu.CompilerParams(vmem_limit_bytes=60 * 1024 * 1024),
        cost_estimate=pl.CostEstimate(flops=flops, bytes_accessed=nbytes, transcendentals=0),
    )(src, live, lcol, pcol, a_tiles, buffer_tiles, p_t)


def body(a_tiles, a_cols, p_tiles, p_cols, send_list):
    col_count = lax.axis_size("col")
    row_count = lax.axis_size("row")
    g = lax.axis_index("row")
    c = lax.axis_index("col")
    own_rows, slot_count = a_cols.shape
    tile_count = p_cols.shape[1]
    block_size = a_tiles.shape[-1]
    window = 3 * CG

    ints = jnp.concatenate([p_cols.reshape(-1), send_list.reshape(-1)])
    all_ints = lax.all_gather(ints, ("row", "col"), tiled=False)
    all_pcols = all_ints[:, : own_rows * tile_count].reshape(-1, own_rows, tile_count)
    all_send = all_ints[:, own_rows * tile_count :]

    group_tiles = lax.all_gather(p_tiles, "col", tiled=True)
    q = jnp.arange(col_count, dtype=jnp.int32)
    my_send = lax.dynamic_slice_in_dim(all_send, g * col_count, col_count, axis=0)

    def pick(t):
        return group_tiles[q * own_rows + my_send[:, 3 * c + t]]

    lower = from_behind(pick(0), "row", 1)
    middle = pick(1)
    upper = from_behind(pick(2), "row", -1)
    buffer_tiles = jnp.concatenate([p_tiles, lower, middle, upper], axis=0)

    stream = jnp.arange(3, dtype=jnp.int32)
    src_group = g + stream - 1
    src_dev = jnp.clip(src_group, 0, row_count - 1)[:, None] * col_count + q[None, :]
    listed = all_send[src_dev, 3 * c + stream[:, None]]
    ghost_cols = all_pcols[src_dev, listed] + CG * stream[:, None, None]
    ghost_ok = jnp.broadcast_to(((src_group >= 0) & (src_group < row_count))[:, None], (3, col_count))
    buffer_cols = jnp.concatenate([p_cols + CG, ghost_cols.reshape(-1, tile_count)], axis=0)
    buffer_ok = jnp.concatenate([jnp.ones((own_rows,), bool), ghost_ok.reshape(-1)])

    b = a_cols.reshape(-1)
    bb = jnp.clip(b, 0, own_rows + 3 * col_count - 1)
    ghost = jnp.maximum(bb - own_rows, 0)
    src = jnp.where(bb < own_rows, bb, own_rows + (ghost % 3) * col_count + ghost // 3)
    live = ((b >= 0) & buffer_ok[src]).astype(jnp.int32)
    lcol = jnp.clip(buffer_cols[src], 0, window - 1).reshape(-1)
    pcol = jnp.clip(p_cols, 0, CG - 1).reshape(-1)
    p_t = jnp.swapaxes(p_tiles, -1, -2)
    partial = local_product(a_tiles, buffer_tiles, p_t, src, live, lcol, pcol, window)
    return lax.psum_scatter(
        partial.reshape(CG * block_size, window * block_size),
        "col",
        scatter_dimension=0,
        tiled=True,
    )


def solution(mesh):
    in_specs = (
        P(("row", "col"), None, None, None),
        P(("row", "col"), None),
        P(("row", "col"), None, None, None),
        P(("row", "col"), None),
        P(("row", "col"), None),
    )
    out_specs = P(("row", "col"), None)
    return jax.shard_map(body, mesh=mesh, in_specs=in_specs, out_specs=out_specs, check_vma=False)
```

time: 649 us -> 735 us (1.13)
  waiting for transfers between devices: 134 us -> 642 us
  blocking collectives: 297 us -> 0 us
  local copies, waits for them, and re-layouts: 98.1 us -> 35 us
  other arithmetic: 62.1 us -> 9.46 us
  Pallas kernels: 0 us -> 24.1 us
  matrix products: 22.3 us -> 0 us
  starting transfers between devices: 16 us -> 6.8 us
    unnamed x1 -> x4, waiting for transfers between devices: 0.02 us -> 503 us
    all_to_all x1 -> x0, blocking collectives: 297 us -> none  [exchange_rows(): lax.all_to_all(send_tiles, 'col', split_axis=0, concat_axis=0, tiled=True)]
    scatter-add x8 -> x0, other arithmetic: 50.3 us -> none  [add_block(): coarse_acc.at[target.reshape(-1)]]
    gather x35 -> x8, local copies, waits for them, and re-layouts: 69.6 us -> 27.2 us  [the longest x3 22.6 us: pick(): return group_tiles[q * own_rows + my_send[:, 3 * c + t]]]
    pallas_call x0 -> x1, Pallas kernels: none -> 24.1 us  [local_product(): pl.pallas_call(functools.partial(product_kernel, rows, slots), out_shape=...]
    dot_general x10 -> x0, matrix products: 22.3 us -> none  [the longest x8 14.5 us: add_block(): jnp.einsum('kxy,kpyz->kpxz', a_block, p_block, preferred_element_type=jnp...]
    reshape x11 -> x4, local copies, waits for them, and re-layouts: 16.2 us -> 1.43 us  [the longest x1 0.67 us: body(): pcol = jnp.clip(p_cols, 0, CG - 1).reshape(-1)]
    reduce_scatter x1, waiting for transfers between devices: 101 us -> 112 us  [body(): lax.psum_scatter(partial.reshape(CG * block_size, window * block_size), '...]
  transfers between devices with their start and end apart: 6 -> 5, of which waited for: 4 -> 4; matrix products, arithmetic and copies ran while one was open for 1% -> 4% of each run, Pallas kernels for 0% -> 0%
where the time goes in v1:
time: 735 us; the launch traced here: 732 us
  waiting for transfers between devices  642 us (87%)
  local copies, waits for them, and re-layouts  35 us (5%)
  Pallas kernels  24.1 us (3%)
  between operations  15 us (2%)
  other arithmetic  9.46 us (1%)
    unnamed x4, waiting for transfers between devices  503 us
    reduce_scatter x1, waiting for transfers between devices, body(): lax.psum_scatter(partial.reshape(CG * block_size, window * block_size), '...  112 us
    ppermute x2, waiting for transfers between devices, from_behind(): lax.ppermute(value, axis, [(source, source + steps) for source in range(l...  26.2 us
    pallas_call x1, Pallas kernels, local_product(): pl.pallas_call(functools.partial(product_kernel, rows, slots), out_shape=...  24.1 us
    gather x3, local copies, waits for them, and re-layouts, pick(): return group_tiles[q * own_rows + my_send[:, 3 * c + t]]  22.6 us
  transfers between devices with their start and end apart: 5, of which 4 were waited for; matrix products, arithmetic and copies ran while one was open for 4% of the time, Pallas kernels for 0%

profile of v1, /device:TPU:1, one launch (start us, length us, event | category | flops | bytes accessed | tf_op | source)
XLA Modules:
  0.0 731.9 jit_solution(3231464253204109217)
XLA Ops:
  7.4 0.8 copy.26
  8.2 0.8 add_dynamic-update-slice_fusion
  9.1 0.7 copy-done.1
  9.8 0.5 all-gather.3.cloned.1.call-update
  10.4 0.7 broadcast_clamp_fusion.1
  11.3 2.1 copy.32
  13.4 0.7 broadcast_compare_fusion
  14.0 0.1 ge.14
  14.6 502.5 %all-reduce.4.cloned.1.call-done = s32[57344]{0:T(1024)} async-done(((s32[57344]{0:T(1024)}), s32[57344]{0:T(1024)}) %all-reduce.4.cloned.1.call-update) | async-done | bytes 229392
  517.1 1.1 reshape.262
  518.2 0.1 slice.23
  518.3 0.1 copy.33
  518.5 0.1 fusion.15
  518.6 7.9 %gather_fusion.6 = bf16[32,2,128,128]{3,2,1,0:T(8,128)(2,1)} fusion(bf16[256,2,128,128]{3,2,1,0:T(8,128)(2,1)} %all-gather.3.cloned.1.call-done, s32[1024]{0:T(1024)S(1)} %pad_clamp_fusion), kind=kCustom, calls=%fused_computation.6 | custom fusion | bytes 4194432 | tf_op jit(solution)/shard_map/gather | solution.py:84
  526.5 1.4 collective-permute-start.1
  528.0 7.9 %gather_fusion.4 = bf16[32,2,128,128]{3,2,1,0:T(8,128)(2,1)} fusion(bf16[256,2,128,128]{3,2,1,0:T(8,128)(2,1)} %all-gather.3.cloned.1.call-done, s32[1024]{0:T(1024)S(1)} %pad_clamp_fusion.2), kind=kCustom, calls=%fused_computation.4 | custom fusion | bytes 4194432 | tf_op jit(solution)/shard_map/gather | solution.py:84
  535.9 5.3 collective-permute-start
  541.3 0.7 reshape.208.pcol_ref
  542.1 1.2 gather_fusion
  543.3 0.6 compare_select_fusion.8.src_ref
  543.9 0.5 and_convert_fusion.live_ref
  544.5 0.6 reshape.267
  545.1 1.5 gather_fusion.1
  546.8 1.1 gather_fusion.2
  548.0 0.6 gather_fusion.3
  548.7 0.7 min.46.lcol_ref
  549.4 6.8 gather_fusion.5
  556.2 17.4 %collective-permute-done.1 = bf16[32,2,128,128]{3,2,1,0:T(8,128)(2,1)} collective-permute-done((bf16[32,2,128,128]{3,2,1,0:T(8,128)(2,1)}, bf16[32,2,128,128]{3,2,1,0:T(8,128)(2,1)}, u32[]{:S(2)}, u32[]{:S(2)}) %collective-permute-start.1) | collective-permute-done | bytes 2097184 | tf_op jit(solution)/shard_map/ppermute | solution.py:16
  573.6 8.8 %collective-permute-done = bf16[32,2,128,128]{3,2,1,0:T(8,128)(2,1)} collective-permute-done((bf16[32,2,128,128]{3,2,1,0:T(8,128)(2,1)}, bf16[32,2,128,128]{3,2,1,0:T(8,128)(2,1)}, u32[]{:S(2)}, u32[]{:S(2)}) %collective-permute-start) | collective-permute-done | bytes 2097184 | tf_op jit(solution)/shard_map/ppermute | solution.py:16
  582.4 5.7 pad_maximum_fusion.b_ref
  588.0 24.1 %shard_map.55 = f32[4,128,1536]{2,1,0:T(8,128)} custom-call(s32[128]{0:T(128)} %compare_select_fusion.8.src_ref, s32[128]{0:T(128)} %and_convert_fusion.live_ref, s32[256]{0:T(256)} %min.46.lcol_ref, s32[16]{0:T(128)} %reshape.208.pcol_ref, bf16[8,16,128,128]{3,2,1,0:T(8,128)(2,1)} %a_ref.1, bf16[104,2,128,128]{3,2,1,0:T(8,128)(2,1)} %pad_maximum_fusion.b_ref, ...), custom_call_target="tpu_custom_call" | custom-call | flops 1879048192 | bytes 14680064 | tf_op jit(solution)/shard_map/pallas_call | solution.py:53
  612.2 112.2 %reduce-scatter.2.cloned.1.call-done = f32[16,1536]{1,0:T(8,128)} async-done(((f32[512,1536]{1,0:T(8,128)}), f32[16,1536]{1,0:T(8,128)}) %reduce-scatter.2.cloned.1.call-update) | async-done | bytes 98320 | tf_op jit(solution)/shard_map/reduce_scatter | solution.py:109
  (39 shorter events, 1.5 us)
Async XLA Ops:
  7.4 509.7 %all-reduce.4.cloned.1.call-start = ((), (), s32[]{:S(2)}) async-start(), calls=%async_computation.3 | async-start | bytes 458752
  9.1 0.7 copy-start.1
  9.8 508.8 %all-gather.3.cloned.1.call-start = ((), (), s32[]{:S(2)}) async-start(), calls=%async_computation.1 | async-start | bytes 17301504 | tf_op jit(solution)/shard_map/all_gather | solution.py:79
  10.4 714.1 %reduce-scatter.2.cloned.1.call-start = ((), (), s32[]{:S(2)}) async-start(), calls=%async_computation.2 | async-start | bytes 3244032 | tf_op jit(solution)/shard_map/reduce_scatter | solution.py:109
  526.5 14.7 %copy-start.2 = (s32[8,2]{0,1:T(2,128)S(1)}, s32[8,2]{0,1:T(2,128)}, u32[]{:S(2)}) copy-start(s32[8,2]{0,1:T(2,128)} %param.8) | copy-start | bytes 196
  526.5 47.0 %collective-permute-start.1 = (bf16[32,2,128,128]{3,2,1,0:T(8,128)(2,1)}, bf16[32,2,128,128]{3,2,1,0:T(8,128)(2,1)}, u32[]{:S(2)}, u32[]{:S(2)}) collective-permute-start(bf16[32,2,128,128]{3,2,1,0:T(8,128)(2,1)} %gather_fusion.6), channel_id=1, source_target_pairs={{32,0},{64,32},{96,64},{128,96},{160,128},{192,160},{224,192},{256... | collective-permute-start | bytes 6291464 | tf_op jit(solution)/shard_map/ppermute | solution.py:16
  535.9 46.5 %collective-permute-start = (bf16[32,2,128,128]{3,2,1,0:T(8,128)(2,1)}, bf16[32,2,128,128]{3,2,1,0:T(8,128)(2,1)}, u32[]{:S(2)}, u32[]{:S(2)}) collective-permute-start(bf16[32,2,128,128]{3,2,1,0:T(8,128)(2,1)} %gather_fusion.4), channel_id=1, source_target_pairs={{0,32},{32,64},{64,96},{96,128},{128,160},{160,192},{192,224},{224... | collective-permute-start | bytes 6291464 | tf_op jit(solution)/shard_map/ppermute | solution.py:16
  549.4 33.0 %copy-start = (bf16[8,2,128,128]{3,2,1,0:T(8,128)(2,1)S(1)}, bf16[8,2,128,128]{3,2,1,0:T(8,128)(2,1)}, u32[]{:S(2)}) copy-start(bf16[8,2,128,128]{3,2,1,0:T(8,128)(2,1)} %param.7) | copy-start | bytes 1572868
Sparse Core Ops, SparseCore 0:
  13.6 503.4 all-reduce.3
Sparse Core Ops, SparseCore 1:
  12.4 112.8 all-gather.2
  612.3 112.1 reduce-scatter.1

commit v2 on v1

v2 whole, which is shorter than its diff:
```python
import functools

import jax
import jax.numpy as jnp
from jax import lax
from jax.experimental import pallas as pl
from jax.experimental.pallas import tpu as pltpu
from jax.sharding import PartitionSpec as P

CG = 4
VMEM_LIMIT = 60 * 1024 * 1024


def from_behind(value, axis, steps):
    count = lax.axis_size(axis)
    leading, last = (max(0, -steps), min(count, count - steps))
    return lax.ppermute(value, axis, [(source, source + steps) for source in range(leading, last)])


def accumulate_rows(rows, slots, src_ref, live_ref, lcol_ref, pcol_ref, a_ref, b_ref, pt_ref, out_ref, acc_ref):
    bs = a_ref.shape[-1]
    out_ref[...] = jnp.zeros_like(out_ref)
    for i in range(rows):
        acc_ref[...] = jnp.zeros_like(acc_ref)

        def slot(k, carry):
            s = i * slots + k

            @pl.when(live_ref[s] != 0)
            def _():
                src = src_ref[s]
                a = a_ref[i, k]
                for p in range(2):
                    col = pl.multiple_of(lcol_ref[2 * s + p] * bs, bs)
                    acc_ref[:, pl.ds(col, bs)] += jnp.dot(
                        a, b_ref[src, p], preferred_element_type=jnp.float32
                    )

            return carry

        lax.fori_loop(0, slots, slot, 0)
        prod = acc_ref[...].astype(jnp.bfloat16)
        for p in range(2):
            m = pcol_ref[2 * i + p]
            out_ref[m] += jnp.dot(pt_ref[i, p], prod, preferred_element_type=jnp.float32)


def middle_kernel(rows, slots, src_ref, live_ref, lcol_ref, pcol_ref, sel_ref, a_ref, group_ref, pt_ref, out_ref, buf_ref, acc_ref, sems):
    own = buf_ref.shape[0] - sel_ref.shape[0]
    me = lax.axis_index("col")
    copies = [pltpu.make_async_copy(group_ref.at[pl.ds(me * own, own)], buf_ref.at[pl.ds(0, own)], sems.at[0])]
    for q in range(sel_ref.shape[0]):
        copies.append(
            pltpu.make_async_copy(group_ref.at[sel_ref[q]], buf_ref.at[own + q], sems.at[q + 1])
        )
    for cp in copies:
        cp.start()
    for cp in copies:
        cp.wait()
    accumulate_rows(rows, slots, src_ref, live_ref, lcol_ref, pcol_ref, a_ref, buf_ref, pt_ref, out_ref, acc_ref)


def side_kernel(rows, slots, src_ref, live_ref, lcol_ref, pcol_ref, a_ref, lower_ref, upper_ref, pt_ref, out_ref, buf_ref, acc_ref, sems):
    half = lower_ref.shape[0]
    copies = [
        pltpu.make_async_copy(lower_ref, buf_ref.at[pl.ds(0, half)], sems.at[0]),
        pltpu.make_async_copy(upper_ref, buf_ref.at[pl.ds(half, half)], sems.at[1]),
    ]
    for cp in copies:
        cp.start()
    for cp in copies:
        cp.wait()
    accumulate_rows(rows, slots, src_ref, live_ref, lcol_ref, pcol_ref, a_ref, buf_ref, pt_ref, out_ref, acc_ref)


def pick_kernel(up_sel, down_sel, group_ref, up_ref, down_ref, sems):
    count = up_sel.shape[0]
    copies = []
    for q in range(count):
        copies.append(pltpu.make_async_copy(group_ref.at[up_sel[q]], up_ref.at[q], sems.at[q]))
        copies.append(
            pltpu.make_async_copy(group_ref.at[down_sel[q]], down_ref.at[q], sems.at[count + q])
        )
    for cp in copies:
        cp.start()
    for cp in copies:
        cp.wait()


SMEM = pl.BlockSpec(memory_space=pltpu.SMEM)
VMEM = pl.BlockSpec(memory_space=pltpu.VMEM)
ANY = pl.BlockSpec(memory_space=pl.ANY)


def cost(a_tiles, width, extra_bytes):
    rows, slots, bs, _ = a_tiles.shape
    flops = 2 * rows * slots * 2 * bs ** 3 + 2 * rows * 2 * bs * bs * width * bs
    return pl.CostEstimate(
        flops=flops,
        bytes_accessed=a_tiles.size * 2 + extra_bytes + CG * bs * width * bs * 4,
        transcendentals=0,
    )


def middle_product(a_tiles, group_tiles, p_t, sel, src, live, lcol, pcol):
    rows, slots, bs, _ = a_tiles.shape
    count = sel.shape[0]
    width = CG
    return pl.pallas_call(
        functools.partial(middle_kernel, rows, slots),
        out_shape=jax.ShapeDtypeStruct((CG, bs, width * bs), jnp.float32),
        in_specs=[SMEM, SMEM, SMEM, SMEM, SMEM, VMEM, ANY, VMEM],
        out_specs=VMEM,
        scratch_shapes=[
            pltpu.VMEM((rows + count, 2, bs, bs), jnp.bfloat16),
            pltpu.VMEM((bs, width * bs), jnp.float32),
            pltpu.SemaphoreType.DMA((count + 1,)),
        ],
        compiler_params=pltpu.CompilerParams(vmem_limit_bytes=VMEM_LIMIT),
        cost_estimate=cost(a_tiles, width, (rows + count) * 2 * bs * bs * 2),
    )(src, live, lcol, pcol, sel, a_tiles, group_tiles, p_t)


def side_product(a_tiles, lower, upper, p_t, src, live, lcol, pcol):
    rows, slots, bs, _ = a_tiles.shape
    count = lower.shape[0]
    width = 2 * CG
    return pl.pallas_call(
        functools.partial(side_kernel, rows, slots),
        out_shape=jax.ShapeDtypeStruct((CG, bs, width * bs), jnp.float32),
        in_specs=[SMEM, SMEM, SMEM, SMEM, VMEM, ANY, ANY, VMEM],
        out_specs=VMEM,
        scratch_shapes=[
            pltpu.VMEM((2 * count, 2, bs, bs), jnp.bfloat16),
            pltpu.VMEM((bs, width * bs), jnp.float32),
            pltpu.SemaphoreType.DMA((2,)),
        ],
        compiler_params=pltpu.CompilerParams(vmem_limit_bytes=VMEM_LIMIT),
        cost_estimate=cost(a_tiles, width, 2 * count * 2 * bs * bs * 2),
    )(src, live, lcol, pcol, a_tiles, lower, upper, p_t)


def pick_rows(group_tiles, up_sel, down_sel):
    count = up_sel.shape[0]
    shape = (count,) + group_tiles.shape[1:]
    out = jax.ShapeDtypeStruct(shape, group_tiles.dtype)
    nbytes = 2 * 2 * count * group_tiles[0].size * 2
    return pl.pallas_call(
        pick_kernel,
        out_shape=(out, out),
        in_specs=[SMEM, SMEM, ANY],
        out_specs=(VMEM, VMEM),
        scratch_shapes=[pltpu.SemaphoreType.DMA((2 * count,))],
        compiler_params=pltpu.CompilerParams(vmem_limit_bytes=VMEM_LIMIT),
        cost_estimate=pl.CostEstimate(flops=0, bytes_accessed=nbytes, transcendentals=0),
    )(up_sel, down_sel, group_tiles)


def body(a_tiles, a_cols, p_tiles, p_cols, send_list):
    col_count = lax.axis_size("col")
    row_count = lax.axis_size("row")
    g = lax.axis_index("row")
    c = lax.axis_index("col")
    own_rows, slot_count = a_cols.shape
    tile_count = p_cols.shape[1]
    block_size = a_tiles.shape[-1]

    ints = jnp.concatenate([p_cols.reshape(-1), send_list.reshape(-1)])
    group_ints = lax.all_gather(ints, "col", tiled=False)
    group_pcols = group_ints[:, : own_rows * tile_count].reshape(-1, tile_count)
    group_send = group_ints[:, own_rows * tile_count :]
    group_tiles = lax.all_gather(p_tiles, "col", tiled=True)

    q = jnp.arange(col_count, dtype=jnp.int32)

    def selection(t):
        return q * own_rows + jnp.clip(group_send[:, 3 * c + t], 0, own_rows - 1)

    up_sel, mid_sel, down_sel = selection(0), selection(1), selection(2)
    up_tiles, down_tiles = pick_rows(group_tiles, up_sel, down_sel)
    lower_tiles, lower_cols = from_behind((up_tiles, group_pcols[up_sel]), "row", 1)
    upper_tiles, upper_cols = from_behind((down_tiles, group_pcols[down_sel]), "row", -1)
    mid_cols = group_pcols[mid_sel]

    b = a_cols.reshape(-1)
    live = b >= 0
    bb = jnp.clip(b, 0, own_rows + 3 * col_count - 1)
    is_own = bb < own_rows
    ghost = jnp.maximum(bb - own_rows, 0)
    ghost_q = ghost // 3
    stream = ghost % 3
    src_group = g + stream - 1
    in_range = (src_group >= 0) & (src_group < row_count)
    pcol = jnp.clip(p_cols, 0, CG - 1)

    mid_src = jnp.where(is_own, bb, own_rows + ghost_q)
    mid_live = (live & (is_own | (stream == 1))).astype(jnp.int32)
    mid_table = jnp.concatenate([pcol, jnp.clip(mid_cols, 0, CG - 1)], axis=0)
    mid_lcol = mid_table[mid_src].reshape(-1)

    side_src = jnp.where(stream == 0, ghost_q, col_count + ghost_q)
    side_live = (live & ~is_own & (stream != 1) & in_range).astype(jnp.int32)
    side_table = jnp.concatenate(
        [jnp.clip(lower_cols, 0, CG - 1), jnp.clip(upper_cols, 0, CG - 1) + CG], axis=0
    )
    side_lcol = side_table[side_src].reshape(-1)

    p_t = jnp.swapaxes(p_tiles, -1, -2)
    pcol = pcol.reshape(-1)
    mid = middle_product(a_tiles, group_tiles, p_t, mid_sel, mid_src, mid_live, mid_lcol, pcol)
    mid = lax.psum_scatter(
        mid.reshape(CG * block_size, CG * block_size), "col", scatter_dimension=0, tiled=True
    )
    side = side_product(
        a_tiles, lower_tiles, upper_tiles, p_t, side_src, side_live, side_lcol, pcol
    )
    side = lax.psum_scatter(
        side.reshape(CG * block_size, 2 * CG * block_size), "col", scatter_dimension=0, tiled=True
    )
    width = CG * block_size
    return jnp.concatenate([side[:, :width], mid, side[:, width:]], axis=1)


def solution(mesh):
    in_specs = (
        P(("row", "col"), None, None, None),
        P(("row", "col"), None),
        P(("row", "col"), None, None, None),
        P(("row", "col"), None),
        P(("row", "col"), None),
    )
    out_specs = P(("row", "col"), None)
    return jax.shard_map(body, mesh=mesh, in_specs=in_specs, out_specs=out_specs, check_vma=False)
```

time: 735 us -> 426 us (0.58)
  waiting for transfers between devices: 642 us -> 246 us
  blocking collectives: 0 us -> 103 us
  local copies, waits for them, and re-layouts: 35 us -> 9.47 us
  Pallas kernels: 24.1 us -> 34.1 us
    unnamed x4 -> x3, waiting for transfers between devices: 503 us -> 0.74 us
    unnamed x0 -> x1, blocking collectives: none -> 103 us
    reduce_scatter x1 -> x2, waiting for transfers between devices: 112 us -> 207 us  [the longest x1 108 us: body(): lax.psum_scatter(mid.reshape(CG * block_size, CG * block_size), 'col', sc...]
    gather x8 -> x5, local copies, waits for them, and re-layouts: 27.2 us -> 3.01 us  [the longest x1 0.64 us: body(): side_lcol = side_table[side_src].reshape(-1)]
    ppermute x2 -> x4, waiting for transfers between devices: 26.2 us -> 37.7 us  [from_behind(): lax.ppermute(value, axis, [(source, source + steps) for source in range(l...]
    pallas_call x1 -> x3, Pallas kernels: 24.1 us -> 34.1 us  [the longest x1 16.2 us: middle_product(): pl.pallas_call(functools.partial(middle_kernel, rows, slots), out_shape=j...]
  transfers between devices with their start and end apart: 5 -> 7, of which waited for: 4 -> 5; matrix products, arithmetic and copies ran while one was open for 4% -> 4% of each run, Pallas kernels for 0% -> 5%
where the time goes in v2:
time: 426 us; the launch traced here: 423 us
  waiting for transfers between devices  246 us (58%)
  blocking collectives  103 us (24%)
  Pallas kernels  34.1 us (8%)
  between operations  13.9 us (3%)
  starting transfers between devices  9.53 us (2%)
  local copies, waits for them, and re-layouts  9.47 us (2%)
  other arithmetic  7.25 us (2%)
    reduce_scatter x1, waiting for transfers between devices, body(): lax.psum_scatter(mid.reshape(CG * block_size, CG * block_size), 'col', sc...  108 us
    unnamed x1, blocking collectives  103 us
    reduce_scatter x1, waiting for transfers between devices, body(): lax.psum_scatter(side.reshape(CG * block_size, 2 * CG * block_size), 'col...  99.5 us
    ppermute x4, waiting for transfers between devices, from_behind(): lax.ppermute(value, axis, [(source, source + steps) for source in range(l...  37.7 us
    pallas_call x1, Pallas kernels, middle_product(): pl.pallas_call(functools.partial(middle_kernel, rows, slots), out_shape=j...  16.2 us
    pallas_call x1, Pallas kernels, side_product(): pl.pallas_call(functools.partial(side_kernel, rows, slots), out_shape=jax...  12.3 us
    ppermute x4, starting transfers between devices, from_behind(): lax.ppermute(value, axis, [(source, source + steps) for source in range(l...  9.45 us
  transfers between devices with their start and end apart: 7, of which 5 were waited for; matrix products, arithmetic and copies ran while one was open for 4% of the time, Pallas kernels for 5%

profile of v2, /device:TPU:1, one launch (start us, length us, event | category | flops | bytes accessed | tf_op | source)
XLA Modules:
  0.0 423.4 jit_solution(6882663645165204380)
XLA Ops:
  6.5 0.7 all-gather.3.cloned.1.call-update
  7.3 0.8 copy.24
  8.1 1.3 dynamic-slice
  10.1 0.8 add_dynamic-update-slice_fusion
  10.9 102.6 %all-reduce = s32[3584]{0:T(1024)S(1)} all-reduce(s32[3584]{0:T(1024)S(1)} %add_dynamic-update-slice_fusion), channel_id=2, replica_groups=mesh['row'=16,'col'=32] {'col'}, use_global_device_ids=true, to_apply=%add | all-reduce | flops 3584 | bytes 28672
  114.1 0.6 gather_fusion
  114.7 3.4 collective-permute-start
  118.1 0.6 gather_fusion.1
  118.7 1.3 collective-permute-start.1
  120.0 0.7 broadcast_clamp_fusion.3
  121.8 0.7 broadcast_compare_fusion
  122.5 0.7 all-gather.3.cloned.1.call-done.group_ref
  123.2 5.5 %shard_map.55 = (bf16[32,2,128,128]{3,2,1,0:T(8,128)(2,1)}, bf16[32,2,128,128]{3,2,1,0:T(8,128)(2,1)}) custom-call(s32[32]{0:T(128)} %fusion.9.up_sel, s32[32]{0:T(128)} %get-tuple-element.24.down_sel, bf16[256,2,128,128]{3,2,1,0:T(8,128)(2,1)} %all-gather.3.cloned.1.call-done.group_ref), custom_call_target="tpu_custom_call" | custom-call | bytes 8388608 | tf_op jit(solution)/shard_map/pallas_call | solution.py:148
  128.8 3.4 collective-permute-start.2
  132.2 1.3 collective-permute-start.3
  133.7 0.6 compare_select_fusion.8
  134.3 0.5 and_convert_fusion
  135.9 1.0 copy.26
  136.9 0.6 reshape.147.pcol_ref
  137.6 0.6 gather_fusion.2
  138.3 0.7 reshape.146.lcol_ref
  139.0 33.7 %collective-permute-done.2.lower_ref = bf16[32,2,128,128]{3,2,1,0:T(8,128)(2,1)S(1)} collective-permute-done((bf16[32,2,128,128]{3,2,1,0:T(8,128)(2,1)}, bf16[32,2,128,128]{3,2,1,0:T(8,128)(2,1)S(1)}, u32[]{:S(2)}, u32[]{:S(2)}) %collective-permute-start.2) | collective-permute-done | bytes 2097184 | tf_op jit(solution)/shard_map/ppermute | solution.py:17
  172.7 4.0 collective-permute-done.3.upper_ref
  176.7 12.3 %shard_map.56 = f32[4,128,1024]{2,1,0:T(8,128)} custom-call(s32[128]{0:T(128)} %compare_select_fusion.7.src_ref, s32[128]{0:T(128)} %and_convert_fusion.1.live_ref, s32[256]{0:T(256)} %reshape.146.lcol_ref, s32[16]{0:T(128)} %reshape.147.pcol_ref, bf16[8,16,128,128]{3,2,1,0:T(8,128)(2,1)} %a_ref.3, bf16[32,2,128,128]{3,2,1,0:T(8,128)(2,1)} %copy-done.1, ...), custom_call_target="tpu_custom_call" | custom-call | flops 1610612736 | bytes 10485760 | tf_op jit(solution)/shard_map/pallas_call | solution.py:128
  189.1 0.6 gather_fusion.3
  189.7 0.6 gather_fusion.4
  190.4 0.7 reshape.149.lcol_ref
  191.1 16.2 %shard_map.57 = f32[4,128,512]{2,1,0:T(8,128)} custom-call(s32[128]{0:T(128)} %get-tuple-element.19.src_ref, s32[128]{0:T(128)} %get-tuple-element.17.live_ref, s32[256]{0:T(256)} %reshape.149.lcol_ref, s32[16]{0:T(128)} %reshape.147.pcol_ref, s32[32]{0:T(128)} %get-tuple-element.23.sel_ref, bf16[8,16,128,128]{3,2,1,0:T(8,128)(2,1)} %a_ref.3, ...), custom_call_target="tpu_custom_call" | custom-call | flops 1342177280 | bytes 7864320 | tf_op jit(solution)/shard_map/pallas_call | solution.py:109
  207.3 99.5 %reduce-scatter.3.cloned.1.call-done = f32[16,1024]{1,0:T(8,128)} async-done(((f32[512,1024]{1,0:T(8,128)}), f32[16,1024]{1,0:T(8,128)}) %reduce-scatter.3.cloned.1.call-update) | async-done | bytes 65552 | tf_op jit(solution)/shard_map/reduce_scatter | solution.py:217
  306.8 0.8 fusion.11
  307.6 107.9 %reduce-scatter.5.cloned.1.call-done = f32[16,512]{1,0:T(8,128)} async-done(((f32[512,512]{1,0:T(8,128)}), f32[16,512]{1,0:T(8,128)}) %reduce-scatter.5.cloned.1.call-update) | async-done | bytes 32784 | tf_op jit(solution)/shard_map/reduce_scatter | solution.py:211
  415.4 1.4 pad_maximum_fusion
  (37 shorter events, 3.2 us)
Async XLA Ops:
  6.5 116.7 %all-gather.3.cloned.1.call-start = ((), (), s32[]{:S(2)}) async-start(), calls=%async_computation.2 | async-start | bytes 17301504 | tf_op jit(solution)/shard_map/all_gather | solution.py:172
  7.3 299.5 %reduce-scatter.3.cloned.1.call-start = ((), (), s32[]{:S(2)}) async-start(), calls=%async_computation.3 | async-start | bytes 2162688 | tf_op jit(solution)/shard_map/reduce_scatter | solution.py:217
  114.7 22.9 %collective-permute-start = (s32[32,2]{1,0:T(8,128)S(1)}, s32[32,2]{1,0:T(8,128)S(1)}, u32[]{:S(2)}, u32[]{:S(2)}) collective-permute-start(s32[32,2]{1,0:T(8,128)S(1)} %gather_fusion), channel_id=1, source_target_pairs={{0,32},{32,64},{64,96},{96,128},{128,160},{160,192},{192,224},{224... | collective-permute-start | bytes 776 | tf_op jit(solution)/shard_map/ppermute | solution.py:17
  118.7 18.9 %collective-permute-start.1 = (s32[32,2]{1,0:T(8,128)S(1)}, s32[32,2]{1,0:T(8,128)S(1)}, u32[]{:S(2)}, u32[]{:S(2)}) collective-permute-start(s32[32,2]{1,0:T(8,128)S(1)} %gather_fusion.1), channel_id=1, source_target_pairs={{32,0},{64,32},{96,64},{128,96},{160,128},{192,160},{224,192},{256... | collective-permute-start | bytes 776 | tf_op jit(solution)/shard_map/ppermute | solution.py:17
  123.2 12.7 %copy-start = (bf16[8,2,128,128]{3,2,1,0:T(8,128)(2,1)S(1)}, bf16[8,2,128,128]{3,2,1,0:T(8,128)(2,1)}, u32[]{:S(2)}) copy-start(bf16[8,2,128,128]{3,2,1,0:T(8,128)(2,1)} %param.7) | copy-start | bytes 1572868
  128.8 44.0 %collective-permute-start.2 = (bf16[32,2,128,128]{3,2,1,0:T(8,128)(2,1)}, bf16[32,2,128,128]{3,2,1,0:T(8,128)(2,1)S(1)}, u32[]{:S(2)}, u32[]{:S(2)}) collective-permute-start(bf16[32,2,128,128]{3,2,1,0:T(8,128)(2,1)} %get-tuple-element.7), channel_id=1, source_target_pairs={{0,32},{32,64},{64,96},{96,128},{128,160},{160,192},{192,224},{224... | collective-permute-start | bytes 6291464 | tf_op jit(solution)/shard_map/ppermute | solution.py:17
  132.2 44.5 %collective-permute-start.3 = (bf16[32,2,128,128]{3,2,1,0:T(8,128)(2,1)}, bf16[32,2,128,128]{3,2,1,0:T(8,128)(2,1)}, u32[]{:S(2)}, u32[]{:S(2)}) collective-permute-start(bf16[32,2,128,128]{3,2,1,0:T(8,128)(2,1)} %get-tuple-element.8), channel_id=1, source_target_pairs={{32,0},{64,32},{96,64},{128,96},{160,128},{192,160},{224,192},{256... | collective-permute-start | bytes 6291464 | tf_op jit(solution)/shard_map/ppermute | solution.py:17
  172.7 4.0 copy-start.1
  189.1 226.4 %reduce-scatter.5.cloned.1.call-start = ((), (), s32[]{:S(2)}) async-start(), calls=%async_computation.4 | async-start | bytes 1081344 | tf_op jit(solution)/shard_map/reduce_scatter | solution.py:211
Sparse Core Ops, SparseCore 0:
  9.5 113.6 all-gather.2
  189.2 117.5 reduce-scatter.2
  309.8 105.5 reduce-scatter.4

commit v3 on v2

--- a/solution.py
+++ b/solution.py
@@ -19,7 +19,6 @@
 
 def accumulate_rows(rows, slots, src_ref, live_ref, lcol_ref, pcol_ref, a_ref, b_ref, pt_ref, out_ref, acc_ref):
     bs = a_ref.shape[-1]
-    out_ref[...] = jnp.zeros_like(out_ref)
     for i in range(rows):
         acc_ref[...] = jnp.zeros_like(acc_ref)
 
@@ -47,7 +46,7 @@
 
 def middle_kernel(rows, slots, src_ref, live_ref, lcol_ref, pcol_ref, sel_ref, a_ref, group_ref, pt_ref, out_ref, buf_ref, acc_ref, sems):
     own = buf_ref.shape[0] - sel_ref.shape[0]
-    me = lax.axis_index("col")
+    me = lax.axis_index("core") * lax.axis_size("z") + lax.axis_index("z")
     copies = [pltpu.make_async_copy(group_ref.at[pl.ds(me * own, own)], buf_ref.at[pl.ds(0, own)], sems.at[0])]
     for q in range(sel_ref.shape[0]):
         copies.append(
@@ -55,12 +54,13 @@
         )
     for cp in copies:
         cp.start()
+    out_ref[...] = jnp.zeros_like(out_ref)
     for cp in copies:
         cp.wait()
     accumulate_rows(rows, slots, src_ref, live_ref, lcol_ref, pcol_ref, a_ref, buf_ref, pt_ref, out_ref, acc_ref)
 
 
-def side_kernel(rows, slots, src_ref, live_ref, lcol_ref, pcol_ref, a_ref, lower_ref, upper_ref, pt_ref, out_ref, buf_ref, acc_ref, sems):
+def side_kernel(rows, slots, src_ref, live_ref, lcol_ref, pcol_ref, a_ref, lower_ref, upper_ref, pt_ref, prior_ref, out_ref, buf_ref, acc_ref, sems):
     half = lower_ref.shape[0]
     copies = [
         pltpu.make_async_copy(lower_ref, buf_ref.at[pl.ds(0, half)], sems.at[0]),
@@ -68,6 +68,7 @@
     ]
     for cp in copies:
         cp.start()
+    out_ref[...] = prior_ref[...]
     for cp in copies:
         cp.wait()
     accumulate_rows(rows, slots, src_ref, live_ref, lcol_ref, pcol_ref, a_ref, buf_ref, pt_ref, out_ref, acc_ref)
@@ -105,7 +106,7 @@
 def middle_product(a_tiles, group_tiles, p_t, sel, src, live, lcol, pcol):
     rows, slots, bs, _ = a_tiles.shape
     count = sel.shape[0]
-    width = CG
+    width = 3 * CG
     return pl.pallas_call(
         functools.partial(middle_kernel, rows, slots),
         out_shape=jax.ShapeDtypeStruct((CG, bs, width * bs), jnp.float32),
@@ -121,14 +122,15 @@
     )(src, live, lcol, pcol, sel, a_tiles, group_tiles, p_t)
 
 
-def side_product(a_tiles, lower, upper, p_t, src, live, lcol, pcol):
+def side_product(a_tiles, lower, upper, p_t, src, live, lcol, pcol, prior):
     rows, slots, bs, _ = a_tiles.shape
     count = lower.shape[0]
-    width = 2 * CG
+    width = 3 * CG
     return pl.pallas_call(
         functools.partial(side_kernel, rows, slots),
         out_shape=jax.ShapeDtypeStruct((CG, bs, width * bs), jnp.float32),
-        in_specs=[SMEM, SMEM, SMEM, SMEM, VMEM, ANY, ANY, VMEM],
+        in_specs=[SMEM, SMEM, SMEM, SMEM, VMEM, ANY, ANY, VMEM, VMEM],
+        input_output_aliases={8: 0},
         out_specs=VMEM,
         scratch_shapes=[
             pltpu.VMEM((2 * count, 2, bs, bs), jnp.bfloat16),
@@ -137,7 +139,7 @@
         ],
         compiler_params=pltpu.CompilerParams(vmem_limit_bytes=VMEM_LIMIT),
         cost_estimate=cost(a_tiles, width, 2 * count * 2 * bs * bs * 2),
-    )(src, live, lcol, pcol, a_tiles, lower, upper, p_t)
+    )(src, live, lcol, pcol, a_tiles, lower, upper, p_t, prior)
 
 
 def pick_rows(group_tiles, up_sel, down_sel):
@@ -157,30 +159,38 @@
 
 
 def body(a_tiles, a_cols, p_tiles, p_cols, send_list):
-    col_count = lax.axis_size("col")
+    z_count = lax.axis_size("z")
+    core_count = lax.axis_size("core")
+    col_count = z_count * core_count
     row_count = lax.axis_size("row")
     g = lax.axis_index("row")
-    c = lax.axis_index("col")
+    c = lax.axis_index("z") * core_count + lax.axis_index("core")
     own_rows, slot_count = a_cols.shape
     tile_count = p_cols.shape[1]
     block_size = a_tiles.shape[-1]
 
     ints = jnp.concatenate([p_cols.reshape(-1), send_list.reshape(-1)])
-    group_ints = lax.all_gather(ints, "col", tiled=False)
+    group_ints = lax.all_gather(lax.all_gather(ints, "z"), "core")
+    group_ints = jnp.swapaxes(group_ints, 0, 1).reshape(col_count, -1)
     group_pcols = group_ints[:, : own_rows * tile_count].reshape(-1, tile_count)
     group_send = group_ints[:, own_rows * tile_count :]
-    group_tiles = lax.all_gather(p_tiles, "col", tiled=True)
+    group_tiles = lax.all_gather(lax.all_gather(p_tiles, "z", tiled=True), "core", tiled=True)
 
     q = jnp.arange(col_count, dtype=jnp.int32)
+    base = ((q % core_count) * z_count + q // core_count) * own_rows
 
     def selection(t):
-        return q * own_rows + jnp.clip(group_send[:, 3 * c + t], 0, own_rows - 1)
+        return base + jnp.clip(group_send[:, 3 * c + t], 0, own_rows - 1)
 
     up_sel, mid_sel, down_sel = selection(0), selection(1), selection(2)
     up_tiles, down_tiles = pick_rows(group_tiles, up_sel, down_sel)
-    lower_tiles, lower_cols = from_behind((up_tiles, group_pcols[up_sel]), "row", 1)
-    upper_tiles, upper_cols = from_behind((down_tiles, group_pcols[down_sel]), "row", -1)
-    mid_cols = group_pcols[mid_sel]
+
+    def cols_of(t):
+        return group_pcols[q * own_rows + jnp.clip(group_send[:, 3 * c + t], 0, own_rows - 1)]
+
+    lower_tiles, lower_cols = from_behind((up_tiles, cols_of(0)), "row", 1)
+    upper_tiles, upper_cols = from_behind((down_tiles, cols_of(2)), "row", -1)
+    mid_cols = cols_of(1)
 
     b = a_cols.reshape(-1)
     live = b >= 0
@@ -195,39 +205,37 @@
 
     mid_src = jnp.where(is_own, bb, own_rows + ghost_q)
     mid_live = (live & (is_own | (stream == 1))).astype(jnp.int32)
-    mid_table = jnp.concatenate([pcol, jnp.clip(mid_cols, 0, CG - 1)], axis=0)
+    mid_table = jnp.concatenate([pcol, jnp.clip(mid_cols, 0, CG - 1)], axis=0) + CG
     mid_lcol = mid_table[mid_src].reshape(-1)
 
     side_src = jnp.where(stream == 0, ghost_q, col_count + ghost_q)
     side_live = (live & ~is_own & (stream != 1) & in_range).astype(jnp.int32)
     side_table = jnp.concatenate(
-        [jnp.clip(lower_cols, 0, CG - 1), jnp.clip(upper_cols, 0, CG - 1) + CG], axis=0
+        [jnp.clip(lower_cols, 0, CG - 1), jnp.clip(upper_cols, 0, CG - 1) + 2 * CG], axis=0
     )
     side_lcol = side_table[side_src].reshape(-1)
 
     p_t = jnp.swapaxes(p_tiles, -1, -2)
     pcol = pcol.reshape(-1)
     mid = middle_product(a_tiles, group_tiles, p_t, mid_sel, mid_src, mid_live, mid_lcol, pcol)
-    mid = lax.psum_scatter(
-        mid.reshape(CG * block_size, CG * block_size), "col", scatter_dimension=0, tiled=True
-    )
-    side = side_product(
-        a_tiles, lower_tiles, upper_tiles, p_t, side_src, side_live, side_lcol, pcol
-    )
-    side = lax.psum_scatter(
-        side.reshape(CG * block_size, 2 * CG * block_size), "col", scatter_dimension=0, tiled=True
-    )
-    width = CG * block_size
-    return jnp.concatenate([side[:, :width], mid, side[:, width:]], axis=1)
+    partial = side_product(
+        a_tiles, lower_tiles, upper_tiles, p_t, side_src, side_live, side_lcol, pcol, mid
+    )
+    partial = partial.reshape(CG * block_size, 3 * CG * block_size)
+    partial = lax.psum_scatter(partial, "z", scatter_dimension=0, tiled=True)
+    return lax.psum_scatter(partial, "core", scatter_dimension=0, tiled=True)
 
 
 def solution(mesh):
+    rows, cols = mesh.devices.shape
+    chip_mesh = jax.sharding.Mesh(mesh.devices.reshape(rows, cols // 2, 2), ("row", "z", "core"))
+    split = ("row", "z", "core")
     in_specs = (
-        P(("row", "col"), None, None, None),
-        P(("row", "col"), None),
-        P(("row", "col"), None, None, None),
-        P(("row", "col"), None),
-        P(("row", "col"), None),
-    )
-    out_specs = P(("row", "col"), None)
-    return jax.shard_map(body, mesh=mesh, in_specs=in_specs, out_specs=out_specs, check_vma=False)
+        P(split, None, None, None),
+        P(split, None),
+        P(split, None, None, None),
+        P(split, None),
+        P(split, None),
+    )
+    out_specs = P(split, None)
+    return jax.shard_map(body, mesh=chip_mesh, in_specs=in_specs, out_specs=out_specs, check_vma=False)

time: 426 us -> 344 us (0.81)
  blocking collectives: 103 us -> 21.4 us
  Pallas kernels: 34.1 us -> 39.1 us
    all_gather x1 -> x2, waiting for transfers between devices: 0.69 us -> 124 us  [the longest x1 113 us: body(): lax.all_gather(p_tiles, 'z', tiled=True)]
    reduce_scatter x2, waiting for transfers between devices: 207 us -> 102 us  [the longest x1 73.4 us: body(): partial = lax.psum_scatter(partial, 'z', scatter_dimension=0, tiled=True)]
    unnamed x1, blocking collectives: 103 us -> 16 us
    ppermute x4, waiting for transfers between devices: 37.7 us -> 22.2 us  [from_behind(): lax.ppermute(value, axis, [(source, source + steps) for source in range(l...]
    all_gather x0 -> x1, blocking collectives: none -> 5.44 us  [body(): group_ints = lax.all_gather(lax.all_gather(ints, 'z'), 'core')]
  transfers between devices with their start and end apart: 7 -> 8, of which waited for: 5 -> 6; matrix products, arithmetic and copies ran while one was open for 4% -> 3% of each run, Pallas kernels for 5% -> 7%
where the time goes in v3:
time: 344 us
  waiting for transfers between devices  249 us (72%)
  Pallas kernels  39.1 us (11%)
  blocking collectives  21.4 us (6%)
  between operations  14 us (4%)
  local copies, waits for them, and re-layouts  8.58 us (2%)
  starting transfers between devices  8.06 us (2%)
  other arithmetic  3.91 us (1%)
    all_gather x1, waiting for transfers between devices, body(): lax.all_gather(p_tiles, 'z', tiled=True)  113 us
    reduce_scatter x1, waiting for transfers between devices, body(): partial = lax.psum_scatter(partial, 'z', scatter_dimension=0, tiled=True)  73.4 us
    reduce_scatter x1, waiting for transfers between devices, body(): return lax.psum_scatter(partial, 'core', scatter_dimension=0, tiled=True)  28.9 us
    ppermute x4, waiting for transfers between devices, from_behind(): lax.ppermute(value, axis, [(source, source + steps) for source in range(l...  22.2 us
    pallas_call x1, Pallas kernels, middle_product(): pl.pallas_call(functools.partial(middle_kernel, rows, slots), out_shape=j...  18 us
    unnamed x1, blocking collectives  16 us
    pallas_call x1, Pallas kernels, side_product(): pl.pallas_call(functools.partial(side_kernel, rows, slots), out_shape=jax...  15.4 us
    all_gather x1, waiting for transfers between devices, body(): lax.all_gather(lax.all_gather(p_tiles, 'z', tiled=True), 'core', tiled=True)  10.2 us
  transfers between devices with their start and end apart: 8, of which 6 were waited for; matrix products, arithmetic and copies ran while one was open for 3% of the time, Pallas kernels for 7%

profile of v3, /device:TPU:1, one launch (start us, length us, event | category | flops | bytes accessed | tf_op | source)
XLA Modules:
  0.0 343.9 jit_solution(411038481088395420)
XLA Ops:
  6.5 0.7 all-gather.5.cloned.1.call-update
  7.3 113.4 %all-gather.5.cloned.1.call-done = bf16[128,2,128,128]{3,2,1,0:T(8,128)(2,1)} async-done(((bf16[8,2,128,128]{3,2,1,0:T(8,128)(2,1)}), bf16[128,2,128,128]{3,2,1,0:T(8,128)(2,1)}) %all-gather.5.cloned.1.call-update) | async-done | bytes 8388624 | tf_op jit(solution)/shard_map/all_gather | solution.py:177
  120.8 0.6 copy-done.3
  121.6 1.3 dynamic-slice
  123.7 16.0 %all-reduce = s32[1792]{0:T(1024)S(1)} all-reduce(s32[1792]{0:T(1024)S(1)} %add_dynamic-update-slice_fusion), channel_id=2, replica_groups=mesh['row'=16,'z'=16,'core'=2] {'z'}, use_global_device_ids=true, to_apply=%add | all-reduce | flops 1792 | bytes 14336
  139.8 5.4 %all-gather.1 = s32[32,112]{1,0:T(8,128)S(1)} all-gather(s32[16,112]{1,0:T(8,128)S(1)} %reshape.191), channel_id=3, replica_groups=mesh['row'=16,'z'=16,'core'=2] {'core'}, dimensions={0}, use_global_device_ids=true | all-gather | bytes 21504 | tf_op jit(solution)/shard_map/all_gather | solution.py:173
  145.7 0.6 gather_fusion
  146.3 3.1 collective-permute-start
  149.4 0.6 gather_fusion.1
  150.0 1.3 collective-permute-start.1
  151.4 0.6 gather_fusion.3
  152.0 0.6 fusion.12
  152.6 10.2 %all-gather.7.cloned.1.call-done.group_ref = bf16[256,2,128,128]{3,2,1,0:T(8,128)(2,1)} async-done(((bf16[128,2,128,128]{3,2,1,0:T(8,128)(2,1)}), bf16[256,2,128,128]{3,2,1,0:T(8,128)(2,1)}) %all-gather.7.cloned.1.call-update) | async-done | bytes 16777232 | tf_op jit(solution)/shard_map/all_gather | solution.py:177
  162.8 5.7 %shard_map.55 = (bf16[32,2,128,128]{3,2,1,0:T(8,128)(2,1)}, bf16[32,2,128,128]{3,2,1,0:T(8,128)(2,1)}) custom-call(s32[32]{0:T(128)} %get-tuple-element.22.up_sel, s32[32]{0:T(128)} %get-tuple-element.21.down_sel, bf16[256,2,128,128]{3,2,1,0:T(8,128)(2,1)} %all-gather.7.cloned.1.call-done.group_ref), custom_call_target="tpu_custom_call" | custom-call | bytes 8388608 | tf_op jit(solution)/shard_map/pallas_call | solution.py:150
  168.5 2.2 collective-permute-start.2
  170.7 1.3 collective-permute-start.3
  172.2 0.5 fusion.11.sel_ref
  172.7 0.6 compare_select_fusion.8
  173.3 0.6 and_convert_fusion
  174.4 0.6 and_convert_fusion.1.live_ref
  175.0 0.7 reshape.148.pcol_ref
  175.7 1.0 copy.31
  176.7 0.6 gather_fusion.4
  177.3 0.7 reshape.149.lcol_ref
  178.0 0.6 gather_fusion.2
  178.7 0.7 reshape.147.lcol_ref
  179.4 18.0 %shard_map.56.prior_ref = f32[4,128,1536]{2,1,0:T(8,128)} custom-call(s32[128]{0:T(128)} %get-tuple-element.19.src_ref, s32[128]{0:T(128)} %get-tuple-element.17.live_ref, s32[256]{0:T(256)} %reshape.149.lcol_ref, s32[16]{0:T(128)} %reshape.148.pcol_ref, s32[32]{0:T(128)} %fusion.11.sel_ref, bf16[8,16,128,128]{3,2,1,0:T(8,128)(2,1)} %a_ref.3, ...), custom_call_target="tpu_custom_call" | custom-call | flops 1879048192 | bytes 9961472 | tf_op jit(solution)/shard_map/pallas_call | solution.py:110
  197.4 18.3 %collective-permute-done.2.lower_ref = bf16[32,2,128,128]{3,2,1,0:T(8,128)(2,1)S(1)} collective-permute-done((bf16[32,2,128,128]{3,2,1,0:T(8,128)(2,1)}, bf16[32,2,128,128]{3,2,1,0:T(8,128)(2,1)S(1)}, u32[]{:S(2)}, u32[]{:S(2)}) %collective-permute-start.2) | collective-permute-done | bytes 2097184 | tf_op jit(solution)/shard_map/ppermute | solution.py:17
  215.7 3.9 %collective-permute-done.3.upper_ref = bf16[32,2,128,128]{3,2,1,0:T(8,128)(2,1)} collective-permute-done((bf16[32,2,128,128]{3,2,1,0:T(8,128)(2,1)}, bf16[32,2,128,128]{3,2,1,0:T(8,128)(2,1)}, u32[]{:S(2)}, u32[]{:S(2)}) %collective-permute-start.3) | collective-permute-done | bytes 2097184 | tf_op jit(solution)/shard_map/ppermute | solution.py:17
  219.7 15.4 %shard_map.57 = f32[4,128,1536]{2,1,0:T(8,128)} custom-call(s32[128]{0:T(128)} %compare_select_fusion.7.src_ref, s32[128]{0:T(128)} %and_convert_fusion.1.live_ref, s32[256]{0:T(256)} %reshape.147.lcol_ref, s32[16]{0:T(128)} %reshape.148.pcol_ref, bf16[8,16,128,128]{3,2,1,0:T(8,128)(2,1)} %a_ref.3, ...), custom_call_target="tpu_custom_call", output_to_operand_aliasing={{}: (8, {})} | custom-call | flops 1879048192 | bytes 11534336 | tf_op jit(solution)/shard_map/pallas_call | solution.py:129
  235.1 73.4 %reduce-scatter.3.cloned.1.call-done = f32[32,1536]{1,0:T(8,128)} async-done(((f32[512,1536]{1,0:T(8,128)}), f32[32,1536]{1,0:T(8,128)}) %reduce-scatter.3.cloned.1.call-update) | async-done | bytes 196624 | tf_op jit(solution)/shard_map/reduce_scatter | solution.py:225
  308.5 28.9 %reduce-scatter.5.cloned.1.call-done = f32[16,1536]{1,0:T(8,128)} async-done(((f32[32,1536]{1,0:T(8,128)}), f32[16,1536]{1,0:T(8,128)}) %reduce-scatter.5.cloned.1.call-update) | async-done | bytes 98320 | tf_op jit(solution)/shard_map/reduce_scatter | solution.py:226
  (46 shorter events, 1.9 us)
Async XLA Ops:
  6.5 114.2 %all-gather.5.cloned.1.call-start = ((), (), s32[]{:S(2)}) async-start(), calls=%async_computation.2 | async-start | bytes 8912896 | tf_op jit(solution)/shard_map/all_gather | solution.py:177
  7.3 155.5 %all-gather.7.cloned.1.call-start = ((), (), s32[]{:S(2)}) async-start(), calls=%async_computation.3 | async-start | bytes 25165824 | tf_op jit(solution)/shard_map/all_gather | solution.py:177
  120.7 0.7 copy-start.3
  120.7 2.8 copy-start.4
  120.7 30.5 %copy-start.2 = (s32[8,16]{1,0:T(8,128)S(1)}, s32[8,16]{1,0:T(8,128)}, u32[]{:S(2)}) copy-start(s32[8,16]{1,0:T(8,128)} %param.6) | copy-start | bytes 1540
  120.7 187.7 %reduce-scatter.3.cloned.1.call-start = ((), (), s32[]{:S(2)}) async-start(), calls=%async_computation.4 | async-start | bytes 3342336 | tf_op jit(solution)/shard_map/reduce_scatter | solution.py:225
  146.3 31.7 %collective-permute-start = (s32[32,2]{1,0:T(8,128)S(1)}, s32[32,2]{1,0:T(8,128)S(1)}, u32[]{:S(2)}, u32[]{:S(2)}) collective-permute-start(s32[32,2]{1,0:T(8,128)S(1)} %gather_fusion), channel_id=1, source_target_pairs={{0,32},{32,64},{64,96},{96,128},{128,160},{160,192},{192,224},{224... | collective-permute-start | bytes 776 | tf_op jit(solution)/shard_map/ppermute | solution.py:17
  150.0 28.0 %collective-permute-start.1 = (s32[32,2]{1,0:T(8,128)S(1)}, s32[32,2]{1,0:T(8,128)S(1)}, u32[]{:S(2)}, u32[]{:S(2)}) collective-permute-start(s32[32,2]{1,0:T(8,128)S(1)} %gather_fusion.1), channel_id=1, source_target_pairs={{32,0},{64,32},{96,64},{128,96},{160,128},{192,160},{224,192},{256... | collective-permute-start | bytes 776 | tf_op jit(solution)/shard_map/ppermute | solution.py:17
  162.8 12.9 %copy-start.1 = (bf16[8,2,128,128]{3,2,1,0:T(8,128)(2,1)S(1)}, bf16[8,2,128,128]{3,2,1,0:T(8,128)(2,1)}, u32[]{:S(2)}) copy-start(bf16[8,2,128,128]{3,2,1,0:T(8,128)(2,1)} %param.7) | copy-start | bytes 1572868
  168.5 47.2 %collective-permute-start.2 = (bf16[32,2,128,128]{3,2,1,0:T(8,128)(2,1)}, bf16[32,2,128,128]{3,2,1,0:T(8,128)(2,1)S(1)}, u32[]{:S(2)}, u32[]{:S(2)}) collective-permute-start(bf16[32,2,128,128]{3,2,1,0:T(8,128)(2,1)} %get-tuple-element.7), channel_id=1, source_target_pairs={{0,32},{32,64},{64,96},{96,128},{128,160},{160,192},{192,224},{224... | collective-permute-start | bytes 6291464 | tf_op jit(solution)/shard_map/ppermute | solution.py:17
  170.7 48.9 %collective-permute-start.3 = (bf16[32,2,128,128]{3,2,1,0:T(8,128)(2,1)}, bf16[32,2,128,128]{3,2,1,0:T(8,128)(2,1)}, u32[]{:S(2)}, u32[]{:S(2)}) collective-permute-start(bf16[32,2,128,128]{3,2,1,0:T(8,128)(2,1)} %get-tuple-element.8), channel_id=1, source_target_pairs={{32,0},{64,32},{96,64},{128,96},{160,128},{192,160},{224,192},{256... | collective-permute-start | bytes 6291464 | tf_op jit(solution)/shard_map/ppermute | solution.py:17
  215.7 3.9 %copy-start = (bf16[32,2,128,128]{3,2,1,0:T(8,128)(2,1)}, bf16[32,2,128,128]{3,2,1,0:T(8,128)(2,1)S(1)}, u32[]{:S(2)}) copy-start(bf16[32,2,128,128]{3,2,1,0:T(8,128)(2,1)S(1)} %collective-permute-done.2.lower_ref) | copy-start | bytes 6291460
  235.0 102.4 %reduce-scatter.5.cloned.1.call-start = ((), (), s32[]{:S(2)}) async-start(), calls=%async_computation.5 | async-start | bytes 294912 | tf_op jit(solution)/shard_map/reduce_scatter | solution.py:226
Sparse Core Ops, SparseCore 0:
  9.4 111.2 all-gather.4
  122.8 39.8 all-gather.6
  235.2 73.2 reduce-scatter.2
  311.1 26.2 reduce-scatter.4

commit v4 on v3

--- a/solution.py
+++ b/solution.py
@@ -17,7 +17,7 @@
     return lax.ppermute(value, axis, [(source, source + steps) for source in range(leading, last)])
 
 
-def accumulate_rows(rows, slots, src_ref, live_ref, lcol_ref, pcol_ref, a_ref, b_ref, pt_ref, out_ref, acc_ref):
+def accumulate_rows(rows, slots, spans, src_ref, live_ref, lcol_ref, pcol_ref, a_ref, b_ref, pt_ref, out_ref, acc_ref):
     bs = a_ref.shape[-1]
     for i in range(rows):
         acc_ref[...] = jnp.zeros_like(acc_ref)
@@ -38,15 +38,18 @@
             return carry
 
         lax.fori_loop(0, slots, slot, 0)
-        prod = acc_ref[...].astype(jnp.bfloat16)
-        for p in range(2):
-            m = pcol_ref[2 * i + p]
-            out_ref[m] += jnp.dot(pt_ref[i, p], prod, preferred_element_type=jnp.float32)
+        for lo, hi in spans:
+            prod = acc_ref[:, lo * bs : hi * bs].astype(jnp.bfloat16)
+            for p in range(2):
+                m = pcol_ref[2 * i + p]
+                out_ref[m, :, lo * bs : hi * bs] += jnp.dot(
+                    pt_ref[i, p], prod, preferred_element_type=jnp.float32
+                )
 
 
 def middle_kernel(rows, slots, src_ref, live_ref, lcol_ref, pcol_ref, sel_ref, a_ref, group_ref, pt_ref, out_ref, buf_ref, acc_ref, sems):
     own = buf_ref.shape[0] - sel_ref.shape[0]
-    me = lax.axis_index("core") * lax.axis_size("z") + lax.axis_index("z")
+    me = lax.axis_index("z") * lax.axis_size("core") + lax.axis_index("core")
     copies = [pltpu.make_async_copy(group_ref.at[pl.ds(me * own, own)], buf_ref.at[pl.ds(0, own)], sems.at[0])]
     for q in range(sel_ref.shape[0]):
         copies.append(
@@ -57,7 +60,8 @@
     out_ref[...] = jnp.zeros_like(out_ref)
     for cp in copies:
         cp.wait()
-    accumulate_rows(rows, slots, src_ref, live_ref, lcol_ref, pcol_ref, a_ref, buf_ref, pt_ref, out_ref, acc_ref)
+    spans = ((CG, 2 * CG),)
+    accumulate_rows(rows, slots, spans, src_ref, live_ref, lcol_ref, pcol_ref, a_ref, buf_ref, pt_ref, out_ref, acc_ref)
 
 
 def side_kernel(rows, slots, src_ref, live_ref, lcol_ref, pcol_ref, a_ref, lower_ref, upper_ref, pt_ref, prior_ref, out_ref, buf_ref, acc_ref, sems):
@@ -71,7 +75,8 @@
     out_ref[...] = prior_ref[...]
     for cp in copies:
         cp.wait()
-    accumulate_rows(rows, slots, src_ref, live_ref, lcol_ref, pcol_ref, a_ref, buf_ref, pt_ref, out_ref, acc_ref)
+    spans = ((0, CG), (2 * CG, 3 * CG))
+    accumulate_rows(rows, slots, spans, src_ref, live_ref, lcol_ref, pcol_ref, a_ref, buf_ref, pt_ref, out_ref, acc_ref)
 
 
 def pick_kernel(up_sel, down_sel, group_ref, up_ref, down_ref, sems):
@@ -170,14 +175,13 @@
     block_size = a_tiles.shape[-1]
 
     ints = jnp.concatenate([p_cols.reshape(-1), send_list.reshape(-1)])
-    group_ints = lax.all_gather(lax.all_gather(ints, "z"), "core")
-    group_ints = jnp.swapaxes(group_ints, 0, 1).reshape(col_count, -1)
+    group_ints = lax.all_gather(ints, ("z", "core"))
     group_pcols = group_ints[:, : own_rows * tile_count].reshape(-1, tile_count)
     group_send = group_ints[:, own_rows * tile_count :]
-    group_tiles = lax.all_gather(lax.all_gather(p_tiles, "z", tiled=True), "core", tiled=True)
+    group_tiles = lax.all_gather(p_tiles, ("z", "core"), tiled=True)
 
     q = jnp.arange(col_count, dtype=jnp.int32)
-    base = ((q % core_count) * z_count + q // core_count) * own_rows
+    base = q * own_rows
 
     def selection(t):
         return base + jnp.clip(group_send[:, 3 * c + t], 0, own_rows - 1)

time: 344 us -> 304 us (0.88)
  waiting for transfers between devices: 249 us -> 123 us
  blocking collectives: 21.4 us -> 103 us
    all_gather x2 -> x1, waiting for transfers between devices: 124 us -> 0.53 us  [body(): group_tiles = lax.all_gather(p_tiles, ('z', 'core'), tiled=True)]
    unnamed x1, blocking collectives: 16 us -> 103 us
    all_gather x1 -> x0, blocking collectives: 5.44 us -> none  [body(): group_ints = lax.all_gather(lax.all_gather(ints, 'z'), 'core')]
    ppermute x4, waiting for transfers between devices: 22.2 us -> 17.8 us  [from_behind(): lax.ppermute(value, axis, [(source, source + steps) for source in range(l...]
  transfers between devices with their start and end apart: 8 -> 7, of which waited for: 6 -> 5; matrix products, arithmetic and copies ran while one was open for 3% -> 5% of each run, Pallas kernels for 7% -> 8%
where the time goes in v4:
time: 304 us; the launch traced here: 303 us
  waiting for transfers between devices  123 us (40%)
  blocking collectives  103 us (34%)
  Pallas kernels  39 us (13%)
  between operations  13.9 us (5%)
  starting transfers between devices  9.72 us (3%)
  local copies, waits for them, and re-layouts  8.73 us (3%)
  other arithmetic  5.9 us (2%)
    unnamed x1, blocking collectives  103 us
    reduce_scatter x1, waiting for transfers between devices, body(): partial = lax.psum_scatter(partial, 'z', scatter_dimension=0, tiled=True)  75.4 us
    reduce_scatter x1, waiting for transfers between devices, body(): return lax.psum_scatter(partial, 'core', scatter_dimension=0, tiled=True)  28.9 us
    pallas_call x1, Pallas kernels, middle_product(): pl.pallas_call(functools.partial(middle_kernel, rows, slots), out_shape=j...  18 us
    ppermute x4, waiting for transfers between devices, from_behind(): lax.ppermute(value, axis, [(source, source + steps) for source in range(l...  17.8 us
    pallas_call x1, Pallas kernels, side_product(): pl.pallas_call(functools.partial(side_kernel, rows, slots), out_shape=jax...  15.3 us
    ppermute x4, starting transfers between devices, from_behind(): lax.ppermute(value, axis, [(source, source + steps) for source in range(l...  9.64 us
  transfers between devices with their start and end apart: 7, of which 5 were waited for; matrix products, arithmetic and copies ran while one was open for 5% of the time, Pallas kernels for 8%

profile of v4, /device:TPU:1, one launch (start us, length us, event | category | flops | bytes accessed | tf_op | source)
XLA Modules:
  0.0 303.4 jit_solution(14423317507377507262)
XLA Ops:
  6.5 0.7 all-gather.3.cloned.1.call-update
  7.3 0.8 copy.25
  8.1 1.3 dynamic-slice
  10.1 0.8 add_dynamic-update-slice_fusion
  10.9 102.6 %all-reduce = s32[3584]{0:T(1024)S(1)} all-reduce(s32[3584]{0:T(1024)S(1)} %add_dynamic-update-slice_fusion), channel_id=2, replica_groups=mesh['row'=16,'z'=16,'core'=2] {'z','core'}, use_global_device_ids=true, to_apply=%add | all-reduce | flops 3584 | bytes 28672
  114.1 0.6 gather_fusion
  114.7 3.4 %collective-permute-start = (s32[32,2]{1,0:T(8,128)S(1)}, s32[32,2]{1,0:T(8,128)S(1)}, u32[]{:S(2)}, u32[]{:S(2)}) collective-permute-start(s32[32,2]{1,0:T(8,128)S(1)} %gather_fusion), channel_id=1, source_target_pairs={{0,32},{32,64},{64,96},{96,128},{128,160},{160,192},{192,224},{224... | collective-permute-start | bytes 776 | tf_op jit(solution)/shard_map/ppermute | solution.py:17
  118.1 0.6 gather_fusion.1
  118.7 1.3 collective-permute-start.1
  120.0 0.7 broadcast_clamp_fusion.3
  120.8 0.6 gather_fusion.3
  121.4 0.6 fusion.8
  122.0 0.7 broadcast_compare_fusion
  122.7 0.5 all-gather.3.cloned.1.call-done.group_ref
  123.2 5.7 %shard_map.55 = (bf16[32,2,128,128]{3,2,1,0:T(8,128)(2,1)}, bf16[32,2,128,128]{3,2,1,0:T(8,128)(2,1)}) custom-call(s32[32]{0:T(128)} %get-tuple-element.22.up_sel, s32[32]{0:T(128)} %get-tuple-element.21.down_sel, bf16[256,2,128,128]{3,2,1,0:T(8,128)(2,1)} %all-gather.3.cloned.1.call-done.group_ref), custom_call_target="tpu_custom_call" | custom-call | bytes 8388608 | tf_op jit(solution)/shard_map/pallas_call | solution.py:155
  128.9 3.6 %collective-permute-start.2 = (bf16[32,2,128,128]{3,2,1,0:T(8,128)(2,1)}, bf16[32,2,128,128]{3,2,1,0:T(8,128)(2,1)S(1)}, u32[]{:S(2)}, u32[]{:S(2)}) collective-permute-start(bf16[32,2,128,128]{3,2,1,0:T(8,128)(2,1)} %get-tuple-element.7), channel_id=1, source_target_pairs={{0,32},{32,64},{64,96},{96,128},{128,160},{160,192},{192,224},{224... | collective-permute-start | bytes 6291464 | tf_op jit(solution)/shard_map/ppermute | solution.py:17
  132.6 1.3 collective-permute-start.3
  134.1 0.5 fusion.7.sel_ref
  134.6 0.6 compare_select_fusion.8
  135.2 0.6 and_convert_fusion
  136.8 0.7 reshape.144.pcol_ref
  137.5 1.0 copy.27
  138.5 0.6 gather_fusion.4
  139.1 0.7 reshape.145.lcol_ref
  139.9 0.6 gather_fusion.2
  140.5 0.7 reshape.143.lcol_ref
  141.2 18.0 %shard_map.56.prior_ref = f32[4,128,1536]{2,1,0:T(8,128)} custom-call(s32[128]{0:T(128)} %get-tuple-element.19.src_ref, s32[128]{0:T(128)} %get-tuple-element.17.live_ref, s32[256]{0:T(256)} %reshape.145.lcol_ref, s32[16]{0:T(128)} %reshape.144.pcol_ref, s32[32]{0:T(128)} %fusion.7.sel_ref, bf16[8,16,128,128]{3,2,1,0:T(8,128)(2,1)} %a_ref.3, ...), custom_call_target="tpu_custom_call" | custom-call | flops 1879048192 | bytes 9961472 | tf_op jit(solution)/shard_map/pallas_call | solution.py:115
  159.2 13.9 %collective-permute-done.2.lower_ref = bf16[32,2,128,128]{3,2,1,0:T(8,128)(2,1)S(1)} collective-permute-done((bf16[32,2,128,128]{3,2,1,0:T(8,128)(2,1)}, bf16[32,2,128,128]{3,2,1,0:T(8,128)(2,1)S(1)}, u32[]{:S(2)}, u32[]{:S(2)}) %collective-permute-start.2) | collective-permute-done | bytes 2097184 | tf_op jit(solution)/shard_map/ppermute | solution.py:17
  173.1 4.0 %collective-permute-done.3.upper_ref = bf16[32,2,128,128]{3,2,1,0:T(8,128)(2,1)} collective-permute-done((bf16[32,2,128,128]{3,2,1,0:T(8,128)(2,1)}, bf16[32,2,128,128]{3,2,1,0:T(8,128)(2,1)}, u32[]{:S(2)}, u32[]{:S(2)}) %collective-permute-start.3) | collective-permute-done | bytes 2097184 | tf_op jit(solution)/shard_map/ppermute | solution.py:17
  177.1 15.3 %shard_map.57 = f32[4,128,1536]{2,1,0:T(8,128)} custom-call(s32[128]{0:T(128)} %compare_select_fusion.7.src_ref, s32[128]{0:T(128)} %and_convert_fusion.1.live_ref, s32[256]{0:T(256)} %reshape.143.lcol_ref, s32[16]{0:T(128)} %reshape.144.pcol_ref, bf16[8,16,128,128]{3,2,1,0:T(8,128)(2,1)} %a_ref.3, ...), custom_call_target="tpu_custom_call", output_to_operand_aliasing={{}: (8, {})} | custom-call | flops 1879048192 | bytes 11534336 | tf_op jit(solution)/shard_map/pallas_call | solution.py:134
  192.5 75.4 %reduce-scatter.3.cloned.1.call-done = f32[32,1536]{1,0:T(8,128)} async-done(((f32[512,1536]{1,0:T(8,128)}), f32[32,1536]{1,0:T(8,128)}) %reduce-scatter.3.cloned.1.call-update) | async-done | bytes 196624 | tf_op jit(solution)/shard_map/reduce_scatter | solution.py:229
  267.9 28.9 %reduce-scatter.5.cloned.1.call-done = f32[16,1536]{1,0:T(8,128)} async-done(((f32[32,1536]{1,0:T(8,128)}), f32[16,1536]{1,0:T(8,128)}) %reduce-scatter.5.cloned.1.call-update) | async-done | bytes 98320 | tf_op jit(solution)/shard_map/reduce_scatter | solution.py:230
  (35 shorter events, 2.1 us)
Async XLA Ops:
  6.5 116.7 %all-gather.3.cloned.1.call-start = ((), (), s32[]{:S(2)}) async-start(), calls=%async_computation.2 | async-start | bytes 17301504 | tf_op jit(solution)/shard_map/all_gather | solution.py:181
  7.3 260.6 %reduce-scatter.3.cloned.1.call-start = ((), (), s32[]{:S(2)}) async-start(), calls=%async_computation.3 | async-start | bytes 3342336 | tf_op jit(solution)/shard_map/reduce_scatter | solution.py:229
  114.7 25.2 %collective-permute-start = (s32[32,2]{1,0:T(8,128)S(1)}, s32[32,2]{1,0:T(8,128)S(1)}, u32[]{:S(2)}, u32[]{:S(2)}) collective-permute-start(s32[32,2]{1,0:T(8,128)S(1)} %gather_fusion), channel_id=1, source_target_pairs={{0,32},{32,64},{64,96},{96,128},{128,160},{160,192},{192,224},{224... | collective-permute-start | bytes 776 | tf_op jit(solution)/shard_map/ppermute | solution.py:17
  118.7 21.2 %collective-permute-start.1 = (s32[32,2]{1,0:T(8,128)S(1)}, s32[32,2]{1,0:T(8,128)S(1)}, u32[]{:S(2)}, u32[]{:S(2)}) collective-permute-start(s32[32,2]{1,0:T(8,128)S(1)} %gather_fusion.1), channel_id=1, source_target_pairs={{32,0},{64,32},{96,64},{128,96},{160,128},{192,160},{224,192},{256... | collective-permute-start | bytes 776 | tf_op jit(solution)/shard_map/ppermute | solution.py:17
  123.2 14.3 %copy-start.1 = (bf16[8,2,128,128]{3,2,1,0:T(8,128)(2,1)S(1)}, bf16[8,2,128,128]{3,2,1,0:T(8,128)(2,1)}, u32[]{:S(2)}) copy-start(bf16[8,2,128,128]{3,2,1,0:T(8,128)(2,1)} %param.7) | copy-start | bytes 1572868
  128.9 44.2 %collective-permute-start.2 = (bf16[32,2,128,128]{3,2,1,0:T(8,128)(2,1)}, bf16[32,2,128,128]{3,2,1,0:T(8,128)(2,1)S(1)}, u32[]{:S(2)}, u32[]{:S(2)}) collective-permute-start(bf16[32,2,128,128]{3,2,1,0:T(8,128)(2,1)} %get-tuple-element.7), channel_id=1, source_target_pairs={{0,32},{32,64},{64,96},{96,128},{128,160},{160,192},{192,224},{224... | collective-permute-start | bytes 6291464 | tf_op jit(solution)/shard_map/ppermute | solution.py:17
  132.6 44.5 %collective-permute-start.3 = (bf16[32,2,128,128]{3,2,1,0:T(8,128)(2,1)}, bf16[32,2,128,128]{3,2,1,0:T(8,128)(2,1)}, u32[]{:S(2)}, u32[]{:S(2)}) collective-permute-start(bf16[32,2,128,128]{3,2,1,0:T(8,128)(2,1)} %get-tuple-element.8), channel_id=1, source_target_pairs={{32,0},{64,32},{96,64},{128,96},{160,128},{192,160},{224,192},{256... | collective-permute-start | bytes 6291464 | tf_op jit(solution)/shard_map/ppermute | solution.py:17
  173.1 4.0 %copy-start = (bf16[32,2,128,128]{3,2,1,0:T(8,128)(2,1)}, bf16[32,2,128,128]{3,2,1,0:T(8,128)(2,1)S(1)}, u32[]{:S(2)}) copy-start(bf16[32,2,128,128]{3,2,1,0:T(8,128)(2,1)S(1)} %collective-permute-done.2.lower_ref) | copy-start | bytes 6291460
  192.4 104.4 %reduce-scatter.5.cloned.1.call-start = ((), (), s32[]{:S(2)}) async-start(), calls=%async_computation.4 | async-start | bytes 294912 | tf_op jit(solution)/shard_map/reduce_scatter | solution.py:230
Sparse Core Ops, SparseCore 0:
  9.5 113.6 all-gather.2
  192.5 75.2 reduce-scatter.2
  270.6 26.1 reduce-scatter.4

commit v5 on v4

--- a/solution.py
+++ b/solution.py
@@ -20,7 +20,8 @@
 def accumulate_rows(rows, slots, spans, src_ref, live_ref, lcol_ref, pcol_ref, a_ref, b_ref, pt_ref, out_ref, acc_ref):
     bs = a_ref.shape[-1]
     for i in range(rows):
-        acc_ref[...] = jnp.zeros_like(acc_ref)
+        for lo, hi in spans:
+            acc_ref[:, lo * bs : hi * bs] = jnp.zeros((bs, (hi - lo) * bs), jnp.float32)
 
         def slot(k, carry):
             s = i * slots + k
@@ -227,7 +228,11 @@
     )
     partial = partial.reshape(CG * block_size, 3 * CG * block_size)
     partial = lax.psum_scatter(partial, "z", scatter_dimension=0, tiled=True)
-    return lax.psum_scatter(partial, "core", scatter_dimension=0, tiled=True)
+    k = lax.axis_index("core")
+    half = partial.shape[0] // 2
+    mine = lax.dynamic_slice_in_dim(partial, k * half, half, axis=0)
+    other = lax.dynamic_slice_in_dim(partial, (1 - k) * half, half, axis=0)
+    return mine + lax.ppermute(other, "core", [(0, 1), (1, 0)])
 
 
 def solution(mesh):

time: 304 us -> 290 us (0.954)
  waiting for transfers between devices: 123 us -> 94.1 us
  starting transfers between devices: 9.72 us -> 21.9 us
    reduce_scatter x1 -> x0, waiting for transfers between devices: 28.9 us -> none  [body(): return lax.psum_scatter(partial, 'core', scatter_dimension=0, tiled=True)]
    ppermute x0 -> x1, starting transfers between devices: none -> 12.2 us  [body(): return mine + lax.ppermute(other, 'core', [(0, 1), (1, 0)])]
where the time goes in v5:
time: 290 us; the launch traced here: 289 us
  blocking collectives  103 us (36%)
  waiting for transfers between devices  94.1 us (32%)
  Pallas kernels  39.1 us (13%)
  starting transfers between devices  21.9 us (8%)
  between operations  14.2 us (5%)
  local copies, waits for them, and re-layouts  9.62 us (3%)
  other arithmetic  7.45 us (3%)
    unnamed x1, blocking collectives  103 us
    reduce_scatter x1, waiting for transfers between devices, body(): partial = lax.psum_scatter(partial, 'z', scatter_dimension=0, tiled=True)  74.4 us
    pallas_call x1, Pallas kernels, middle_product(): pl.pallas_call(functools.partial(middle_kernel, rows, slots), out_shape=j...  18.3 us
    ppermute x4, waiting for transfers between devices, from_behind(): lax.ppermute(value, axis, [(source, source + steps) for source in range(l...  17.6 us
    pallas_call x1, Pallas kernels, side_product(): pl.pallas_call(functools.partial(side_kernel, rows, slots), out_shape=jax...  15.1 us
    ppermute x1, starting transfers between devices, body(): return mine + lax.ppermute(other, 'core', [(0, 1), (1, 0)])  12.2 us
    ppermute x4, starting transfers between devices, from_behind(): lax.ppermute(value, axis, [(source, source + steps) for source in range(l...  9.64 us
  transfers between devices with their start and end apart: 7, of which 5 were waited for; matrix products, arithmetic and copies ran while one was open for 5% of the time, Pallas kernels for 8%

profile of v5, /device:TPU:1, one launch (start us, length us, event | category | flops | bytes accessed | tf_op | source)
XLA Modules:
  0.0 289.1 jit_solution(12571714758364620006)
XLA Ops:
  6.5 0.7 all-gather.3.cloned.1.call-update
  7.3 0.8 copy.25
  8.1 1.3 dynamic-slice
  10.1 0.8 add_dynamic-update-slice_fusion
  10.9 102.6 %all-reduce = s32[3584]{0:T(1024)S(1)} all-reduce(s32[3584]{0:T(1024)S(1)} %add_dynamic-update-slice_fusion), channel_id=2, replica_groups=mesh['row'=16,'z'=16,'core'=2] {'z','core'}, use_global_device_ids=true, to_apply=%add | all-reduce | flops 3584 | bytes 28672
  114.1 0.6 gather_fusion
  114.7 3.4 %collective-permute-start = (s32[32,2]{1,0:T(8,128)S(1)}, s32[32,2]{1,0:T(8,128)S(1)}, u32[]{:S(2)}, u32[]{:S(2)}) collective-permute-start(s32[32,2]{1,0:T(8,128)S(1)} %gather_fusion), channel_id=1, source_target_pairs={{0,32},{32,64},{64,96},{96,128},{128,160},{160,192},{192,224},{224... | collective-permute-start | bytes 776 | tf_op jit(solution)/shard_map/ppermute | solution.py:17
  118.7 1.3 collective-permute-start.1
  120.0 0.7 broadcast_clamp_fusion.3
  120.8 0.6 gather_fusion.3
  121.4 0.6 fusion.8
  122.0 0.7 broadcast_compare_fusion
  123.2 5.7 %shard_map.55 = (bf16[32,2,128,128]{3,2,1,0:T(8,128)(2,1)}, bf16[32,2,128,128]{3,2,1,0:T(8,128)(2,1)}) custom-call(s32[32]{0:T(128)} %get-tuple-element.22.up_sel, s32[32]{0:T(128)} %get-tuple-element.21.down_sel, bf16[256,2,128,128]{3,2,1,0:T(8,128)(2,1)} %all-gather.3.cloned.1.call-done.group_ref), custom_call_target="tpu_custom_call" | custom-call | bytes 8388608 | tf_op jit(solution)/shard_map/pallas_call | solution.py:156
  128.9 3.6 %collective-permute-start.2 = (bf16[32,2,128,128]{3,2,1,0:T(8,128)(2,1)}, bf16[32,2,128,128]{3,2,1,0:T(8,128)(2,1)S(1)}, u32[]{:S(2)}, u32[]{:S(2)}) collective-permute-start(bf16[32,2,128,128]{3,2,1,0:T(8,128)(2,1)} %get-tuple-element.7), channel_id=1, source_target_pairs={{0,32},{32,64},{64,96},{96,128},{128,160},{160,192},{192,224},{224... | collective-permute-start | bytes 6291464 | tf_op jit(solution)/shard_map/ppermute | solution.py:17
  132.6 1.3 collective-permute-start.3
  134.6 0.6 compare_select_fusion.8
  135.2 0.6 and_convert_fusion
  136.8 0.7 reshape.144.pcol_ref
  137.5 1.0 copy.27
  138.5 0.6 gather_fusion.4
  139.1 0.7 reshape.145.lcol_ref
  139.9 0.6 gather_fusion.2
  140.5 0.7 reshape.143.lcol_ref
  141.2 18.3 %shard_map.56.prior_ref = f32[4,128,1536]{2,1,0:T(8,128)} custom-call(s32[128]{0:T(128)} %get-tuple-element.19.src_ref, s32[128]{0:T(128)} %get-tuple-element.17.live_ref, s32[256]{0:T(256)} %reshape.145.lcol_ref, s32[16]{0:T(128)} %reshape.144.pcol_ref, s32[32]{0:T(128)} %fusion.7.sel_ref, bf16[8,16,128,128]{3,2,1,0:T(8,128)(2,1)} %a_ref.3, ...), custom_call_target="tpu_custom_call" | custom-call | flops 1879048192 | bytes 9961472 | tf_op jit(solution)/shard_map/pallas_call | solution.py:116
  159.5 13.6 %collective-permute-done.2.lower_ref = bf16[32,2,128,128]{3,2,1,0:T(8,128)(2,1)S(1)} collective-permute-done((bf16[32,2,128,128]{3,2,1,0:T(8,128)(2,1)}, bf16[32,2,128,128]{3,2,1,0:T(8,128)(2,1)S(1)}, u32[]{:S(2)}, u32[]{:S(2)}) %collective-permute-start.2) | collective-permute-done | bytes 2097184 | tf_op jit(solution)/shard_map/ppermute | solution.py:17
  173.1 4.0 %collective-permute-done.3.upper_ref = bf16[32,2,128,128]{3,2,1,0:T(8,128)(2,1)} collective-permute-done((bf16[32,2,128,128]{3,2,1,0:T(8,128)(2,1)}, bf16[32,2,128,128]{3,2,1,0:T(8,128)(2,1)}, u32[]{:S(2)}, u32[]{:S(2)}) %collective-permute-start.3) | collective-permute-done | bytes 2097184 | tf_op jit(solution)/shard_map/ppermute | solution.py:17
  177.1 15.1 %shard_map.57 = f32[4,128,1536]{2,1,0:T(8,128)} custom-call(s32[128]{0:T(128)} %compare_select_fusion.7.src_ref, s32[128]{0:T(128)} %and_convert_fusion.1.live_ref, s32[256]{0:T(256)} %reshape.143.lcol_ref, s32[16]{0:T(128)} %reshape.144.pcol_ref, bf16[8,16,128,128]{3,2,1,0:T(8,128)(2,1)} %a_ref.3, ...), custom_call_target="tpu_custom_call", output_to_operand_aliasing={{}: (8, {})} | custom-call | flops 1879048192 | bytes 11534336 | tf_op jit(solution)/shard_map/pallas_call | solution.py:135
  192.2 74.4 %reduce-scatter.2.cloned.1.call-done = f32[32,1536]{1,0:T(8,128)} async-done(((f32[512,1536]{1,0:T(8,128)}), f32[32,1536]{1,0:T(8,128)}) %reduce-scatter.2.cloned.1.call-update) | async-done | bytes 196624 | tf_op jit(solution)/shard_map/reduce_scatter | solution.py:230
  266.6 0.9 constant_dynamic-slice_fusion
  267.5 12.2 %collective-permute-start.4 = (f32[16,1536]{1,0:T(8,128)S(1)}, f32[16,1536]{1,0:T(8,128)S(1)}, u32[]{:S(2)}, u32[]{:S(2)}) collective-permute-start(f32[16,1536]{1,0:T(8,128)S(1)} %constant_dynamic-slice_fusion), channel_id=1, source_target_pairs={{0,1},{1,0},{2,3},{3,2},{4,5},{5,4},{6,7},{7,6},{8,9},{9,8},{10,11... | collective-permute-start | bytes 294920 | tf_op jit(solution)/shard_map/ppermute | solution.py:235
  279.8 0.9 collective-permute-done.4
  280.7 1.5 dynamic-slice_add_fusion
  (36 shorter events, 3.7 us)
Async XLA Ops:
  6.5 116.7 %all-gather.3.cloned.1.call-start = ((), (), s32[]{:S(2)}) async-start(), calls=%async_computation.1 | async-start | bytes 17301504 | tf_op jit(solution)/shard_map/all_gather | solution.py:182
  7.3 259.4 %reduce-scatter.2.cloned.1.call-start = ((), (), s32[]{:S(2)}) async-start(), calls=%async_computation.2 | async-start | bytes 3342336 | tf_op jit(solution)/shard_map/reduce_scatter | solution.py:230
  114.7 25.2 %collective-permute-start = (s32[32,2]{1,0:T(8,128)S(1)}, s32[32,2]{1,0:T(8,128)S(1)}, u32[]{:S(2)}, u32[]{:S(2)}) collective-permute-start(s32[32,2]{1,0:T(8,128)S(1)} %gather_fusion), channel_id=1, source_target_pairs={{0,32},{32,64},{64,96},{96,128},{128,160},{160,192},{192,224},{224... | collective-permute-start | bytes 776 | tf_op jit(solution)/shard_map/ppermute | solution.py:17
  118.7 21.2 %collective-permute-start.1 = (s32[32,2]{1,0:T(8,128)S(1)}, s32[32,2]{1,0:T(8,128)S(1)}, u32[]{:S(2)}, u32[]{:S(2)}) collective-permute-start(s32[32,2]{1,0:T(8,128)S(1)} %gather_fusion.1), channel_id=1, source_target_pairs={{32,0},{64,32},{96,64},{128,96},{160,128},{192,160},{224,192},{256... | collective-permute-start | bytes 776 | tf_op jit(solution)/shard_map/ppermute | solution.py:17
  123.2 14.3 %copy-start.1 = (bf16[8,2,128,128]{3,2,1,0:T(8,128)(2,1)S(1)}, bf16[8,2,128,128]{3,2,1,0:T(8,128)(2,1)}, u32[]{:S(2)}) copy-start(bf16[8,2,128,128]{3,2,1,0:T(8,128)(2,1)} %param.7) | copy-start | bytes 1572868
  128.9 44.2 %collective-permute-start.2 = (bf16[32,2,128,128]{3,2,1,0:T(8,128)(2,1)}, bf16[32,2,128,128]{3,2,1,0:T(8,128)(2,1)S(1)}, u32[]{:S(2)}, u32[]{:S(2)}) collective-permute-start(bf16[32,2,128,128]{3,2,1,0:T(8,128)(2,1)} %get-tuple-element.7), channel_id=1, source_target_pairs={{0,32},{32,64},{64,96},{96,128},{128,160},{160,192},{192,224},{224... | collective-permute-start | bytes 6291464 | tf_op jit(solution)/shard_map/ppermute | solution.py:17
  132.6 44.5 %collective-permute-start.3 = (bf16[32,2,128,128]{3,2,1,0:T(8,128)(2,1)}, bf16[32,2,128,128]{3,2,1,0:T(8,128)(2,1)}, u32[]{:S(2)}, u32[]{:S(2)}) collective-permute-start(bf16[32,2,128,128]{3,2,1,0:T(8,128)(2,1)} %get-tuple-element.8), channel_id=1, source_target_pairs={{32,0},{64,32},{96,64},{128,96},{160,128},{192,160},{224,192},{256... | collective-permute-start | bytes 6291464 | tf_op jit(solution)/shard_map/ppermute | solution.py:17
  173.1 4.0 %copy-start = (bf16[32,2,128,128]{3,2,1,0:T(8,128)(2,1)}, bf16[32,2,128,128]{3,2,1,0:T(8,128)(2,1)S(1)}, u32[]{:S(2)}) copy-start(bf16[32,2,128,128]{3,2,1,0:T(8,128)(2,1)S(1)} %collective-permute-done.2.lower_ref) | copy-start | bytes 6291460
  267.5 13.2 %collective-permute-start.4 = (f32[16,1536]{1,0:T(8,128)S(1)}, f32[16,1536]{1,0:T(8,128)S(1)}, u32[]{:S(2)}, u32[]{:S(2)}) collective-permute-start(f32[16,1536]{1,0:T(8,128)S(1)} %constant_dynamic-slice_fusion), channel_id=1, source_target_pairs={{0,1},{1,0},{2,3},{3,2},{4,5},{5,4},{6,7},{7,6},{8,9},{9,8},{10,11... | collective-permute-start | bytes 294920 | tf_op jit(solution)/shard_map/ppermute | solution.py:235
Sparse Core Ops, SparseCore 0:
  9.5 113.6 all-gather.2
  192.4 74.2 reduce-scatter.1

commit v6 on v5

--- a/solution.py
+++ b/solution.py
@@ -33,7 +33,7 @@
                 for p in range(2):
                     col = pl.multiple_of(lcol_ref[2 * s + p] * bs, bs)
                     acc_ref[:, pl.ds(col, bs)] += jnp.dot(
-                        a, b_ref[src, p], preferred_element_type=jnp.float32
+                        a, b_ref[p][src], preferred_element_type=jnp.float32
                     )
 
             return carry
@@ -48,14 +48,21 @@
                 )
 
 
-def middle_kernel(rows, slots, src_ref, live_ref, lcol_ref, pcol_ref, sel_ref, a_ref, group_ref, pt_ref, out_ref, buf_ref, acc_ref, sems):
-    own = buf_ref.shape[0] - sel_ref.shape[0]
+def middle_kernel(rows, slots, src_ref, live_ref, lcol_ref, pcol_ref, sel_ref, a_ref, group0_ref, group1_ref, pt_ref, out_ref, buf0_ref, buf1_ref, acc_ref, sems):
+    count = sel_ref.shape[0]
+    own = buf0_ref.shape[0] - count
     me = lax.axis_index("z") * lax.axis_size("core") + lax.axis_index("core")
-    copies = [pltpu.make_async_copy(group_ref.at[pl.ds(me * own, own)], buf_ref.at[pl.ds(0, own)], sems.at[0])]
-    for q in range(sel_ref.shape[0]):
+    copies = []
+    for p, (group_ref, buf_ref) in enumerate(((group0_ref, buf0_ref), (group1_ref, buf1_ref))):
+        base = p * (count + 1)
         copies.append(
-            pltpu.make_async_copy(group_ref.at[sel_ref[q]], buf_ref.at[own + q], sems.at[q + 1])
+            pltpu.make_async_copy(group_ref.at[pl.ds(me * own, own)], buf_ref.at[pl.ds(0, own)], sems.at[base])
         )
+        for q in range(count):
+            copies.append(
+                pltpu.make_async_copy(group_ref.at[sel_ref[q]], buf_ref.at[own + q], sems.at[base + q + 1])
+            )
+    buf_ref = (buf0_ref, buf1_ref)
     for cp in copies:
         cp.start()
     out_ref[...] = jnp.zeros_like(out_ref)
@@ -65,12 +72,15 @@
     accumulate_rows(rows, slots, spans, src_ref, live_ref, lcol_ref, pcol_ref, a_ref, buf_ref, pt_ref, out_ref, acc_ref)
 
 
-def side_kernel(rows, slots, src_ref, live_ref, lcol_ref, pcol_ref, a_ref, lower_ref, upper_ref, pt_ref, prior_ref, out_ref, buf_ref, acc_ref, sems):
-    half = lower_ref.shape[0]
+def side_kernel(rows, slots, src_ref, live_ref, lcol_ref, pcol_ref, a_ref, lower0_ref, lower1_ref, upper0_ref, upper1_ref, pt_ref, prior_ref, out_ref, buf0_ref, buf1_ref, acc_ref, sems):
+    half = lower0_ref.shape[0]
     copies = [
-        pltpu.make_async_copy(lower_ref, buf_ref.at[pl.ds(0, half)], sems.at[0]),
-        pltpu.make_async_copy(upper_ref, buf_ref.at[pl.ds(half, half)], sems.at[1]),
+        pltpu.make_async_copy(lower0_ref, buf0_ref.at[pl.ds(0, half)], sems.at[0]),
+        pltpu.make_async_copy(upper0_ref, buf0_ref.at[pl.ds(half, half)], sems.at[1]),
+        pltpu.make_async_copy(lower1_ref, buf1_ref.at[pl.ds(0, half)], sems.at[2]),
+        pltpu.make_async_copy(upper1_ref, buf1_ref.at[pl.ds(half, half)], sems.at[3]),
     ]
+    buf_ref = (buf0_ref, buf1_ref)
     for cp in copies:
         cp.start()
     out_ref[...] = prior_ref[...]
@@ -109,50 +119,52 @@
     )
 
 
-def middle_product(a_tiles, group_tiles, p_t, sel, src, live, lcol, pcol):
+def middle_product(a_tiles, group0, group1, p_t, sel, src, live, lcol, pcol):
     rows, slots, bs, _ = a_tiles.shape
     count = sel.shape[0]
     width = 3 * CG
     return pl.pallas_call(
         functools.partial(middle_kernel, rows, slots),
         out_shape=jax.ShapeDtypeStruct((CG, bs, width * bs), jnp.float32),
-        in_specs=[SMEM, SMEM, SMEM, SMEM, SMEM, VMEM, ANY, VMEM],
+        in_specs=[SMEM, SMEM, SMEM, SMEM, SMEM, VMEM, ANY, ANY, VMEM],
         out_specs=VMEM,
         scratch_shapes=[
-            pltpu.VMEM((rows + count, 2, bs, bs), jnp.bfloat16),
+            pltpu.VMEM((rows + count, bs, bs), jnp.bfloat16),
+            pltpu.VMEM((rows + count, bs, bs), jnp.bfloat16),
             pltpu.VMEM((bs, width * bs), jnp.float32),
-            pltpu.SemaphoreType.DMA((count + 1,)),
+            pltpu.SemaphoreType.DMA((2 * (count + 1),)),
         ],
         compiler_params=pltpu.CompilerParams(vmem_limit_bytes=VMEM_LIMIT),
         cost_estimate=cost(a_tiles, width, (rows + count) * 2 * bs * bs * 2),
-    )(src, live, lcol, pcol, sel, a_tiles, group_tiles, p_t)
-
-
-def side_product(a_tiles, lower, upper, p_t, src, live, lcol, pcol, prior):
+    )(src, live, lcol, pcol, sel, a_tiles, group0, group1, p_t)
+
+
+def side_product(a_tiles, lower0, lower1, upper0, upper1, p_t, src, live, lcol, pcol, prior):
     rows, slots, bs, _ = a_tiles.shape
-    count = lower.shape[0]
+    count = lower0.shape[0]
     width = 3 * CG
     return pl.pallas_call(
         functools.partial(side_kernel, rows, slots),
         out_shape=jax.ShapeDtypeStruct((CG, bs, width * bs), jnp.float32),
-        in_specs=[SMEM, SMEM, SMEM, SMEM, VMEM, ANY, ANY, VMEM, VMEM],
-        input_output_aliases={8: 0},
+        in_specs=[SMEM, SMEM, SMEM, SMEM, VMEM, ANY, ANY, ANY, ANY, VMEM, VMEM],
+        input_output_aliases={10: 0},
         out_specs=VMEM,
         scratch_shapes=[
-            pltpu.VMEM((2 * count, 2, bs, bs), jnp.bfloat16),
+            pltpu.VMEM((2 * count, bs, bs), jnp.bfloat16),
+            pltpu.VMEM((2 * count, bs, bs), jnp.bfloat16),
             pltpu.VMEM((bs, width * bs), jnp.float32),
-            pltpu.SemaphoreType.DMA((2,)),
+            pltpu.SemaphoreType.DMA((4,)),
         ],
         compiler_params=pltpu.CompilerParams(vmem_limit_bytes=VMEM_LIMIT),
         cost_estimate=cost(a_tiles, width, 2 * count * 2 * bs * bs * 2),
-    )(src, live, lcol, pcol, a_tiles, lower, upper, p_t, prior)
+    )(src, live, lcol, pcol, a_tiles, lower0, lower1, upper0, upper1, p_t, prior)
 
 
 def pick_rows(group_tiles, up_sel, down_sel):
     count = up_sel.shape[0]
     shape = (count,) + group_tiles.shape[1:]
     out = jax.ShapeDtypeStruct(shape, group_tiles.dtype)
-    nbytes = 2 * 2 * count * group_tiles[0].size * 2
+    nbytes = 2 * 2 * count * group_tiles[0].size
     return pl.pallas_call(
         pick_kernel,
         out_shape=(out, out),
@@ -179,7 +191,7 @@
     group_ints = lax.all_gather(ints, ("z", "core"))
     group_pcols = group_ints[:, : own_rows * tile_count].reshape(-1, tile_count)
     group_send = group_ints[:, own_rows * tile_count :]
-    group_tiles = lax.all_gather(p_tiles, ("z", "core"), tiled=True)
+    group0 = lax.all_gather(p_tiles[:, 0], ("z", "core"), tiled=True)
 
     q = jnp.arange(col_count, dtype=jnp.int32)
     base = q * own_rows
@@ -188,13 +200,18 @@
         return base + jnp.clip(group_send[:, 3 * c + t], 0, own_rows - 1)
 
     up_sel, mid_sel, down_sel = selection(0), selection(1), selection(2)
-    up_tiles, down_tiles = pick_rows(group_tiles, up_sel, down_sel)
+    up0, down0 = pick_rows(group0, up_sel, down_sel)
+    second, up0, down0 = lax.optimization_barrier((p_tiles[:, 1], up0, down0))
+    lower0, upper0 = from_behind(up0, "row", 1), from_behind(down0, "row", -1)
+    group1 = lax.all_gather(second, ("z", "core"), tiled=True)
+    up1, down1 = pick_rows(group1, up_sel, down_sel)
+    lower1, upper1 = from_behind(up1, "row", 1), from_behind(down1, "row", -1)
 
     def cols_of(t):
         return group_pcols[q * own_rows + jnp.clip(group_send[:, 3 * c + t], 0, own_rows - 1)]
 
-    lower_tiles, lower_cols = from_behind((up_tiles, cols_of(0)), "row", 1)
-    upper_tiles, upper_cols = from_behind((down_tiles, cols_of(2)), "row", -1)
+    lower_cols = from_behind(cols_of(0), "row", 1)
+    upper_cols = from_behind(cols_of(2), "row", -1)
     mid_cols = cols_of(1)
 
     b = a_cols.reshape(-1)
@@ -222,9 +239,9 @@
 
     p_t = jnp.swapaxes(p_tiles, -1, -2)
     pcol = pcol.reshape(-1)
-    mid = middle_product(a_tiles, group_tiles, p_t, mid_sel, mid_src, mid_live, mid_lcol, pcol)
+    mid = middle_product(a_tiles, group0, group1, p_t, mid_sel, mid_src, mid_live, mid_lcol, pcol)
     partial = side_product(
-        a_tiles, lower_tiles, upper_tiles, p_t, side_src, side_live, side_lcol, pcol, mid
+        a_tiles, lower0, lower1, upper0, upper1, p_t, side_src, side_live, side_lcol, pcol, mid
     )
     partial = partial.reshape(CG * block_size, 3 * CG * block_size)
     partial = lax.psum_scatter(partial, "z", scatter_dimension=0, tiled=True)

time: 290 us -> 355 us (1.22)
  waiting for transfers between devices: 94.1 us -> 155 us
  starting transfers between devices: 21.9 us -> 26.7 us
  blocking collectives: 103 us -> 98.7 us
    all_gather x1 -> x2, waiting for transfers between devices: 0.53 us -> 68.2 us  [the longest x1 68.2 us: body(): group1 = lax.all_gather(second, ('z', 'core'), tiled=True)]
    reduce_scatter x1, waiting for transfers between devices: 74.4 us -> 65.9 us  [body(): partial = lax.psum_scatter(partial, 'z', scatter_dimension=0, tiled=True)]
    ppermute x4 -> x6, starting transfers between devices: 9.64 us -> 14.6 us  [from_behind(): lax.ppermute(value, axis, [(source, source + steps) for source in range(l...]
    unnamed x1, blocking collectives: 103 us -> 98.7 us
    pallas_call x1 -> x2, Pallas kernels: 5.72 us -> 8.34 us  [pick_rows(): pl.pallas_call(pick_kernel, out_shape=(out, out), in_specs=[SMEM, SMEM, A...]
    ppermute x4 -> x6, waiting for transfers between devices: 17.6 us -> 20.1 us  [from_behind(): lax.ppermute(value, axis, [(source, source + steps) for source in range(l...]
  transfers between devices with their start and end apart: 7 -> 10, of which waited for: 5 -> 4; matrix products, arithmetic and copies ran while one was open for 5% -> 4% of each run, Pallas kernels for 8% -> 6%
where the time goes in v6:
time: 355 us; the launch traced here: 354 us
  waiting for transfers between devices  155 us (44%)
  blocking collectives  98.7 us (28%)
  Pallas kernels  40.9 us (12%)
  starting transfers between devices  26.7 us (8%)
  between operations  14 us (4%)
  local copies, waits for them, and re-layouts  12.7 us (4%)
  other arithmetic  6.04 us (2%)
    unnamed x1, blocking collectives  98.7 us
    all_gather x1, waiting for transfers between devices, body(): group1 = lax.all_gather(second, ('z', 'core'), tiled=True)  68.2 us
    reduce_scatter x1, waiting for transfers between devices, body(): partial = lax.psum_scatter(partial, 'z', scatter_dimension=0, tiled=True)  65.9 us
    ppermute x6, waiting for transfers between devices, from_behind(): lax.ppermute(value, axis, [(source, source + steps) for source in range(l...  20.1 us
    pallas_call x1, Pallas kernels, middle_product(): pl.pallas_call(functools.partial(middle_kernel, rows, slots), out_shape=j...  17.4 us
    pallas_call x1, Pallas kernels, side_product(): pl.pallas_call(functools.partial(side_kernel, rows, slots), out_shape=jax...  15.2 us
    ppermute x6, starting transfers between devices, from_behind(): lax.ppermute(value, axis, [(source, source + steps) for source in range(l...  14.6 us
    ppermute x1, starting transfers between devices, body(): return mine + lax.ppermute(other, 'core', [(0, 1), (1, 0)])  12 us
  transfers between devices with their start and end apart: 10, of which 4 were waited for; matrix products, arithmetic and copies ran while one was open for 4% of the time, Pallas kernels for 6%

profile of v6, /device:TPU:1, one launch (start us, length us, event | category | flops | bytes accessed | tf_op | source)
XLA Modules:
  0.0 354.2 jit_solution(5309491099455114916)
XLA Ops:
  6.5 1.9 fusion.11
  8.5 0.8 copy.32
  9.3 1.3 dynamic-slice
  11.3 0.8 add_dynamic-update-slice_fusion
  12.1 98.7 %all-reduce = s32[3584]{0:T(1024)S(1)} all-reduce(s32[3584]{0:T(1024)S(1)} %add_dynamic-update-slice_fusion), channel_id=2, replica_groups=mesh['row'=16,'z'=16,'core'=2] {'z','core'}, use_global_device_ids=true, to_apply=%add | all-reduce | flops 3584 | bytes 28672
  111.7 4.2 %shard_map.55 = (bf16[32,128,128]{2,1,0:T(8,128)(2,1)}, bf16[32,128,128]{2,1,0:T(8,128)(2,1)}) custom-call(s32[32]{0:T(128)} %get-tuple-element.34.up_sel, s32[32]{0:T(128)} %get-tuple-element.33.down_sel, bf16[256,128,128]{2,1,0:T(8,128)(2,1)} %bitcast.14), custom_call_target="tpu_custom_call" | custom-call | bytes 2097152 | tf_op jit(solution)/shard_map/pallas_call | solution.py:168
  116.1 0.6 gather_fusion
  116.7 3.4 collective-permute-start
  120.4 0.6 gather_fusion.3
  121.6 0.6 compare_select_fusion.8
  123.3 3.2 collective-permute-start.2
  126.5 1.3 collective-permute-start.4
  127.8 68.2 %all-gather.5.cloned.1.call-done.group_ref.group1_ref = bf16[256,128,128]{2,1,0:T(8,128)(2,1)} async-done(((bf16[8,128,128]{2,1,0:T(8,128)(2,1)}), bf16[256,128,128]{2,1,0:T(8,128)(2,1)}) %all-gather.5.cloned.1.call-update) | async-done | bytes 8388624 | tf_op jit(solution)/shard_map/all_gather | solution.py:206
  196.1 4.1 %shard_map.56 = (bf16[32,128,128]{2,1,0:T(8,128)(2,1)}, bf16[32,128,128]{2,1,0:T(8,128)(2,1)}) custom-call(s32[32]{0:T(128)} %get-tuple-element.34.up_sel, s32[32]{0:T(128)} %get-tuple-element.33.down_sel, bf16[256,128,128]{2,1,0:T(8,128)(2,1)} %all-gather.5.cloned.1.call-done.group_ref.group1_ref), custom_call_target="tpu_custom_call" | custom-call | bytes 2097152 | tf_op jit(solution)/shard_map/pallas_call | solution.py:168
  200.2 4.2 %collective-permute-start.3 = (bf16[32,128,128]{2,1,0:T(8,128)(2,1)}, bf16[32,128,128]{2,1,0:T(8,128)(2,1)}, u32[]{:S(2)}, u32[]{:S(2)}) collective-permute-start(bf16[32,128,128]{2,1,0:T(8,128)(2,1)} %get-tuple-element.16), channel_id=1, source_target_pairs={{0,32},{32,64},{64,96},{96,128},{128,160},{160,192},{192,224},{224... | collective-permute-start | bytes 3145736 | tf_op jit(solution)/shard_map/ppermute | solution.py:17
  204.4 1.3 collective-permute-start.5
  206.2 0.6 reshape.144.pcol_ref
  206.8 1.0 copy.35
  208.4 0.6 gather_fusion.4
  209.0 0.7 reshape.145.lcol_ref
  209.7 1.3 collective-permute-start.1
  211.0 20.1 %collective-permute-done.1 = s32[32,2]{1,0:T(8,128)S(1)} collective-permute-done((s32[32,2]{1,0:T(8,128)S(1)}, s32[32,2]{1,0:T(8,128)S(1)}, u32[]{:S(2)}, u32[]{:S(2)}) %collective-permute-start.1) | collective-permute-done | bytes 288 | tf_op jit(solution)/shard_map/ppermute | solution.py:17
  231.1 0.6 gather_fusion.2
  231.8 0.7 reshape.143.lcol_ref
  232.5 17.4 %shard_map.57.prior_ref = f32[4,128,1536]{2,1,0:T(8,128)} custom-call(s32[128]{0:T(128)} %get-tuple-element.29.src_ref, s32[128]{0:T(128)} %get-tuple-element.27.live_ref, s32[256]{0:T(256)} %reshape.145.lcol_ref, s32[16]{0:T(128)} %reshape.144.pcol_ref, s32[32]{0:T(128)} %fusion.7.sel_ref, bf16[8,16,128,128]{3,2,1,0:T(8,128)(2,1)} %a_ref.3, ...), custom_call_target="tpu_custom_call" | custom-call | flops 1879048192 | bytes 9961472 | tf_op jit(solution)/shard_map/pallas_call | solution.py:126
  249.9 0.9 copy-done.1
  251.2 15.2 %shard_map.58 = f32[4,128,1536]{2,1,0:T(8,128)} custom-call(s32[128]{0:T(128)} %compare_select_fusion.7.src_ref, s32[128]{0:T(128)} %and_convert_fusion.1.live_ref, s32[256]{0:T(256)} %reshape.143.lcol_ref, s32[16]{0:T(128)} %reshape.144.pcol_ref, bf16[8,16,128,128]{3,2,1,0:T(8,128)(2,1)} %a_ref.3, ...), custom_call_target="tpu_custom_call", output_to_operand_aliasing={{}: (10, {})} | custom-call | flops 1879048192 | bytes 11534336 | tf_op jit(solution)/shard_map/pallas_call | solution.py:146
  266.4 65.9 %reduce-scatter.2.cloned.1.call-done = f32[32,1536]{1,0:T(8,128)} async-done(((f32[512,1536]{1,0:T(8,128)}), f32[32,1536]{1,0:T(8,128)}) %reduce-scatter.2.cloned.1.call-update) | async-done | bytes 196624 | tf_op jit(solution)/shard_map/reduce_scatter | solution.py:247
  332.3 0.9 constant_dynamic-slice_fusion
  333.2 12.0 %collective-permute-start.6 = (f32[16,1536]{1,0:T(8,128)S(1)}, f32[16,1536]{1,0:T(8,128)S(1)}, u32[]{:S(2)}, u32[]{:S(2)}) collective-permute-start(f32[16,1536]{1,0:T(8,128)S(1)} %constant_dynamic-slice_fusion), channel_id=1, source_target_pairs={{0,1},{1,0},{2,3},{3,2},{4,5},{5,4},{6,7},{7,6},{8,9},{9,8},{10,11... | collective-permute-start | bytes 294920 | tf_op jit(solution)/shard_map/ppermute | solution.py:252
  345.2 0.9 collective-permute-done.6
  346.1 1.5 dynamic-slice_add_fusion
  (49 shorter events, 4.7 us)
Async XLA Ops:
  6.5 105.2 %all-gather.7.cloned.1.call-start = ((), (), s32[]{:S(2)}) async-start(), calls=%async_computation.3 | async-start | bytes 8650752 | tf_op jit(solution)/shard_map/all_gather | solution.py:194
  8.4 187.6 %all-gather.5.cloned.1.call-start = ((), (), s32[]{:S(2)}) async-start(), calls=%async_computation.1 | async-start | bytes 8650752 | tf_op jit(solution)/shard_map/all_gather | solution.py:206
  111.7 8.4 %copy-start.3 = (s32[8,16]{1,0:T(8,128)S(1)}, s32[8,16]{1,0:T(8,128)}, u32[]{:S(2)}) copy-start(s32[8,16]{1,0:T(8,128)} %param.6) | copy-start | bytes 1540
  116.0 216.3 %reduce-scatter.2.cloned.1.call-start = ((), (), s32[]{:S(2)}) async-start(), calls=%async_computation.2 | async-start | bytes 3342336 | tf_op jit(solution)/shard_map/reduce_scatter | solution.py:247
  116.7 93.0 %collective-permute-start = (s32[32,2]{1,0:T(8,128)S(1)}, s32[32,2]{1,0:T(8,128)S(1)}, u32[]{:S(2)}, u32[]{:S(2)}) collective-permute-start(s32[32,2]{1,0:T(8,128)S(1)} %gather_fusion), channel_id=1, source_target_pairs={{0,32},{32,64},{64,96},{96,128},{128,160},{160,192},{192,224},{224... | collective-permute-start | bytes 776 | tf_op jit(solution)/shard_map/ppermute | solution.py:17
  123.3 83.5 %copy-start = (bf16[8,2,128,128]{3,2,1,0:T(8,128)(2,1)S(1)}, bf16[8,2,128,128]{3,2,1,0:T(8,128)(2,1)}, u32[]{:S(2)}) copy-start(bf16[8,2,128,128]{3,2,1,0:T(8,128)(2,1)} %param.7) | copy-start | bytes 1572868
  123.3 126.5 %collective-permute-start.2 = (bf16[32,128,128]{2,1,0:T(8,128)(2,1)}, bf16[32,128,128]{2,1,0:T(8,128)(2,1)S(1)}, u32[]{:S(2)}, u32[]{:S(2)}) collective-permute-start(bf16[32,128,128]{2,1,0:T(8,128)(2,1)} %get-tuple-element.14), channel_id=1, source_target_pairs={{0,32},{32,64},{64,96},{96,128},{128,160},{160,192},{192,224},{224... | collective-permute-start | bytes 3145736 | tf_op jit(solution)/shard_map/ppermute | solution.py:17
  126.5 123.3 %collective-permute-start.4 = (bf16[32,128,128]{2,1,0:T(8,128)(2,1)}, bf16[32,128,128]{2,1,0:T(8,128)(2,1)S(1)}, u32[]{:S(2)}, u32[]{:S(2)}) collective-permute-start(bf16[32,128,128]{2,1,0:T(8,128)(2,1)} %get-tuple-element.17), channel_id=1, source_target_pairs={{32,0},{64,32},{96,64},{128,96},{160,128},{192,160},{224,192},{256... | collective-permute-start | bytes 3145736 | tf_op jit(solution)/shard_map/ppermute | solution.py:17
  200.2 49.7 %collective-permute-start.3 = (bf16[32,128,128]{2,1,0:T(8,128)(2,1)}, bf16[32,128,128]{2,1,0:T(8,128)(2,1)}, u32[]{:S(2)}, u32[]{:S(2)}) collective-permute-start(bf16[32,128,128]{2,1,0:T(8,128)(2,1)} %get-tuple-element.16), channel_id=1, source_target_pairs={{0,32},{32,64},{64,96},{96,128},{128,160},{160,192},{192,224},{224... | collective-permute-start | bytes 3145736 | tf_op jit(solution)/shard_map/ppermute | solution.py:17
  204.4 45.5 %collective-permute-start.5 = (bf16[32,128,128]{2,1,0:T(8,128)(2,1)}, bf16[32,128,128]{2,1,0:T(8,128)(2,1)}, u32[]{:S(2)}, u32[]{:S(2)}) collective-permute-start(bf16[32,128,128]{2,1,0:T(8,128)(2,1)} %get-tuple-element.18), channel_id=1, source_target_pairs={{32,0},{64,32},{96,64},{128,96},{160,128},{192,160},{224,192},{256... | collective-permute-start | bytes 3145736 | tf_op jit(solution)/shard_map/ppermute | solution.py:17
  209.7 21.4 %collective-permute-start.1 = (s32[32,2]{1,0:T(8,128)S(1)}, s32[32,2]{1,0:T(8,128)S(1)}, u32[]{:S(2)}, u32[]{:S(2)}) collective-permute-start(s32[32,2]{1,0:T(8,128)S(1)} %gather_fusion.1), channel_id=1, source_target_pairs={{32,0},{64,32},{96,64},{128,96},{160,128},{192,160},{224,192},{256... | collective-permute-start | bytes 776 | tf_op jit(solution)/shard_map/ppermute | solution.py:17
  249.8 1.0 copy-start.1
  249.9 1.3 copy-start.2
  333.2 12.9 %collective-permute-start.6 = (f32[16,1536]{1,0:T(8,128)S(1)}, f32[16,1536]{1,0:T(8,128)S(1)}, u32[]{:S(2)}, u32[]{:S(2)}) collective-permute-start(f32[16,1536]{1,0:T(8,128)S(1)} %constant_dynamic-slice_fusion), channel_id=1, source_target_pairs={{0,1},{1,0},{2,3},{3,2},{4,5},{5,4},{6,7},{7,6},{8,9},{9,8},{10,11... | collective-permute-start | bytes 294920 | tf_op jit(solution)/shard_map/ppermute | solution.py:252
Sparse Core Ops, SparseCore 0:
  9.5 85.2 all-gather.6
  116.1 79.9 all-gather.4
  266.5 65.7 reduce-scatter.1

commit v7 on v5

--- a/solution.py
+++ b/solution.py
@@ -193,8 +193,11 @@
     def cols_of(t):
         return group_pcols[q * own_rows + jnp.clip(group_send[:, 3 * c + t], 0, own_rows - 1)]
 
-    lower_tiles, lower_cols = from_behind((up_tiles, cols_of(0)), "row", 1)
-    upper_tiles, upper_cols = from_behind((down_tiles, cols_of(2)), "row", -1)
+    lower_tiles = from_behind(up_tiles, "row", 1)
+    upper_tiles = from_behind(down_tiles, "row", -1)
+    up_cols, down_cols, up_tiles = lax.optimization_barrier((cols_of(0), cols_of(2), up_tiles))
+    lower_cols = from_behind(up_cols, "row", 1)
+    upper_cols = from_behind(down_cols, "row", -1)
     mid_cols = cols_of(1)
 
     b = a_cols.reshape(-1)

time: 290 us -> 292 us (level)
  transfers between devices with their start and end apart: 7 -> 7, of which waited for: 5 -> 4; matrix products, arithmetic and copies ran while one was open for 5% -> 5% of each run, Pallas kernels for 8% -> 6%
where the time goes in v7:
time: 292 us
  blocking collectives  102 us (35%)
  waiting for transfers between devices  94.3 us (32%)
  Pallas kernels  38.7 us (13%)
  starting transfers between devices  22.8 us (8%)
  between operations  14.2 us (5%)
  local copies, waits for them, and re-layouts  11.9 us (4%)
  other arithmetic  7.51 us (3%)
    unnamed x1, blocking collectives  102 us
    reduce_scatter x1, waiting for transfers between devices, body(): partial = lax.psum_scatter(partial, 'z', scatter_dimension=0, tiled=True)  72.8 us
    ppermute x4, waiting for transfers between devices, from_behind(): lax.ppermute(value, axis, [(source, source + steps) for source in range(l...  18.4 us
    pallas_call x1, Pallas kernels, middle_product(): pl.pallas_call(functools.partial(middle_kernel, rows, slots), out_shape=j...  18.1 us
    pallas_call x1, Pallas kernels, side_product(): pl.pallas_call(functools.partial(side_kernel, rows, slots), out_shape=jax...  15.1 us
    ppermute x1, starting transfers between devices, body(): return mine + lax.ppermute(other, 'core', [(0, 1), (1, 0)])  12.4 us
    ppermute x4, starting transfers between devices, from_behind(): lax.ppermute(value, axis, [(source, source + steps) for source in range(l...  10.4 us
  transfers between devices with their start and end apart: 7, of which 4 were waited for; matrix products, arithmetic and copies ran while one was open for 5% of the time, Pallas kernels for 6%

profile of v7, /device:TPU:1, one launch (start us, length us, event | category | flops | bytes accessed | tf_op | source)
XLA Modules:
  0.0 291.8 jit_solution(7098703515419240252)
XLA Ops:
  6.5 0.7 all-gather.3.cloned.1.call-update
  7.3 0.7 broadcast_clamp_fusion.3
  8.2 2.0 copy.27
  10.2 0.7 broadcast_compare_fusion
  11.0 0.8 copy.25
  11.8 1.3 dynamic-slice
  13.8 0.8 add_dynamic-update-slice_fusion
  14.6 102.4 %all-reduce = s32[3584]{0:T(1024)S(1)} all-reduce(s32[3584]{0:T(1024)S(1)} %add_dynamic-update-slice_fusion), channel_id=2, replica_groups=mesh['row'=16,'z'=16,'core'=2] {'z','core'}, use_global_device_ids=true, to_apply=%add | all-reduce | flops 3584 | bytes 28672
  118.7 0.6 reshape.144.pcol_ref
  119.9 0.6 gather_fusion.4
  120.6 0.7 reshape.145.lcol_ref
  121.3 0.6 fusion.8
  121.9 1.4 all-gather.3.cloned.1.call-done.group_ref
  123.3 5.4 %shard_map.55 = (bf16[32,2,128,128]{3,2,1,0:T(8,128)(2,1)}, bf16[32,2,128,128]{3,2,1,0:T(8,128)(2,1)}) custom-call(s32[32]{0:T(128)} %get-tuple-element.28.up_sel, s32[32]{0:T(128)} %get-tuple-element.27.down_sel, bf16[256,2,128,128]{3,2,1,0:T(8,128)(2,1)} %all-gather.3.cloned.1.call-done.group_ref), custom_call_target="tpu_custom_call" | custom-call | bytes 8388608 | tf_op jit(solution)/shard_map/pallas_call | solution.py:156
  128.7 3.2 %collective-permute-start.2 = (bf16[32,2,128,128]{3,2,1,0:T(8,128)(2,1)}, bf16[32,2,128,128]{3,2,1,0:T(8,128)(2,1)S(1)}, u32[]{:S(2)}, u32[]{:S(2)}) collective-permute-start(bf16[32,2,128,128]{3,2,1,0:T(8,128)(2,1)} %get-tuple-element.9), channel_id=1, source_target_pairs={{0,32},{32,64},{64,96},{96,128},{128,160},{160,192},{192,224},{224... | collective-permute-start | bytes 6291464 | tf_op jit(solution)/shard_map/ppermute | solution.py:17
  132.0 1.3 collective-permute-start.3
  133.3 0.6 fusion.7.sel_ref
  133.9 0.6 compare_select_fusion.8
  134.5 0.6 and_convert_fusion
  136.1 1.3 collective-permute-start.1
  137.4 4.6 %collective-permute-start = (s32[32,2]{1,0:T(8,128)S(1)}, s32[32,2]{1,0:T(8,128)S(1)}, u32[]{:S(2)}, u32[]{:S(2)}) collective-permute-start(s32[32,2]{1,0:T(8,128)S(1)} %gather_fusion), channel_id=1, source_target_pairs={{0,32},{32,64},{64,96},{96,128},{128,160},{160,192},{192,224},{224... | collective-permute-start | bytes 776 | tf_op jit(solution)/shard_map/ppermute | solution.py:17
  142.0 18.1 %shard_map.56.prior_ref = f32[4,128,1536]{2,1,0:T(8,128)} custom-call(s32[128]{0:T(128)} %get-tuple-element.23.src_ref, s32[128]{0:T(128)} %get-tuple-element.21.live_ref, s32[256]{0:T(256)} %reshape.145.lcol_ref, s32[16]{0:T(128)} %reshape.144.pcol_ref, s32[32]{0:T(128)} %fusion.7.sel_ref, bf16[8,16,128,128]{3,2,1,0:T(8,128)(2,1)} %a_ref.3, ...), custom_call_target="tpu_custom_call" | custom-call | flops 1879048192 | bytes 9961472 | tf_op jit(solution)/shard_map/pallas_call | solution.py:116
  160.1 18.4 %collective-permute-done.1 = s32[32,2]{1,0:T(8,128)S(1)} collective-permute-done((s32[32,2]{1,0:T(8,128)S(1)}, s32[32,2]{1,0:T(8,128)S(1)}, u32[]{:S(2)}, u32[]{:S(2)}) %collective-permute-start.1) | collective-permute-done | bytes 288 | tf_op jit(solution)/shard_map/ppermute | solution.py:17
  178.6 0.6 gather_fusion.2
  179.2 0.7 reshape.143.lcol_ref
  179.9 1.3 copy-done
  181.3 15.1 %shard_map.57 = f32[4,128,1536]{2,1,0:T(8,128)} custom-call(s32[128]{0:T(128)} %compare_select_fusion.7.src_ref, s32[128]{0:T(128)} %and_convert_fusion.1.live_ref, s32[256]{0:T(256)} %reshape.143.lcol_ref, s32[16]{0:T(128)} %reshape.144.pcol_ref, bf16[8,16,128,128]{3,2,1,0:T(8,128)(2,1)} %a_ref.3, ...), custom_call_target="tpu_custom_call", output_to_operand_aliasing={{}: (8, {})} | custom-call | flops 1879048192 | bytes 11534336 | tf_op jit(solution)/shard_map/pallas_call | solution.py:135
  196.4 72.8 %reduce-scatter.2.cloned.1.call-done = f32[32,1536]{1,0:T(8,128)} async-done(((f32[512,1536]{1,0:T(8,128)}), f32[32,1536]{1,0:T(8,128)}) %reduce-scatter.2.cloned.1.call-update) | async-done | bytes 196624 | tf_op jit(solution)/shard_map/reduce_scatter | solution.py:233
  269.2 0.9 constant_dynamic-slice_fusion
  270.1 12.4 %collective-permute-start.4 = (f32[16,1536]{1,0:T(8,128)S(1)}, f32[16,1536]{1,0:T(8,128)S(1)}, u32[]{:S(2)}, u32[]{:S(2)}) collective-permute-start(f32[16,1536]{1,0:T(8,128)S(1)} %constant_dynamic-slice_fusion), channel_id=1, source_target_pairs={{0,1},{1,0},{2,3},{3,2},{4,5},{5,4},{6,7},{7,6},{8,9},{9,8},{10,11... | collective-permute-start | bytes 294920 | tf_op jit(solution)/shard_map/ppermute | solution.py:238
  282.5 0.9 collective-permute-done.4
  283.4 1.6 dynamic-slice_add_fusion
  (33 shorter events, 3.7 us)
Async XLA Ops:
  6.5 116.8 %all-gather.3.cloned.1.call-start = ((), (), s32[]{:S(2)}) async-start(), calls=%async_computation.1 | async-start | bytes 17301504 | tf_op jit(solution)/shard_map/all_gather | solution.py:182
  7.3 262.0 %reduce-scatter.2.cloned.1.call-start = ((), (), s32[]{:S(2)}) async-start(), calls=%async_computation.2 | async-start | bytes 3342336 | tf_op jit(solution)/shard_map/reduce_scatter | solution.py:233
  128.7 51.2 %collective-permute-start.2 = (bf16[32,2,128,128]{3,2,1,0:T(8,128)(2,1)}, bf16[32,2,128,128]{3,2,1,0:T(8,128)(2,1)S(1)}, u32[]{:S(2)}, u32[]{:S(2)}) collective-permute-start(bf16[32,2,128,128]{3,2,1,0:T(8,128)(2,1)} %get-tuple-element.9), channel_id=1, source_target_pairs={{0,32},{32,64},{64,96},{96,128},{128,160},{160,192},{192,224},{224... | collective-permute-start | bytes 6291464 | tf_op jit(solution)/shard_map/ppermute | solution.py:17
  132.0 47.9 %collective-permute-start.3 = (bf16[32,2,128,128]{3,2,1,0:T(8,128)(2,1)}, bf16[32,2,128,128]{3,2,1,0:T(8,128)(2,1)}, u32[]{:S(2)}, u32[]{:S(2)}) collective-permute-start(bf16[32,2,128,128]{3,2,1,0:T(8,128)(2,1)} %get-tuple-element.12), channel_id=1, source_target_pairs={{32,0},{64,32},{96,64},{128,96},{160,128},{192,160},{224,192},{256... | collective-permute-start | bytes 6291464 | tf_op jit(solution)/shard_map/ppermute | solution.py:17
  136.1 42.4 %collective-permute-start.1 = (s32[32,2]{1,0:T(8,128)S(1)}, s32[32,2]{1,0:T(8,128)S(1)}, u32[]{:S(2)}, u32[]{:S(2)}) collective-permute-start(s32[32,2]{1,0:T(8,128)S(1)} %gather_fusion.1), channel_id=1, source_target_pairs={{32,0},{64,32},{96,64},{128,96},{160,128},{192,160},{224,192},{256... | collective-permute-start | bytes 776 | tf_op jit(solution)/shard_map/ppermute | solution.py:17
  137.4 41.1 %collective-permute-start = (s32[32,2]{1,0:T(8,128)S(1)}, s32[32,2]{1,0:T(8,128)S(1)}, u32[]{:S(2)}, u32[]{:S(2)}) collective-permute-start(s32[32,2]{1,0:T(8,128)S(1)} %gather_fusion), channel_id=1, source_target_pairs={{0,32},{32,64},{64,96},{96,128},{128,160},{160,192},{192,224},{224... | collective-permute-start | bytes 776 | tf_op jit(solution)/shard_map/ppermute | solution.py:17
  179.9 1.4 copy-start
  270.1 13.3 %collective-permute-start.4 = (f32[16,1536]{1,0:T(8,128)S(1)}, f32[16,1536]{1,0:T(8,128)S(1)}, u32[]{:S(2)}, u32[]{:S(2)}) collective-permute-start(f32[16,1536]{1,0:T(8,128)S(1)} %constant_dynamic-slice_fusion), channel_id=1, source_target_pairs={{0,1},{1,0},{2,3},{3,2},{4,5},{5,4},{6,7},{7,6},{8,9},{9,8},{10,11... | collective-permute-start | bytes 294920 | tf_op jit(solution)/shard_map/ppermute | solution.py:238
Sparse Core Ops, SparseCore 0:
  9.5 113.7 all-gather.2
  196.6 72.6 reduce-scatter.1

commit v8 on v7

--- a/solution.py
+++ b/solution.py
@@ -68,12 +68,12 @@
 def side_kernel(rows, slots, src_ref, live_ref, lcol_ref, pcol_ref, a_ref, lower_ref, upper_ref, pt_ref, prior_ref, out_ref, buf_ref, acc_ref, sems):
     half = lower_ref.shape[0]
     copies = [
+        pltpu.make_async_copy(prior_ref, out_ref, sems.at[2]),
         pltpu.make_async_copy(lower_ref, buf_ref.at[pl.ds(0, half)], sems.at[0]),
         pltpu.make_async_copy(upper_ref, buf_ref.at[pl.ds(half, half)], sems.at[1]),
     ]
     for cp in copies:
         cp.start()
-    out_ref[...] = prior_ref[...]
     for cp in copies:
         cp.wait()
     spans = ((0, CG), (2 * CG, 3 * CG))
@@ -135,13 +135,13 @@
     return pl.pallas_call(
         functools.partial(side_kernel, rows, slots),
         out_shape=jax.ShapeDtypeStruct((CG, bs, width * bs), jnp.float32),
-        in_specs=[SMEM, SMEM, SMEM, SMEM, VMEM, ANY, ANY, VMEM, VMEM],
+        in_specs=[SMEM, SMEM, SMEM, SMEM, VMEM, ANY, ANY, VMEM, ANY],
         input_output_aliases={8: 0},
         out_specs=VMEM,
         scratch_shapes=[
             pltpu.VMEM((2 * count, 2, bs, bs), jnp.bfloat16),
             pltpu.VMEM((bs, width * bs), jnp.float32),
-            pltpu.SemaphoreType.DMA((2,)),
+            pltpu.SemaphoreType.DMA((3,)),
         ],
         compiler_params=pltpu.CompilerParams(vmem_limit_bytes=VMEM_LIMIT),
         cost_estimate=cost(a_tiles, width, 2 * count * 2 * bs * bs * 2),
@@ -157,7 +157,7 @@
         pick_kernel,
         out_shape=(out, out),
         in_specs=[SMEM, SMEM, ANY],
-        out_specs=(VMEM, VMEM),
+        out_specs=(ANY, ANY),
         scratch_shapes=[pltpu.SemaphoreType.DMA((2 * count,))],
         compiler_params=pltpu.CompilerParams(vmem_limit_bytes=VMEM_LIMIT),
         cost_estimate=pl.CostEstimate(flops=0, bytes_accessed=nbytes, transcendentals=0),

time: 292 us -> 416 us (1.42)
  Pallas kernels: 38.7 us -> 160 us
    pallas_call x1, Pallas kernels: 5.45 us -> 129 us  [pick_rows(): pl.pallas_call(pick_kernel, out_shape=(out, out), in_specs=[SMEM, SMEM, A...]
  transfers between devices with their start and end apart: 7 -> 7, of which waited for: 4 -> 4; matrix products, arithmetic and copies ran while one was open for 5% -> 4% of each run, Pallas kernels for 6% -> 4%
where the time goes in v8:
time: 416 us; the launch traced here: 415 us
  Pallas kernels  160 us (38%)
  blocking collectives  102 us (25%)
  waiting for transfers between devices  97 us (23%)
  starting transfers between devices  22.4 us (5%)
  between operations  14.2 us (3%)
  local copies, waits for them, and re-layouts  11.9 us (3%)
  other arithmetic  7.51 us (2%)
    pallas_call x1, Pallas kernels, pick_rows(): pl.pallas_call(pick_kernel, out_shape=(out, out), in_specs=[SMEM, SMEM, A...  129 us
    unnamed x1, blocking collectives  102 us
    reduce_scatter x1, waiting for transfers between devices, body(): partial = lax.psum_scatter(partial, 'z', scatter_dimension=0, tiled=True)  74.1 us
    ppermute x4, waiting for transfers between devices, from_behind(): lax.ppermute(value, axis, [(source, source + steps) for source in range(l...  19.9 us
    pallas_call x1, Pallas kernels, middle_product(): pl.pallas_call(functools.partial(middle_kernel, rows, slots), out_shape=j...  16.7 us
    pallas_call x1, Pallas kernels, side_product(): pl.pallas_call(functools.partial(side_kernel, rows, slots), out_shape=jax...  13.9 us
    ppermute x1, starting transfers between devices, body(): return mine + lax.ppermute(other, 'core', [(0, 1), (1, 0)])  11.9 us
    ppermute x4, starting transfers between devices, from_behind(): lax.ppermute(value, axis, [(source, source + steps) for source in range(l...  10.4 us
  transfers between devices with their start and end apart: 7, of which 4 were waited for; matrix products, arithmetic and copies ran while one was open for 4% of the time, Pallas kernels for 4%

profile of v8, /device:TPU:1, one launch (start us, length us, event | category | flops | bytes accessed | tf_op | source)
XLA Modules:
  0.0 415.5 jit_solution(9871057766102697564)
XLA Ops:
  6.5 0.7 all-gather.3.cloned.1.call-update
  7.3 0.7 broadcast_clamp_fusion.3
  8.2 2.0 copy.27
  10.2 0.7 broadcast_compare_fusion
  11.0 0.8 copy.25
  11.8 1.3 dynamic-slice
  13.8 0.8 add_dynamic-update-slice_fusion
  14.6 102.4 %all-reduce = s32[3584]{0:T(1024)S(1)} all-reduce(s32[3584]{0:T(1024)S(1)} %add_dynamic-update-slice_fusion), channel_id=2, replica_groups=mesh['row'=16,'z'=16,'core'=2] {'z','core'}, use_global_device_ids=true, to_apply=%add | all-reduce | flops 3584 | bytes 28672
  118.7 0.6 reshape.144.pcol_ref
  119.9 0.6 gather_fusion.4
  120.6 0.7 reshape.145.lcol_ref
  121.3 0.6 fusion.8
  121.9 1.4 all-gather.3.cloned.1.call-done.group_ref
  123.3 129.4 %shard_map.55 = (bf16[32,2,128,128]{3,2,1,0:T(8,128)(2,1)}, bf16[32,2,128,128]{3,2,1,0:T(8,128)(2,1)}) custom-call(s32[32]{0:T(128)} %get-tuple-element.28.up_sel, s32[32]{0:T(128)} %get-tuple-element.27.down_sel, bf16[256,2,128,128]{3,2,1,0:T(8,128)(2,1)} %all-gather.3.cloned.1.call-done.group_ref), custom_call_target="tpu_custom_call" | custom-call | bytes 8388608 | tf_op jit(solution)/shard_map/pallas_call | solution.py:156
  252.7 3.2 collective-permute-start.2
  256.0 1.3 collective-permute-start.3
  257.3 0.6 fusion.7.sel_ref
  257.9 0.6 compare_select_fusion.8
  258.5 0.6 and_convert_fusion
  260.1 1.3 collective-permute-start.1
  261.4 4.6 %collective-permute-start = (s32[32,2]{1,0:T(8,128)S(1)}, s32[32,2]{1,0:T(8,128)S(1)}, u32[]{:S(2)}, u32[]{:S(2)}) collective-permute-start(s32[32,2]{1,0:T(8,128)S(1)} %gather_fusion), channel_id=1, source_target_pairs={{0,32},{32,64},{64,96},{96,128},{128,160},{160,192},{192,224},{224... | collective-permute-start | bytes 776 | tf_op jit(solution)/shard_map/ppermute | solution.py:17
  266.0 16.7 %shard_map.56.prior_ref = f32[4,128,1536]{2,1,0:T(8,128)} custom-call(s32[128]{0:T(128)} %get-tuple-element.23.src_ref, s32[128]{0:T(128)} %get-tuple-element.21.live_ref, s32[256]{0:T(256)} %reshape.145.lcol_ref, s32[16]{0:T(128)} %reshape.144.pcol_ref, s32[32]{0:T(128)} %fusion.7.sel_ref, bf16[8,16,128,128]{3,2,1,0:T(8,128)(2,1)} %a_ref.3, ...), custom_call_target="tpu_custom_call" | custom-call | flops 1879048192 | bytes 9961472 | tf_op jit(solution)/shard_map/pallas_call | solution.py:116
  282.7 19.9 %collective-permute-done.1 = s32[32,2]{1,0:T(8,128)S(1)} collective-permute-done((s32[32,2]{1,0:T(8,128)S(1)}, s32[32,2]{1,0:T(8,128)S(1)}, u32[]{:S(2)}, u32[]{:S(2)}) %collective-permute-start.1) | collective-permute-done | bytes 288 | tf_op jit(solution)/shard_map/ppermute | solution.py:17
  302.6 0.6 gather_fusion.2
  303.2 0.7 reshape.143.lcol_ref
  303.9 1.3 copy-done
  305.3 13.9 %shard_map.57 = f32[4,128,1536]{2,1,0:T(8,128)} custom-call(s32[128]{0:T(128)} %compare_select_fusion.7.src_ref, s32[128]{0:T(128)} %and_convert_fusion.1.live_ref, s32[256]{0:T(256)} %reshape.143.lcol_ref, s32[16]{0:T(128)} %reshape.144.pcol_ref, bf16[8,16,128,128]{3,2,1,0:T(8,128)(2,1)} %a_ref.3, ...), custom_call_target="tpu_custom_call", output_to_operand_aliasing={{}: (8, {})} | custom-call | flops 1879048192 | bytes 11534336 | tf_op jit(solution)/shard_map/pallas_call | solution.py:135
  319.2 74.1 %reduce-scatter.2.cloned.1.call-done = f32[32,1536]{1,0:T(8,128)} async-done(((f32[512,1536]{1,0:T(8,128)}), f32[32,1536]{1,0:T(8,128)}) %reduce-scatter.2.cloned.1.call-update) | async-done | bytes 196624 | tf_op jit(solution)/shard_map/reduce_scatter | solution.py:233
  393.3 0.9 constant_dynamic-slice_fusion
  394.2 11.9 %collective-permute-start.4 = (f32[16,1536]{1,0:T(8,128)S(1)}, f32[16,1536]{1,0:T(8,128)S(1)}, u32[]{:S(2)}, u32[]{:S(2)}) collective-permute-start(f32[16,1536]{1,0:T(8,128)S(1)} %constant_dynamic-slice_fusion), channel_id=1, source_target_pairs={{0,1},{1,0},{2,3},{3,2},{4,5},{5,4},{6,7},{7,6},{8,9},{9,8},{10,11... | collective-permute-start | bytes 294920 | tf_op jit(solution)/shard_map/ppermute | solution.py:238
  406.2 0.9 collective-permute-done.4
  407.1 1.6 dynamic-slice_add_fusion
  (33 shorter events, 3.7 us)
Async XLA Ops:
  6.5 116.8 %all-gather.3.cloned.1.call-start = ((), (), s32[]{:S(2)}) async-start(), calls=%async_computation.1 | async-start | bytes 17301504 | tf_op jit(solution)/shard_map/all_gather | solution.py:182
  7.3 386.1 %reduce-scatter.2.cloned.1.call-start = ((), (), s32[]{:S(2)}) async-start(), calls=%async_computation.2 | async-start | bytes 3342336 | tf_op jit(solution)/shard_map/reduce_scatter | solution.py:233
  252.7 51.2 %collective-permute-start.2 = (bf16[32,2,128,128]{3,2,1,0:T(8,128)(2,1)}, bf16[32,2,128,128]{3,2,1,0:T(8,128)(2,1)S(1)}, u32[]{:S(2)}, u32[]{:S(2)}) collective-permute-start(bf16[32,2,128,128]{3,2,1,0:T(8,128)(2,1)} %get-tuple-element.9), channel_id=1, source_target_pairs={{0,32},{32,64},{64,96},{96,128},{128,160},{160,192},{192,224},{224... | collective-permute-start | bytes 6291464 | tf_op jit(solution)/shard_map/ppermute | solution.py:17
  256.0 47.9 %collective-permute-start.3 = (bf16[32,2,128,128]{3,2,1,0:T(8,128)(2,1)}, bf16[32,2,128,128]{3,2,1,0:T(8,128)(2,1)}, u32[]{:S(2)}, u32[]{:S(2)}) collective-permute-start(bf16[32,2,128,128]{3,2,1,0:T(8,128)(2,1)} %get-tuple-element.12), channel_id=1, source_target_pairs={{32,0},{64,32},{96,64},{128,96},{160,128},{192,160},{224,192},{256... | collective-permute-start | bytes 6291464 | tf_op jit(solution)/shard_map/ppermute | solution.py:17
  260.1 42.4 %collective-permute-start.1 = (s32[32,2]{1,0:T(8,128)S(1)}, s32[32,2]{1,0:T(8,128)S(1)}, u32[]{:S(2)}, u32[]{:S(2)}) collective-permute-start(s32[32,2]{1,0:T(8,128)S(1)} %gather_fusion.1), channel_id=1, source_target_pairs={{32,0},{64,32},{96,64},{128,96},{160,128},{192,160},{224,192},{256... | collective-permute-start | bytes 776 | tf_op jit(solution)/shard_map/ppermute | solution.py:17
  261.4 41.1 %collective-permute-start = (s32[32,2]{1,0:T(8,128)S(1)}, s32[32,2]{1,0:T(8,128)S(1)}, u32[]{:S(2)}, u32[]{:S(2)}) collective-permute-start(s32[32,2]{1,0:T(8,128)S(1)} %gather_fusion), channel_id=1, source_target_pairs={{0,32},{32,64},{64,96},{96,128},{128,160},{160,192},{192,224},{224... | collective-permute-start | bytes 776 | tf_op jit(solution)/shard_map/ppermute | solution.py:17
  303.9 1.4 copy-start
  394.2 12.8 %collective-permute-start.4 = (f32[16,1536]{1,0:T(8,128)S(1)}, f32[16,1536]{1,0:T(8,128)S(1)}, u32[]{:S(2)}, u32[]{:S(2)}) collective-permute-start(f32[16,1536]{1,0:T(8,128)S(1)} %constant_dynamic-slice_fusion), channel_id=1, source_target_pairs={{0,1},{1,0},{2,3},{3,2},{4,5},{5,4},{6,7},{7,6},{8,9},{9,8},{10,11... | collective-permute-start | bytes 294920 | tf_op jit(solution)/shard_map/ppermute | solution.py:238
Sparse Core Ops, SparseCore 0:
  9.5 113.7 all-gather.2
  319.3 73.9 reduce-scatter.1

commit v9 on v5

--- a/solution.py
+++ b/solution.py
@@ -29,12 +29,10 @@
             @pl.when(live_ref[s] != 0)
             def _():
                 src = src_ref[s]
-                a = a_ref[i, k]
+                both = jnp.dot(a_ref[i, k], b_ref[src], preferred_element_type=jnp.float32)
                 for p in range(2):
                     col = pl.multiple_of(lcol_ref[2 * s + p] * bs, bs)
-                    acc_ref[:, pl.ds(col, bs)] += jnp.dot(
-                        a, b_ref[src, p], preferred_element_type=jnp.float32
-                    )
+                    acc_ref[:, pl.ds(col, bs)] += both[:, p * bs : (p + 1) * bs]
 
             return carry
 
@@ -49,13 +47,21 @@
 
 
 def middle_kernel(rows, slots, src_ref, live_ref, lcol_ref, pcol_ref, sel_ref, a_ref, group_ref, pt_ref, out_ref, buf_ref, acc_ref, sems):
-    own = buf_ref.shape[0] - sel_ref.shape[0]
+    count = sel_ref.shape[0]
+    own = buf_ref.shape[0] - count
+    bs = group_ref.shape[-1]
     me = lax.axis_index("z") * lax.axis_size("core") + lax.axis_index("core")
-    copies = [pltpu.make_async_copy(group_ref.at[pl.ds(me * own, own)], buf_ref.at[pl.ds(0, own)], sems.at[0])]
-    for q in range(sel_ref.shape[0]):
-        copies.append(
-            pltpu.make_async_copy(group_ref.at[sel_ref[q]], buf_ref.at[own + q], sems.at[q + 1])
-        )
+    copies = []
+    for p in range(2):
+        base = p * (count + 1)
+        lanes = pl.ds(p * bs, bs)
+        copies.append(
+            pltpu.make_async_copy(group_ref.at[pl.ds(me * own, own), p], buf_ref.at[pl.ds(0, own), :, lanes], sems.at[base])
+        )
+        for q in range(count):
+            copies.append(
+                pltpu.make_async_copy(group_ref.at[sel_ref[q], p], buf_ref.at[own + q, :, lanes], sems.at[base + q + 1])
+            )
     for cp in copies:
         cp.start()
     out_ref[...] = jnp.zeros_like(out_ref)
@@ -67,10 +73,16 @@
 
 def side_kernel(rows, slots, src_ref, live_ref, lcol_ref, pcol_ref, a_ref, lower_ref, upper_ref, pt_ref, prior_ref, out_ref, buf_ref, acc_ref, sems):
     half = lower_ref.shape[0]
-    copies = [
-        pltpu.make_async_copy(lower_ref, buf_ref.at[pl.ds(0, half)], sems.at[0]),
-        pltpu.make_async_copy(upper_ref, buf_ref.at[pl.ds(half, half)], sems.at[1]),
-    ]
+    bs = lower_ref.shape[-1]
+    copies = []
+    for p in range(2):
+        lanes = pl.ds(p * bs, bs)
+        copies.append(
+            pltpu.make_async_copy(lower_ref.at[:, p], buf_ref.at[pl.ds(0, half), :, lanes], sems.at[2 * p])
+        )
+        copies.append(
+            pltpu.make_async_copy(upper_ref.at[:, p], buf_ref.at[pl.ds(half, half), :, lanes], sems.at[2 * p + 1])
+        )
     for cp in copies:
         cp.start()
     out_ref[...] = prior_ref[...]
@@ -119,9 +131,9 @@
         in_specs=[SMEM, SMEM, SMEM, SMEM, SMEM, VMEM, ANY, VMEM],
         out_specs=VMEM,
         scratch_shapes=[
-            pltpu.VMEM((rows + count, 2, bs, bs), jnp.bfloat16),
+            pltpu.VMEM((rows + count, bs, 2 * bs), jnp.bfloat16),
             pltpu.VMEM((bs, width * bs), jnp.float32),
-            pltpu.SemaphoreType.DMA((count + 1,)),
+            pltpu.SemaphoreType.DMA((2 * (count + 1),)),
         ],
         compiler_params=pltpu.CompilerParams(vmem_limit_bytes=VMEM_LIMIT),
         cost_estimate=cost(a_tiles, width, (rows + count) * 2 * bs * bs * 2),
@@ -139,9 +151,9 @@
         input_output_aliases={8: 0},
         out_specs=VMEM,
         scratch_shapes=[
-            pltpu.VMEM((2 * count, 2, bs, bs), jnp.bfloat16),
+            pltpu.VMEM((2 * count, bs, 2 * bs), jnp.bfloat16),
             pltpu.VMEM((bs, width * bs), jnp.float32),
-            pltpu.SemaphoreType.DMA((2,)),
+            pltpu.SemaphoreType.DMA((4,)),
         ],
         compiler_params=pltpu.CompilerParams(vmem_limit_bytes=VMEM_LIMIT),
         cost_estimate=cost(a_tiles, width, 2 * count * 2 * bs * bs * 2),

time: 290 us -> 290 us (level)
  waiting for transfers between devices: 94.1 us -> 97.5 us
  Pallas kernels: 39.1 us -> 36.1 us
where the time goes in v9:
time: 290 us; the launch traced here: 289 us
  blocking collectives  103 us (36%)
  waiting for transfers between devices  97.5 us (34%)
  Pallas kernels  36.1 us (12%)
  starting transfers between devices  21.7 us (7%)
  between operations  14.2 us (5%)
  local copies, waits for them, and re-layouts  9.62 us (3%)
  other arithmetic  7.45 us (3%)
    unnamed x1, blocking collectives  103 us
    reduce_scatter x1, waiting for transfers between devices, body(): partial = lax.psum_scatter(partial, 'z', scatter_dimension=0, tiled=True)  75.6 us
    ppermute x4, waiting for transfers between devices, from_behind(): lax.ppermute(value, axis, [(source, source + steps) for source in range(l...  19.7 us
    pallas_call x1, Pallas kernels, middle_product(): pl.pallas_call(functools.partial(middle_kernel, rows, slots), out_shape=j...  16.1 us
    pallas_call x1, Pallas kernels, side_product(): pl.pallas_call(functools.partial(side_kernel, rows, slots), out_shape=jax...  14.3 us
    ppermute x1, starting transfers between devices, body(): return mine + lax.ppermute(other, 'core', [(0, 1), (1, 0)])  12.1 us
    ppermute x4, starting transfers between devices, from_behind(): lax.ppermute(value, axis, [(source, source + steps) for source in range(l...  9.64 us
  transfers between devices with their start and end apart: 7, of which 5 were waited for; matrix products, arithmetic and copies ran while one was open for 5% of the time, Pallas kernels for 8%

profile of v9, /device:TPU:1, one launch (start us, length us, event | category | flops | bytes accessed | tf_op | source)
XLA Modules:
  0.0 289.3 jit_solution(3762591118289059128)
XLA Ops:
  6.5 0.7 all-gather.3.cloned.1.call-update
  7.3 0.8 copy.25
  8.1 1.3 dynamic-slice
  10.1 0.8 add_dynamic-update-slice_fusion
  10.9 102.6 %all-reduce = s32[3584]{0:T(1024)S(1)} all-reduce(s32[3584]{0:T(1024)S(1)} %add_dynamic-update-slice_fusion), channel_id=2, replica_groups=mesh['row'=16,'z'=16,'core'=2] {'z','core'}, use_global_device_ids=true, to_apply=%add | all-reduce | flops 3584 | bytes 28672
  114.1 0.6 gather_fusion
  114.7 3.4 %collective-permute-start = (s32[32,2]{1,0:T(8,128)S(1)}, s32[32,2]{1,0:T(8,128)S(1)}, u32[]{:S(2)}, u32[]{:S(2)}) collective-permute-start(s32[32,2]{1,0:T(8,128)S(1)} %gather_fusion), channel_id=1, source_target_pairs={{0,32},{32,64},{64,96},{96,128},{128,160},{160,192},{192,224},{224... | collective-permute-start | bytes 776 | tf_op jit(solution)/shard_map/ppermute | solution.py:17
  118.7 1.3 collective-permute-start.1
  120.0 0.7 broadcast_clamp_fusion.3
  120.8 0.6 gather_fusion.3
  121.4 0.6 fusion.8
  122.0 0.7 broadcast_compare_fusion
  123.2 5.7 %shard_map.55 = (bf16[32,2,128,128]{3,2,1,0:T(8,128)(2,1)}, bf16[32,2,128,128]{3,2,1,0:T(8,128)(2,1)}) custom-call(s32[32]{0:T(128)} %get-tuple-element.22.up_sel, s32[32]{0:T(128)} %get-tuple-element.21.down_sel, bf16[256,2,128,128]{3,2,1,0:T(8,128)(2,1)} %all-gather.3.cloned.1.call-done.group_ref), custom_call_target="tpu_custom_call" | custom-call | bytes 8388608 | tf_op jit(solution)/shard_map/pallas_call | solution.py:168
  128.9 3.6 %collective-permute-start.2 = (bf16[32,2,128,128]{3,2,1,0:T(8,128)(2,1)}, bf16[32,2,128,128]{3,2,1,0:T(8,128)(2,1)S(1)}, u32[]{:S(2)}, u32[]{:S(2)}) collective-permute-start(bf16[32,2,128,128]{3,2,1,0:T(8,128)(2,1)} %get-tuple-element.7), channel_id=1, source_target_pairs={{0,32},{32,64},{64,96},{96,128},{128,160},{160,192},{192,224},{224... | collective-permute-start | bytes 6291464 | tf_op jit(solution)/shard_map/ppermute | solution.py:17
  132.6 1.3 collective-permute-start.3
  134.6 0.6 compare_select_fusion.8
  135.2 0.6 and_convert_fusion
  136.8 0.7 reshape.144.pcol_ref
  137.5 1.0 copy.27
  138.5 0.6 gather_fusion.4
  139.1 0.7 reshape.145.lcol_ref
  139.9 0.6 gather_fusion.2
  140.5 0.7 reshape.143.lcol_ref
  141.2 16.1 %shard_map.56.prior_ref = f32[4,128,1536]{2,1,0:T(8,128)} custom-call(s32[128]{0:T(128)} %get-tuple-element.19.src_ref, s32[128]{0:T(128)} %get-tuple-element.17.live_ref, s32[256]{0:T(256)} %reshape.145.lcol_ref, s32[16]{0:T(128)} %reshape.144.pcol_ref, s32[32]{0:T(128)} %fusion.7.sel_ref, bf16[8,16,128,128]{3,2,1,0:T(8,128)(2,1)} %a_ref.3, ...), custom_call_target="tpu_custom_call" | custom-call | flops 1879048192 | bytes 9961472 | tf_op jit(solution)/shard_map/pallas_call | solution.py:128
  157.3 15.7 %collective-permute-done.2.lower_ref = bf16[32,2,128,128]{3,2,1,0:T(8,128)(2,1)S(1)} collective-permute-done((bf16[32,2,128,128]{3,2,1,0:T(8,128)(2,1)}, bf16[32,2,128,128]{3,2,1,0:T(8,128)(2,1)S(1)}, u32[]{:S(2)}, u32[]{:S(2)}) %collective-permute-start.2) | collective-permute-done | bytes 2097184 | tf_op jit(solution)/shard_map/ppermute | solution.py:17
  173.1 4.0 %collective-permute-done.3.upper_ref = bf16[32,2,128,128]{3,2,1,0:T(8,128)(2,1)} collective-permute-done((bf16[32,2,128,128]{3,2,1,0:T(8,128)(2,1)}, bf16[32,2,128,128]{3,2,1,0:T(8,128)(2,1)}, u32[]{:S(2)}, u32[]{:S(2)}) %collective-permute-start.3) | collective-permute-done | bytes 2097184 | tf_op jit(solution)/shard_map/ppermute | solution.py:17
  177.1 14.3 %shard_map.57 = f32[4,128,1536]{2,1,0:T(8,128)} custom-call(s32[128]{0:T(128)} %compare_select_fusion.7.src_ref, s32[128]{0:T(128)} %and_convert_fusion.1.live_ref, s32[256]{0:T(256)} %reshape.143.lcol_ref, s32[16]{0:T(128)} %reshape.144.pcol_ref, bf16[8,16,128,128]{3,2,1,0:T(8,128)(2,1)} %a_ref.3, ...), custom_call_target="tpu_custom_call", output_to_operand_aliasing={{}: (8, {})} | custom-call | flops 1879048192 | bytes 11534336 | tf_op jit(solution)/shard_map/pallas_call | solution.py:147
  191.4 75.6 %reduce-scatter.2.cloned.1.call-done = f32[32,1536]{1,0:T(8,128)} async-done(((f32[512,1536]{1,0:T(8,128)}), f32[32,1536]{1,0:T(8,128)}) %reduce-scatter.2.cloned.1.call-update) | async-done | bytes 196624 | tf_op jit(solution)/shard_map/reduce_scatter | solution.py:242
  267.1 0.9 constant_dynamic-slice_fusion
  268.0 12.1 %collective-permute-start.4 = (f32[16,1536]{1,0:T(8,128)S(1)}, f32[16,1536]{1,0:T(8,128)S(1)}, u32[]{:S(2)}, u32[]{:S(2)}) collective-permute-start(f32[16,1536]{1,0:T(8,128)S(1)} %constant_dynamic-slice_fusion), channel_id=1, source_target_pairs={{0,1},{1,0},{2,3},{3,2},{4,5},{5,4},{6,7},{7,6},{8,9},{9,8},{10,11... | collective-permute-start | bytes 294920 | tf_op jit(solution)/shard_map/ppermute | solution.py:247
  280.0 0.9 collective-permute-done.4
  280.9 1.5 dynamic-slice_add_fusion
  (36 shorter events, 3.7 us)
Async XLA Ops:
  6.5 116.7 %all-gather.3.cloned.1.call-start = ((), (), s32[]{:S(2)}) async-start(), calls=%async_computation.1 | async-start | bytes 17301504 | tf_op jit(solution)/shard_map/all_gather | solution.py:194
  7.3 259.8 %reduce-scatter.2.cloned.1.call-start = ((), (), s32[]{:S(2)}) async-start(), calls=%async_computation.2 | async-start | bytes 3342336 | tf_op jit(solution)/shard_map/reduce_scatter | solution.py:242
  114.7 25.2 %collective-permute-start = (s32[32,2]{1,0:T(8,128)S(1)}, s32[32,2]{1,0:T(8,128)S(1)}, u32[]{:S(2)}, u32[]{:S(2)}) collective-permute-start(s32[32,2]{1,0:T(8,128)S(1)} %gather_fusion), channel_id=1, source_target_pairs={{0,32},{32,64},{64,96},{96,128},{128,160},{160,192},{192,224},{224... | collective-permute-start | bytes 776 | tf_op jit(solution)/shard_map/ppermute | solution.py:17
  118.7 21.2 %collective-permute-start.1 = (s32[32,2]{1,0:T(8,128)S(1)}, s32[32,2]{1,0:T(8,128)S(1)}, u32[]{:S(2)}, u32[]{:S(2)}) collective-permute-start(s32[32,2]{1,0:T(8,128)S(1)} %gather_fusion.1), channel_id=1, source_target_pairs={{32,0},{64,32},{96,64},{128,96},{160,128},{192,160},{224,192},{256... | collective-permute-start | bytes 776 | tf_op jit(solution)/shard_map/ppermute | solution.py:17
  123.2 14.3 %copy-start.1 = (bf16[8,2,128,128]{3,2,1,0:T(8,128)(2,1)S(1)}, bf16[8,2,128,128]{3,2,1,0:T(8,128)(2,1)}, u32[]{:S(2)}) copy-start(bf16[8,2,128,128]{3,2,1,0:T(8,128)(2,1)} %param.7) | copy-start | bytes 1572868
  128.9 44.2 %collective-permute-start.2 = (bf16[32,2,128,128]{3,2,1,0:T(8,128)(2,1)}, bf16[32,2,128,128]{3,2,1,0:T(8,128)(2,1)S(1)}, u32[]{:S(2)}, u32[]{:S(2)}) collective-permute-start(bf16[32,2,128,128]{3,2,1,0:T(8,128)(2,1)} %get-tuple-element.7), channel_id=1, source_target_pairs={{0,32},{32,64},{64,96},{96,128},{128,160},{160,192},{192,224},{224... | collective-permute-start | bytes 6291464 | tf_op jit(solution)/shard_map/ppermute | solution.py:17
  132.6 44.5 %collective-permute-start.3 = (bf16[32,2,128,128]{3,2,1,0:T(8,128)(2,1)}, bf16[32,2,128,128]{3,2,1,0:T(8,128)(2,1)}, u32[]{:S(2)}, u32[]{:S(2)}) collective-permute-start(bf16[32,2,128,128]{3,2,1,0:T(8,128)(2,1)} %get-tuple-element.8), channel_id=1, source_target_pairs={{32,0},{64,32},{96,64},{128,96},{160,128},{192,160},{224,192},{256... | collective-permute-start | bytes 6291464 | tf_op jit(solution)/shard_map/ppermute | solution.py:17
  173.1 4.0 %copy-start = (bf16[32,2,128,128]{3,2,1,0:T(8,128)(2,1)}, bf16[32,2,128,128]{3,2,1,0:T(8,128)(2,1)S(1)}, u32[]{:S(2)}) copy-start(bf16[32,2,128,128]{3,2,1,0:T(8,128)(2,1)S(1)} %collective-permute-done.2.lower_ref) | copy-start | bytes 6291460
  268.0 13.0 %collective-permute-start.4 = (f32[16,1536]{1,0:T(8,128)S(1)}, f32[16,1536]{1,0:T(8,128)S(1)}, u32[]{:S(2)}, u32[]{:S(2)}) collective-permute-start(f32[16,1536]{1,0:T(8,128)S(1)} %constant_dynamic-slice_fusion), channel_id=1, source_target_pairs={{0,1},{1,0},{2,3},{3,2},{4,5},{5,4},{6,7},{7,6},{8,9},{9,8},{10,11... | collective-permute-start | bytes 294920 | tf_op jit(solution)/shard_map/ppermute | solution.py:247
Sparse Core Ops, SparseCore 0:
  9.5 113.6 all-gather.2
  191.5 75.4 reduce-scatter.1

commit v10 on v9

--- a/solution.py
+++ b/solution.py
@@ -71,18 +71,16 @@
     accumulate_rows(rows, slots, spans, src_ref, live_ref, lcol_ref, pcol_ref, a_ref, buf_ref, pt_ref, out_ref, acc_ref)
 
 
-def side_kernel(rows, slots, src_ref, live_ref, lcol_ref, pcol_ref, a_ref, lower_ref, upper_ref, pt_ref, prior_ref, out_ref, buf_ref, acc_ref, sems):
-    half = lower_ref.shape[0]
-    bs = lower_ref.shape[-1]
+def side_kernel(rows, slots, src_ref, live_ref, lcol_ref, pcol_ref, a_ref, lower_a, lower_b, upper_a, upper_b, pt_ref, prior_ref, out_ref, buf_ref, acc_ref, sems):
+    part = lower_a.shape[0]
+    bs = lower_a.shape[-1]
     copies = []
-    for p in range(2):
-        lanes = pl.ds(p * bs, bs)
-        copies.append(
-            pltpu.make_async_copy(lower_ref.at[:, p], buf_ref.at[pl.ds(0, half), :, lanes], sems.at[2 * p])
-        )
-        copies.append(
-            pltpu.make_async_copy(upper_ref.at[:, p], buf_ref.at[pl.ds(half, half), :, lanes], sems.at[2 * p + 1])
-        )
+    for n, piece in enumerate((lower_a, lower_b, upper_a, upper_b)):
+        for p in range(2):
+            lanes = pl.ds(p * bs, bs)
+            copies.append(
+                pltpu.make_async_copy(piece.at[:, p], buf_ref.at[pl.ds(n * part, part), :, lanes], sems.at[2 * n + p])
+            )
     for cp in copies:
         cp.start()
     out_ref[...] = prior_ref[...]
@@ -142,22 +140,22 @@
 
 def side_product(a_tiles, lower, upper, p_t, src, live, lcol, pcol, prior):
     rows, slots, bs, _ = a_tiles.shape
-    count = lower.shape[0]
+    count = 2 * lower[0].shape[0]
     width = 3 * CG
     return pl.pallas_call(
         functools.partial(side_kernel, rows, slots),
         out_shape=jax.ShapeDtypeStruct((CG, bs, width * bs), jnp.float32),
-        in_specs=[SMEM, SMEM, SMEM, SMEM, VMEM, ANY, ANY, VMEM, VMEM],
-        input_output_aliases={8: 0},
+        in_specs=[SMEM, SMEM, SMEM, SMEM, VMEM, ANY, ANY, ANY, ANY, VMEM, VMEM],
+        input_output_aliases={10: 0},
         out_specs=VMEM,
         scratch_shapes=[
             pltpu.VMEM((2 * count, bs, 2 * bs), jnp.bfloat16),
             pltpu.VMEM((bs, width * bs), jnp.float32),
-            pltpu.SemaphoreType.DMA((4,)),
+            pltpu.SemaphoreType.DMA((8,)),
         ],
         compiler_params=pltpu.CompilerParams(vmem_limit_bytes=VMEM_LIMIT),
         cost_estimate=cost(a_tiles, width, 2 * count * 2 * bs * bs * 2),
-    )(src, live, lcol, pcol, a_tiles, lower, upper, p_t, prior)
+    )(src, live, lcol, pcol, a_tiles, *lower, *upper, p_t, prior)
 
 
 def pick_rows(group_tiles, up_sel, down_sel):
@@ -200,13 +198,18 @@
         return base + jnp.clip(group_send[:, 3 * c + t], 0, own_rows - 1)
 
     up_sel, mid_sel, down_sel = selection(0), selection(1), selection(2)
-    up_tiles, down_tiles = pick_rows(group_tiles, up_sel, down_sel)
+    half = col_count // 2
+    up_a, down_a = pick_rows(group_tiles, up_sel[:half], down_sel[:half])
+    lower_a, upper_a = from_behind(up_a, "row", 1), from_behind(down_a, "row", -1)
+    later_up, later_down, up_a = lax.optimization_barrier((up_sel[half:], down_sel[half:], up_a))
+    up_b, down_b = pick_rows(group_tiles, later_up, later_down)
+    lower_b, upper_b = from_behind(up_b, "row", 1), from_behind(down_b, "row", -1)
 
     def cols_of(t):
         return group_pcols[q * own_rows + jnp.clip(group_send[:, 3 * c + t], 0, own_rows - 1)]
 
-    lower_tiles, lower_cols = from_behind((up_tiles, cols_of(0)), "row", 1)
-    upper_tiles, upper_cols = from_behind((down_tiles, cols_of(2)), "row", -1)
+    lower_cols = from_behind(cols_of(0), "row", 1)
+    upper_cols = from_behind(cols_of(2), "row", -1)
     mid_cols = cols_of(1)
 
     b = a_cols.reshape(-1)
@@ -236,7 +239,7 @@
     pcol = pcol.reshape(-1)
     mid = middle_product(a_tiles, group_tiles, p_t, mid_sel, mid_src, mid_live, mid_lcol, pcol)
     partial = side_product(
-        a_tiles, lower_tiles, upper_tiles, p_t, side_src, side_live, side_lcol, pcol, mid
+        a_tiles, (lower_a, lower_b), (upper_a, upper_b), p_t, side_src, side_live, side_lcol, pcol, mid
     )
     partial = partial.reshape(CG * block_size, 3 * CG * block_size)
     partial = lax.psum_scatter(partial, "z", scatter_dimension=0, tiled=True)

time: 290 us -> 302 us (1.041)
  starting transfers between devices: 21.7 us -> 27.5 us
  Pallas kernels: 36.1 us -> 39.7 us
    ppermute x4 -> x6, starting transfers between devices: 9.64 us -> 14.8 us  [from_behind(): lax.ppermute(value, axis, [(source, source + steps) for source in range(l...]
    reduce_scatter x1, waiting for transfers between devices: 75.6 us -> 71.6 us  [body(): partial = lax.psum_scatter(partial, 'z', scatter_dimension=0, tiled=True)]
    ppermute x4 -> x6, waiting for transfers between devices: 19.7 us -> 23.2 us  [from_behind(): lax.ppermute(value, axis, [(source, source + steps) for source in range(l...]
    pallas_call x1 -> x2, Pallas kernels: 5.72 us -> 7.83 us  [pick_rows(): pl.pallas_call(pick_kernel, out_shape=(out, out), in_specs=[SMEM, SMEM, A...]
  transfers between devices with their start and end apart: 7 -> 9, of which waited for: 5 -> 4; matrix products, arithmetic and copies ran while one was open for 5% -> 5% of each run, Pallas kernels for 8% -> 8%
where the time goes in v10:
time: 302 us; the launch traced here: 301 us
  blocking collectives  103 us (34%)
  waiting for transfers between devices  97.9 us (32%)
  Pallas kernels  39.7 us (13%)
  starting transfers between devices  27.5 us (9%)
  between operations  14.3 us (5%)
  local copies, waits for them, and re-layouts  12 us (4%)
  other arithmetic  7 us (2%)
    unnamed x1, blocking collectives  103 us
    reduce_scatter x1, waiting for transfers between devices, body(): partial = lax.psum_scatter(partial, 'z', scatter_dimension=0, tiled=True)  71.6 us
    ppermute x6, waiting for transfers between devices, from_behind(): lax.ppermute(value, axis, [(source, source + steps) for source in range(l...  23.2 us
    pallas_call x1, Pallas kernels, middle_product(): pl.pallas_call(functools.partial(middle_kernel, rows, slots), out_shape=j...  17.7 us
    ppermute x6, starting transfers between devices, from_behind(): lax.ppermute(value, axis, [(source, source + steps) for source in range(l...  14.8 us
    pallas_call x1, Pallas kernels, side_product(): pl.pallas_call(functools.partial(side_kernel, rows, slots), out_shape=jax...  14.2 us
    ppermute x1, starting transfers between devices, body(): return mine + lax.ppermute(other, 'core', [(0, 1), (1, 0)])  12.7 us
    pallas_call x2, Pallas kernels, pick_rows(): pl.pallas_call(pick_kernel, out_shape=(out, out), in_specs=[SMEM, SMEM, A...  7.83 us
  transfers between devices with their start and end apart: 9, of which 4 were waited for; matrix products, arithmetic and copies ran while one was open for 5% of the time, Pallas kernels for 8%

profile of v10, /device:TPU:1, one launch (start us, length us, event | category | flops | bytes accessed | tf_op | source)
XLA Modules:
  0.0 301.0 jit_solution(12497532314033787654)
XLA Ops:
  6.5 0.7 all-gather.3.cloned.1.call-update
  7.3 0.8 copy.25
  8.1 1.3 dynamic-slice
  10.1 0.8 add_dynamic-update-slice_fusion
  10.9 102.6 %all-reduce = s32[3584]{0:T(1024)S(1)} all-reduce(s32[3584]{0:T(1024)S(1)} %add_dynamic-update-slice_fusion), channel_id=2, replica_groups=mesh['row'=16,'z'=16,'core'=2] {'z','core'}, use_global_device_ids=true, to_apply=%add | all-reduce | flops 3584 | bytes 28672
  114.7 1.3 collective-permute-start.1
  116.0 0.7 broadcast_clamp_fusion.3
  116.8 0.7 broadcast_compare_fusion
  120.0 0.6 fusion.11
  121.8 1.4 all-gather.3.cloned.1.call-done.group_ref
  123.2 3.9 %shard_map.55 = (bf16[16,2,128,128]{3,2,1,0:T(8,128)(2,1)}, bf16[16,2,128,128]{3,2,1,0:T(8,128)(2,1)}) custom-call(s32[16]{0:T(128)} %get-tuple-element.32.up_sel, s32[16]{0:T(128)} %get-tuple-element.30.down_sel, bf16[256,2,128,128]{3,2,1,0:T(8,128)(2,1)} %all-gather.3.cloned.1.call-done.group_ref), custom_call_target="tpu_custom_call" | custom-call | bytes 4194304 | tf_op jit(solution)/shard_map/pallas_call | solution.py:166
  127.1 3.2 %collective-permute-start.2 = (bf16[16,2,128,128]{3,2,1,0:T(8,128)(2,1)}, bf16[16,2,128,128]{3,2,1,0:T(8,128)(2,1)S(1)}, u32[]{:S(2)}, u32[]{:S(2)}) collective-permute-start(bf16[16,2,128,128]{3,2,1,0:T(8,128)(2,1)} %get-tuple-element.11), channel_id=1, source_target_pairs={{0,32},{32,64},{64,96},{96,128},{128,160},{160,192},{192,224},{224... | collective-permute-start | bytes 3145736 | tf_op jit(solution)/shard_map/ppermute | solution.py:17
  130.3 4.0 %shard_map.56 = (bf16[16,2,128,128]{3,2,1,0:T(8,128)(2,1)}, bf16[16,2,128,128]{3,2,1,0:T(8,128)(2,1)}) custom-call(s32[16]{0:T(128)} %get-tuple-element.12.up_sel, s32[16]{0:T(128)} %get-tuple-element.13.down_sel, bf16[256,2,128,128]{3,2,1,0:T(8,128)(2,1)} %all-gather.3.cloned.1.call-done.group_ref), custom_call_target="tpu_custom_call" | custom-call | bytes 4194304 | tf_op jit(solution)/shard_map/pallas_call | solution.py:166
  134.3 3.1 %collective-permute-start.3 = (bf16[16,2,128,128]{3,2,1,0:T(8,128)(2,1)}, bf16[16,2,128,128]{3,2,1,0:T(8,128)(2,1)S(1)}, u32[]{:S(2)}, u32[]{:S(2)}) collective-permute-start(bf16[16,2,128,128]{3,2,1,0:T(8,128)(2,1)} %get-tuple-element.14), channel_id=1, source_target_pairs={{0,32},{32,64},{64,96},{96,128},{128,160},{160,192},{192,224},{224... | collective-permute-start | bytes 3145736 | tf_op jit(solution)/shard_map/ppermute | solution.py:17
  137.4 1.3 collective-permute-start.4
  138.7 1.3 collective-permute-start.5
  140.5 0.6 reshape.144.pcol_ref
  141.1 1.0 copy.27
  142.7 0.6 gather_fusion.4
  143.4 0.7 reshape.145.lcol_ref
  144.1 4.6 %collective-permute-start = (s32[32,2]{1,0:T(8,128)S(1)}, s32[32,2]{1,0:T(8,128)S(1)}, u32[]{:S(2)}, u32[]{:S(2)}) collective-permute-start(s32[32,2]{1,0:T(8,128)S(1)} %gather_fusion), channel_id=1, source_target_pairs={{0,32},{32,64},{64,96},{96,128},{128,160},{160,192},{192,224},{224... | collective-permute-start | bytes 776 | tf_op jit(solution)/shard_map/ppermute | solution.py:17
  148.7 23.2 %collective-permute-done = s32[32,2]{1,0:T(8,128)S(1)} collective-permute-done((s32[32,2]{1,0:T(8,128)S(1)}, s32[32,2]{1,0:T(8,128)S(1)}, u32[]{:S(2)}, u32[]{:S(2)}) %collective-permute-start) | collective-permute-done | bytes 288 | tf_op jit(solution)/shard_map/ppermute | solution.py:17
  171.9 0.6 gather_fusion.2
  172.6 0.7 reshape.143.lcol_ref
  173.3 17.7 %shard_map.57.prior_ref = f32[4,128,1536]{2,1,0:T(8,128)} custom-call(s32[128]{0:T(128)} %get-tuple-element.27.src_ref, s32[128]{0:T(128)} %get-tuple-element.25.live_ref, s32[256]{0:T(256)} %reshape.145.lcol_ref, s32[16]{0:T(128)} %reshape.144.pcol_ref, s32[32]{0:T(128)} %fusion.7.sel_ref, bf16[8,16,128,128]{3,2,1,0:T(8,128)(2,1)} %a_ref.3, ...), custom_call_target="tpu_custom_call" | custom-call | flops 1879048192 | bytes 9961472 | tf_op jit(solution)/shard_map/pallas_call | solution.py:126
  191.0 0.9 copy-done.1
  192.3 14.2 %shard_map.58 = f32[4,128,1536]{2,1,0:T(8,128)} custom-call(s32[128]{0:T(128)} %compare_select_fusion.7.src_ref, s32[128]{0:T(128)} %and_convert_fusion.1.live_ref, s32[256]{0:T(256)} %reshape.143.lcol_ref, s32[16]{0:T(128)} %reshape.144.pcol_ref, bf16[8,16,128,128]{3,2,1,0:T(8,128)(2,1)} %a_ref.3, ...), custom_call_target="tpu_custom_call", output_to_operand_aliasing={{}: (10, {})} | custom-call | flops 1879048192 | bytes 11534336 | tf_op jit(solution)/shard_map/pallas_call | solution.py:145
  206.5 71.6 %reduce-scatter.2.cloned.1.call-done = f32[32,1536]{1,0:T(8,128)} async-done(((f32[512,1536]{1,0:T(8,128)}), f32[32,1536]{1,0:T(8,128)}) %reduce-scatter.2.cloned.1.call-update) | async-done | bytes 196624 | tf_op jit(solution)/shard_map/reduce_scatter | solution.py:245
  278.1 0.9 constant_dynamic-slice_fusion
  279.0 12.7 %collective-permute-start.6 = (f32[16,1536]{1,0:T(8,128)S(1)}, f32[16,1536]{1,0:T(8,128)S(1)}, u32[]{:S(2)}, u32[]{:S(2)}) collective-permute-start(f32[16,1536]{1,0:T(8,128)S(1)} %constant_dynamic-slice_fusion), channel_id=1, source_target_pairs={{0,1},{1,0},{2,3},{3,2},{4,5},{5,4},{6,7},{7,6},{8,9},{9,8},{10,11... | collective-permute-start | bytes 294920 | tf_op jit(solution)/shard_map/ppermute | solution.py:250
  291.7 0.9 collective-permute-done.6
  292.6 1.5 dynamic-slice_add_fusion
  (45 shorter events, 6.5 us)
Async XLA Ops:
  6.5 116.7 %all-gather.3.cloned.1.call-start = ((), (), s32[]{:S(2)}) async-start(), calls=%async_computation.1 | async-start | bytes 17301504 | tf_op jit(solution)/shard_map/all_gather | solution.py:192
  7.3 270.9 %reduce-scatter.2.cloned.1.call-start = ((), (), s32[]{:S(2)}) async-start(), calls=%async_computation.2 | async-start | bytes 3342336 | tf_op jit(solution)/shard_map/reduce_scatter | solution.py:245
  114.7 29.4 %collective-permute-start.1 = (s32[32,2]{1,0:T(8,128)S(1)}, s32[32,2]{1,0:T(8,128)S(1)}, u32[]{:S(2)}, u32[]{:S(2)}) collective-permute-start(s32[32,2]{1,0:T(8,128)S(1)} %gather_fusion.1), channel_id=1, source_target_pairs={{32,0},{64,32},{96,64},{128,96},{160,128},{192,160},{224,192},{256... | collective-permute-start | bytes 776 | tf_op jit(solution)/shard_map/ppermute | solution.py:17
  127.1 63.9 %collective-permute-start.2 = (bf16[16,2,128,128]{3,2,1,0:T(8,128)(2,1)}, bf16[16,2,128,128]{3,2,1,0:T(8,128)(2,1)S(1)}, u32[]{:S(2)}, u32[]{:S(2)}) collective-permute-start(bf16[16,2,128,128]{3,2,1,0:T(8,128)(2,1)} %get-tuple-element.11), channel_id=1, source_target_pairs={{0,32},{32,64},{64,96},{96,128},{128,160},{160,192},{192,224},{224... | collective-permute-start | bytes 3145736 | tf_op jit(solution)/shard_map/ppermute | solution.py:17
  130.3 10.9 %copy-start = (bf16[8,2,128,128]{3,2,1,0:T(8,128)(2,1)S(1)}, bf16[8,2,128,128]{3,2,1,0:T(8,128)(2,1)}, u32[]{:S(2)}) copy-start(bf16[8,2,128,128]{3,2,1,0:T(8,128)(2,1)} %param.7) | copy-start | bytes 1572868
  134.3 56.7 %collective-permute-start.3 = (bf16[16,2,128,128]{3,2,1,0:T(8,128)(2,1)}, bf16[16,2,128,128]{3,2,1,0:T(8,128)(2,1)S(1)}, u32[]{:S(2)}, u32[]{:S(2)}) collective-permute-start(bf16[16,2,128,128]{3,2,1,0:T(8,128)(2,1)} %get-tuple-element.14), channel_id=1, source_target_pairs={{0,32},{32,64},{64,96},{96,128},{128,160},{160,192},{192,224},{224... | collective-permute-start | bytes 3145736 | tf_op jit(solution)/shard_map/ppermute | solution.py:17
  137.4 53.6 %collective-permute-start.4 = (bf16[16,2,128,128]{3,2,1,0:T(8,128)(2,1)}, bf16[16,2,128,128]{3,2,1,0:T(8,128)(2,1)}, u32[]{:S(2)}, u32[]{:S(2)}) collective-permute-start(bf16[16,2,128,128]{3,2,1,0:T(8,128)(2,1)} %get-tuple-element.15), channel_id=1, source_target_pairs={{32,0},{64,32},{96,64},{128,96},{160,128},{192,160},{224,192},{256... | collective-permute-start | bytes 3145736 | tf_op jit(solution)/shard_map/ppermute | solution.py:17
  138.7 52.3 %collective-permute-start.5 = (bf16[16,2,128,128]{3,2,1,0:T(8,128)(2,1)}, bf16[16,2,128,128]{3,2,1,0:T(8,128)(2,1)}, u32[]{:S(2)}, u32[]{:S(2)}) collective-permute-start(bf16[16,2,128,128]{3,2,1,0:T(8,128)(2,1)} %get-tuple-element.16), channel_id=1, source_target_pairs={{32,0},{64,32},{96,64},{128,96},{160,128},{192,160},{224,192},{256... | collective-permute-start | bytes 3145736 | tf_op jit(solution)/shard_map/ppermute | solution.py:17
  144.1 27.8 %collective-permute-start = (s32[32,2]{1,0:T(8,128)S(1)}, s32[32,2]{1,0:T(8,128)S(1)}, u32[]{:S(2)}, u32[]{:S(2)}) collective-permute-start(s32[32,2]{1,0:T(8,128)S(1)} %gather_fusion), channel_id=1, source_target_pairs={{0,32},{32,64},{64,96},{96,128},{128,160},{160,192},{192,224},{224... | collective-permute-start | bytes 776 | tf_op jit(solution)/shard_map/ppermute | solution.py:17
  191.0 1.0 copy-start.1
  191.0 1.3 copy-start.2
  279.0 13.6 %collective-permute-start.6 = (f32[16,1536]{1,0:T(8,128)S(1)}, f32[16,1536]{1,0:T(8,128)S(1)}, u32[]{:S(2)}, u32[]{:S(2)}) collective-permute-start(f32[16,1536]{1,0:T(8,128)S(1)} %constant_dynamic-slice_fusion), channel_id=1, source_target_pairs={{0,1},{1,0},{2,3},{3,2},{4,5},{5,4},{6,7},{7,6},{8,9},{9,8},{10,11... | collective-permute-start | bytes 294920 | tf_op jit(solution)/shard_map/ppermute | solution.py:250
Sparse Core Ops, SparseCore 0:
  9.5 113.6 all-gather.2
  206.6 71.4 reduce-scatter.1

commit v11 on v9

--- a/solution.py
+++ b/solution.py
@@ -92,18 +92,21 @@
     accumulate_rows(rows, slots, spans, src_ref, live_ref, lcol_ref, pcol_ref, a_ref, buf_ref, pt_ref, out_ref, acc_ref)
 
 
-def pick_kernel(up_sel, down_sel, group_ref, up_ref, down_ref, sems):
+def pick_kernel(up_sel, down_sel, group_ref, up_ref, down_ref, stage, sems_in, sems_out):
     count = up_sel.shape[0]
-    copies = []
+    reads, writes = [], []
     for q in range(count):
-        copies.append(pltpu.make_async_copy(group_ref.at[up_sel[q]], up_ref.at[q], sems.at[q]))
-        copies.append(
-            pltpu.make_async_copy(group_ref.at[down_sel[q]], down_ref.at[q], sems.at[count + q])
-        )
-    for cp in copies:
+        for n, (sel, out_ref) in enumerate(((up_sel, up_ref), (down_sel, down_ref))):
+            j = n * count + q
+            reads.append(pltpu.make_async_copy(group_ref.at[sel[q]], stage.at[j], sems_in.at[j]))
+            writes.append(pltpu.make_async_copy(stage.at[j], out_ref.at[q], sems_out.at[j]))
+    for cp in reads:
         cp.start()
-    for cp in copies:
-        cp.wait()
+    for rd, wr in zip(reads, writes):
+        rd.wait()
+        wr.start()
+    for wr in writes:
+        wr.wait()
 
 
 SMEM = pl.BlockSpec(memory_space=pltpu.SMEM)
@@ -169,8 +172,12 @@
         pick_kernel,
         out_shape=(out, out),
         in_specs=[SMEM, SMEM, ANY],
-        out_specs=(VMEM, VMEM),
-        scratch_shapes=[pltpu.SemaphoreType.DMA((2 * count,))],
+        out_specs=(ANY, ANY),
+        scratch_shapes=[
+            pltpu.VMEM((2 * count,) + group_tiles.shape[1:], group_tiles.dtype),
+            pltpu.SemaphoreType.DMA((2 * count,)),
+            pltpu.SemaphoreType.DMA((2 * count,)),
+        ],
         compiler_params=pltpu.CompilerParams(vmem_limit_bytes=VMEM_LIMIT),
         cost_estimate=pl.CostEstimate(flops=0, bytes_accessed=nbytes, transcendentals=0),
     )(up_sel, down_sel, group_tiles)

time: 290 us -> 290 us (level)
  Pallas kernels: 36.1 us -> 39.5 us
    ppermute x4, waiting for transfers between devices: 19.7 us -> 16.7 us  [from_behind(): lax.ppermute(value, axis, [(source, source + steps) for source in range(l...]
    pallas_call x1, Pallas kernels: 16.1 us -> 19.1 us  [middle_product(): pl.pallas_call(functools.partial(middle_kernel, rows, slots), out_shape=j...]
  transfers between devices with their start and end apart: 7 -> 7, of which waited for: 5 -> 5; matrix products, arithmetic and copies ran while one was open for 5% -> 5% of each run, Pallas kernels for 8% -> 9%
where the time goes in v11:
time: 290 us; the launch traced here: 291 us
  blocking collectives  103 us (36%)
  waiting for transfers between devices  95.9 us (33%)
  Pallas kernels  39.5 us (14%)
  starting transfers between devices  21.3 us (7%)
  between operations  14.2 us (5%)
  local copies, waits for them, and re-layouts  9.62 us (3%)
  other arithmetic  7.45 us (3%)
    unnamed x1, blocking collectives  103 us
    reduce_scatter x1, waiting for transfers between devices, body(): partial = lax.psum_scatter(partial, 'z', scatter_dimension=0, tiled=True)  77 us
    pallas_call x1, Pallas kernels, middle_product(): pl.pallas_call(functools.partial(middle_kernel, rows, slots), out_shape=j...  19.1 us
    ppermute x4, waiting for transfers between devices, from_behind(): lax.ppermute(value, axis, [(source, source + steps) for source in range(l...  16.7 us
    pallas_call x1, Pallas kernels, side_product(): pl.pallas_call(functools.partial(side_kernel, rows, slots), out_shape=jax...  14.5 us
    ppermute x1, starting transfers between devices, body(): return mine + lax.ppermute(other, 'core', [(0, 1), (1, 0)])  11.7 us
    ppermute x4, starting transfers between devices, from_behind(): lax.ppermute(value, axis, [(source, source + steps) for source in range(l...  9.63 us
    pallas_call x1, Pallas kernels, pick_rows(): pl.pallas_call(pick_kernel, out_shape=(out, out), in_specs=[SMEM, SMEM, A...  5.96 us
  transfers between devices with their start and end apart: 7, of which 5 were waited for; matrix products, arithmetic and copies ran while one was open for 5% of the time, Pallas kernels for 9%

profile of v11, /device:TPU:1, one launch (start us, length us, event | category | flops | bytes accessed | tf_op | source)
XLA Modules:
  0.0 290.7 jit_solution(16955592340884600357)
XLA Ops:
  6.5 0.7 all-gather.3.cloned.1.call-update
  7.3 0.8 copy.25
  8.1 1.3 dynamic-slice
  10.1 0.8 add_dynamic-update-slice_fusion
  10.9 102.6 %all-reduce = s32[3584]{0:T(1024)S(1)} all-reduce(s32[3584]{0:T(1024)S(1)} %add_dynamic-update-slice_fusion), channel_id=2, replica_groups=mesh['row'=16,'z'=16,'core'=2] {'z','core'}, use_global_device_ids=true, to_apply=%add | all-reduce | flops 3584 | bytes 28672
  114.1 0.6 gather_fusion
  114.7 3.4 %collective-permute-start = (s32[32,2]{1,0:T(8,128)S(1)}, s32[32,2]{1,0:T(8,128)S(1)}, u32[]{:S(2)}, u32[]{:S(2)}) collective-permute-start(s32[32,2]{1,0:T(8,128)S(1)} %gather_fusion), channel_id=1, source_target_pairs={{0,32},{32,64},{64,96},{96,128},{128,160},{160,192},{192,224},{224... | collective-permute-start | bytes 776 | tf_op jit(solution)/shard_map/ppermute | solution.py:17
  118.7 1.3 collective-permute-start.1
  120.0 0.7 broadcast_clamp_fusion.3
  120.8 0.6 gather_fusion.3
  121.4 0.6 fusion.8
  122.0 0.7 broadcast_compare_fusion
  123.2 6.0 %shard_map.55 = (bf16[32,2,128,128]{3,2,1,0:T(8,128)(2,1)}, bf16[32,2,128,128]{3,2,1,0:T(8,128)(2,1)}) custom-call(s32[32]{0:T(128)} %get-tuple-element.22.up_sel, s32[32]{0:T(128)} %get-tuple-element.21.down_sel, bf16[256,2,128,128]{3,2,1,0:T(8,128)(2,1)} %all-gather.3.cloned.1.call-done.group_ref), custom_call_target="tpu_custom_call" | custom-call | bytes 8388608 | tf_op jit(solution)/shard_map/pallas_call | solution.py:171
  129.2 3.6 %collective-permute-start.2 = (bf16[32,2,128,128]{3,2,1,0:T(8,128)(2,1)}, bf16[32,2,128,128]{3,2,1,0:T(8,128)(2,1)S(1)}, u32[]{:S(2)}, u32[]{:S(2)}) collective-permute-start(bf16[32,2,128,128]{3,2,1,0:T(8,128)(2,1)} %get-tuple-element.7), channel_id=1, source_target_pairs={{0,32},{32,64},{64,96},{96,128},{128,160},{160,192},{192,224},{224... | collective-permute-start | bytes 6291464 | tf_op jit(solution)/shard_map/ppermute | solution.py:17
  132.8 1.3 collective-permute-start.3
  134.8 0.6 compare_select_fusion.8
  135.4 0.6 and_convert_fusion
  137.0 0.7 reshape.144.pcol_ref
  137.7 1.0 copy.27
  138.7 0.6 gather_fusion.4
  139.3 0.7 reshape.145.lcol_ref
  140.1 0.6 gather_fusion.2
  140.8 0.7 reshape.143.lcol_ref
  141.5 19.1 %shard_map.56.prior_ref = f32[4,128,1536]{2,1,0:T(8,128)} custom-call(s32[128]{0:T(128)} %get-tuple-element.19.src_ref, s32[128]{0:T(128)} %get-tuple-element.17.live_ref, s32[256]{0:T(256)} %reshape.145.lcol_ref, s32[16]{0:T(128)} %reshape.144.pcol_ref, s32[32]{0:T(128)} %fusion.7.sel_ref, bf16[8,16,128,128]{3,2,1,0:T(8,128)(2,1)} %a_ref.3, ...), custom_call_target="tpu_custom_call" | custom-call | flops 1879048192 | bytes 9961472 | tf_op jit(solution)/shard_map/pallas_call | solution.py:131
  160.5 12.8 %collective-permute-done.2.lower_ref = bf16[32,2,128,128]{3,2,1,0:T(8,128)(2,1)S(1)} collective-permute-done((bf16[32,2,128,128]{3,2,1,0:T(8,128)(2,1)}, bf16[32,2,128,128]{3,2,1,0:T(8,128)(2,1)S(1)}, u32[]{:S(2)}, u32[]{:S(2)}) %collective-permute-start.2) | collective-permute-done | bytes 2097184 | tf_op jit(solution)/shard_map/ppermute | solution.py:17
  173.3 4.0 %collective-permute-done.3.upper_ref = bf16[32,2,128,128]{3,2,1,0:T(8,128)(2,1)} collective-permute-done((bf16[32,2,128,128]{3,2,1,0:T(8,128)(2,1)}, bf16[32,2,128,128]{3,2,1,0:T(8,128)(2,1)}, u32[]{:S(2)}, u32[]{:S(2)}) %collective-permute-start.3) | collective-permute-done | bytes 2097184 | tf_op jit(solution)/shard_map/ppermute | solution.py:17
  177.3 14.5 %shard_map.57 = f32[4,128,1536]{2,1,0:T(8,128)} custom-call(s32[128]{0:T(128)} %compare_select_fusion.7.src_ref, s32[128]{0:T(128)} %and_convert_fusion.1.live_ref, s32[256]{0:T(256)} %reshape.143.lcol_ref, s32[16]{0:T(128)} %reshape.144.pcol_ref, bf16[8,16,128,128]{3,2,1,0:T(8,128)(2,1)} %a_ref.3, ...), custom_call_target="tpu_custom_call", output_to_operand_aliasing={{}: (8, {})} | custom-call | flops 1879048192 | bytes 11534336 | tf_op jit(solution)/shard_map/pallas_call | solution.py:150
  191.8 77.0 %reduce-scatter.2.cloned.1.call-done = f32[32,1536]{1,0:T(8,128)} async-done(((f32[512,1536]{1,0:T(8,128)}), f32[32,1536]{1,0:T(8,128)}) %reduce-scatter.2.cloned.1.call-update) | async-done | bytes 196624 | tf_op jit(solution)/shard_map/reduce_scatter | solution.py:249
  268.8 0.9 constant_dynamic-slice_fusion
  269.7 11.7 %collective-permute-start.4 = (f32[16,1536]{1,0:T(8,128)S(1)}, f32[16,1536]{1,0:T(8,128)S(1)}, u32[]{:S(2)}, u32[]{:S(2)}) collective-permute-start(f32[16,1536]{1,0:T(8,128)S(1)} %constant_dynamic-slice_fusion), channel_id=1, source_target_pairs={{0,1},{1,0},{2,3},{3,2},{4,5},{5,4},{6,7},{7,6},{8,9},{9,8},{10,11... | collective-permute-start | bytes 294920 | tf_op jit(solution)/shard_map/ppermute | solution.py:254
  281.4 0.9 collective-permute-done.4
  282.3 1.5 dynamic-slice_add_fusion
  (36 shorter events, 3.7 us)
Async XLA Ops:
  6.5 116.7 %all-gather.3.cloned.1.call-start = ((), (), s32[]{:S(2)}) async-start(), calls=%async_computation.1 | async-start | bytes 17301504 | tf_op jit(solution)/shard_map/all_gather | solution.py:201
  7.3 261.6 %reduce-scatter.2.cloned.1.call-start = ((), (), s32[]{:S(2)}) async-start(), calls=%async_computation.2 | async-start | bytes 3342336 | tf_op jit(solution)/shard_map/reduce_scatter | solution.py:249
  114.7 25.4 %collective-permute-start = (s32[32,2]{1,0:T(8,128)S(1)}, s32[32,2]{1,0:T(8,128)S(1)}, u32[]{:S(2)}, u32[]{:S(2)}) collective-permute-start(s32[32,2]{1,0:T(8,128)S(1)} %gather_fusion), channel_id=1, source_target_pairs={{0,32},{32,64},{64,96},{96,128},{128,160},{160,192},{192,224},{224... | collective-permute-start | bytes 776 | tf_op jit(solution)/shard_map/ppermute | solution.py:17
  118.7 21.4 %collective-permute-start.1 = (s32[32,2]{1,0:T(8,128)S(1)}, s32[32,2]{1,0:T(8,128)S(1)}, u32[]{:S(2)}, u32[]{:S(2)}) collective-permute-start(s32[32,2]{1,0:T(8,128)S(1)} %gather_fusion.1), channel_id=1, source_target_pairs={{32,0},{64,32},{96,64},{128,96},{160,128},{192,160},{224,192},{256... | collective-permute-start | bytes 776 | tf_op jit(solution)/shard_map/ppermute | solution.py:17
  123.2 14.5 %copy-start.1 = (bf16[8,2,128,128]{3,2,1,0:T(8,128)(2,1)S(1)}, bf16[8,2,128,128]{3,2,1,0:T(8,128)(2,1)}, u32[]{:S(2)}) copy-start(bf16[8,2,128,128]{3,2,1,0:T(8,128)(2,1)} %param.7) | copy-start | bytes 1572868
  129.2 44.1 %collective-permute-start.2 = (bf16[32,2,128,128]{3,2,1,0:T(8,128)(2,1)}, bf16[32,2,128,128]{3,2,1,0:T(8,128)(2,1)S(1)}, u32[]{:S(2)}, u32[]{:S(2)}) collective-permute-start(bf16[32,2,128,128]{3,2,1,0:T(8,128)(2,1)} %get-tuple-element.7), channel_id=1, source_target_pairs={{0,32},{32,64},{64,96},{96,128},{128,160},{160,192},{192,224},{224... | collective-permute-start | bytes 6291464 | tf_op jit(solution)/shard_map/ppermute | solution.py:17
  132.8 44.5 %collective-permute-start.3 = (bf16[32,2,128,128]{3,2,1,0:T(8,128)(2,1)}, bf16[32,2,128,128]{3,2,1,0:T(8,128)(2,1)}, u32[]{:S(2)}, u32[]{:S(2)}) collective-permute-start(bf16[32,2,128,128]{3,2,1,0:T(8,128)(2,1)} %get-tuple-element.8), channel_id=1, source_target_pairs={{32,0},{64,32},{96,64},{128,96},{160,128},{192,160},{224,192},{256... | collective-permute-start | bytes 6291464 | tf_op jit(solution)/shard_map/ppermute | solution.py:17
  173.3 4.0 %copy-start = (bf16[32,2,128,128]{3,2,1,0:T(8,128)(2,1)}, bf16[32,2,128,128]{3,2,1,0:T(8,128)(2,1)S(1)}, u32[]{:S(2)}) copy-start(bf16[32,2,128,128]{3,2,1,0:T(8,128)(2,1)S(1)} %collective-permute-done.2.lower_ref) | copy-start | bytes 6291460
  269.7 12.6 %collective-permute-start.4 = (f32[16,1536]{1,0:T(8,128)S(1)}, f32[16,1536]{1,0:T(8,128)S(1)}, u32[]{:S(2)}, u32[]{:S(2)}) collective-permute-start(f32[16,1536]{1,0:T(8,128)S(1)} %constant_dynamic-slice_fusion), channel_id=1, source_target_pairs={{0,1},{1,0},{2,3},{3,2},{4,5},{5,4},{6,7},{7,6},{8,9},{9,8},{10,11... | collective-permute-start | bytes 294920 | tf_op jit(solution)/shard_map/ppermute | solution.py:254
Sparse Core Ops, SparseCore 0:
  9.5 113.6 all-gather.2
  191.9 76.8 reduce-scatter.1
